TPU v7x, 32 devices: a whole 2x2x4 slice. The times are simulated.
32 devices in a mesh: state: 2 (over x), member: 16 (over z, y, core).
Axes of the slice: x: 2, y: 2, z: 4, core: 2. Of those that a mesh axis runs over, the one named last changes fastest.
Arguments:
- state: float32 [2048, 1280], P('member', 'state'), may hold values from -6 to 6
- obs_values: float32 [2, 384], replicated, may hold values from -8 to 8
- noise_var: float32 [2, 384], replicated, may hold values from 0.3 to 3
- obs_rows: int32 [2, 384], replicated, may hold values from 0 to 639
- owner: int32 [2, 3], replicated, may hold values from 0 to 1
Outputs:
- analysis: float32 [2048, 1280], P('member', 'state')
All inputs are finite; a program needn't handle non-finite values.
Results may differ from a plain program's by a relative error of at most 0.0003.
Values sent between devices are 32-bit elements; how exact they have to be, the bound alone decides.
No kernel may reach another device: no remote copies, remote signals or barrier semaphores. Data moves between devices by JAX's collectives and lax.ppermute only.
A program may use at most 64 MiB of HBM per device.

v0:
```python
import jax
import jax.numpy as jnp
from jax import lax
from jax.sharding import PartitionSpec as P


def from_root(x, axis, root):
    mine = lax.axis_index(axis) == root
    return lax.psum(jnp.where(mine, x, jnp.zeros_like(x)), axis)


def full_dot(left, right):
    return jnp.dot(left, right, precision=lax.Precision.HIGHEST, preferred_element_type=jnp.float32)


def solve_gram(factor, right):
    half = lax.linalg.triangular_solve(factor, right, left_side=True, lower=True)
    return lax.linalg.triangular_solve(factor, half, left_side=True, lower=True, transpose_a=True)


def tile_rows(state, picks, source):
    local_rows = jnp.take(state, picks, axis=1)
    return from_root(local_rows, "state", source)


def owner_rows(state, picks, owners_block):
    num_tiles = owners_block.shape[0]
    tile_width = picks.shape[0] // num_tiles
    pieces = []
    for tile in range(num_tiles):
        pieces.append(
            tile_rows(state, picks[tile * tile_width : (tile + 1) * tile_width], owners_block[tile])
        )
    return jnp.concatenate(pieces, axis=1)


def analyse(current, observed, target, noise):
    count = observed.shape[0] * lax.axis_size("member")
    row_sums, obs_sums = lax.psum((jnp.sum(current, axis=0), jnp.sum(observed, axis=0)), "member")
    row_mean = row_sums / count
    obs_mean = obs_sums / count
    row_anom = current - row_mean[None, :]
    obs_anom = observed - obs_mean[None, :]
    cross_sum, gram_sum = lax.psum(
        (full_dot(obs_anom.T, row_anom), full_dot(obs_anom.T, obs_anom)), "member"
    )
    cross = cross_sum / (count - 1.0)
    innov_cov = gram_sum / (count - 1.0) + jnp.diag(noise)
    factor = jnp.linalg.cholesky(innov_cov)
    weights = solve_gram(factor, (target - obs_mean)[:, None])
    transformed = solve_gram(factor, obs_anom.T)
    shift = full_dot(weights.T, cross)
    return row_mean[None, :] + shift + row_anom - 0.5 * full_dot(transformed.T, cross)


def shards(state, obs_values, noise_var, obs_rows, owner):
    num_blocks = obs_rows.shape[0]
    current = state
    for block in range(num_blocks):
        observed = owner_rows(current, obs_rows[block], owner[block])
        current = analyse(current, observed, obs_values[block], noise_var[block])
    return current


def solution(mesh):
    placed = (P("member", "state"), P(), P(), P(), P())
    return jax.shard_map(
        shards, mesh=mesh, in_specs=placed, out_specs=P("member", "state"), check_vma=False
    )
```

profile of v0, /device:TPU:0, one launch (start us, length us, event | category | flops | bytes accessed | tf_op | source)
XLA Modules:
  0.0 544.9 jit_solution(4166436160607081989)
XLA Ops:
  7.3 1.1 copy.6
  17.4 23.3 %all-reduce.18.cloned.1.call-done = (f32[128,128]{0,1:T(8,128)}, f32[128,128]{0,1:T(8,128)}, f32[128,128]{0,1:T(8,128)}) async-done(((f32[128,128]{0,1:T(8,128)}, f32[128,128]{0,1:T(8,128)}, f32[128,128]{0,1:T(8,128)}), (f32[128,128]{0,1:T(8,128)}, f32[128,128]{0,1:T(8,128)}, f32[128,128]{0,1:T(8,128)})) %all-reduce.18.cloned.1.call-update) | async-done | bytes 196624 | tf_op jit(solution)/shard_map/psum | solution.py:9
  42.5 33.1 %all-reduce.2 = (f32[640]{0:T(1024)S(1)}, f32[384]{0:T(512)S(1)}) all-reduce(f32[640]{0:T(1024)S(1)} %reduce_sum.36, f32[384]{0:T(512)S(1)} %reduce_sum.37), channel_id=1, replica_groups=mesh['state'=2,'member'=16] {'member'}, use_global_device_ids=true, to_apply=%region_1.2 | all-reduce | flops 1024 | bytes 8192 | tf_op jit(solution)/shard_map/psum | solution.py:39
  75.7 1.5 fusion.38
  77.2 2.0 fusion.22
  80.3 91.4 %all-reduce.14.cloned.1.call-done = (f32[384,640]{1,0:T(8,128)}, f32[384,384]{0,1:T(8,128)}) async-done(((f32[384,640]{1,0:T(8,128)}, f32[384,384]{0,1:T(8,128)}), (f32[384,640]{1,0:T(8,128)}, f32[384,384]{0,1:T(8,128)})) %all-reduce.14.cloned.1.call-update) | async-done | bytes 1572880 | tf_op jit(solution)/shard_map/psum | solution.py:44
  174.0 11.7 %cholesky.208 = f32[128,128]{1,0:T(8,128)S(1)} custom-call(f32[128,128]{1,0:T(8,128)S(1)} %cholesky.310), custom_call_target="Cholesky" | custom-call | tf_op jit(solution)/shard_map/jit(cholesky)/cholesky | solution.py:49
  185.8 9.8 %custom-call.32 = f32[1,128,128]{1,2,0:T(8,128)S(1)} custom-call(f32[1,128,128]{2,1,0:T(8,128)S(1)} %get-tuple-element.138), custom_call_target="InvertDiagBlocksLowerTriangular" | custom-call | tf_op jit(solution)/shard_map/jit(cholesky)/cholesky | solution.py:49
  196.2 11.7 %cholesky.227 = f32[128,128]{1,0:T(8,128)S(1)} custom-call(f32[128,128]{1,0:T(8,128)S(1)} %cholesky.314), custom_call_target="Cholesky" | custom-call | tf_op jit(solution)/shard_map/jit(cholesky)/cholesky | solution.py:49
  209.3 10.2 %custom-call.33 = f32[1,128,128]{1,2,0:T(8,128)S(1)} custom-call(f32[1,128,128]{2,1,0:T(8,128)S(1)} %get-tuple-element.135), custom_call_target="InvertDiagBlocksLowerTriangular" | custom-call | tf_op jit(solution)/shard_map/jit(cholesky)/cholesky | solution.py:49
  220.0 11.7 %cholesky.246 = f32[128,128]{1,0:T(8,128)S(1)} custom-call(f32[128,128]{1,0:T(8,128)S(1)} %convolution_subtract_fusion.11), custom_call_target="Cholesky" | custom-call | tf_op jit(solution)/shard_map/jit(cholesky)/cholesky | solution.py:49
  234.3 6.3 %while.16 = (s32[]{:T(128)}, f32[384,384]{1,0:T(8,128)S(1)}, s32[3,2]{0,1:T(2,128)S(1)}, f32[3,128,128]{2,1,0:T(8,128)S(1)}, s32[]{:T(128)}) while((s32[]{:T(128)}, f32[384,384]{1,0:T(8,128)S(1)}, s32[3,2]{0,1:T(2,128)S(1)}, f32[3,128,128]{2,1,0:T(8,128)S(1)}, s32[]{:T(128)}) %tuple.98), condition=%wide.while_cond.1, body=%wide.while_body.1.sunk | while | flops 2 | bytes 131181 | solution.py:18
  235.0 1.4 bitcast_dynamic-update-slice_fusion.4
  237.1 1.4 bitcast_dynamic-update-slice_fusion.4
  239.1 1.4 bitcast_dynamic-update-slice_fusion.4
  240.6 29.5 %custom-call.35 = f32[3,128,128]{1,2,0:T(8,128)S(1)} custom-call(f32[3,128,128]{2,1,0:T(8,128)S(1)} %get-tuple-element.68), custom_call_target="InvertDiagBlocksLowerTriangular" | custom-call | tf_op jit(solution)/shard_map/triangular_solve/custom-call.6 | solution.py:18
  279.9 21.5 %all-reduce.16.cloned.1.call-done = (f32[128,128]{0,1:T(8,128)}, f32[128,128]{0,1:T(8,128)}, f32[128,128]{0,1:T(8,128)}) async-done(((f32[128,128]{0,1:T(8,128)}, f32[128,128]{0,1:T(8,128)}, f32[128,128]{0,1:T(8,128)}), (f32[128,128]{0,1:T(8,128)}, f32[128,128]{0,1:T(8,128)}, f32[128,128]{0,1:T(8,128)})) %all-reduce.16.cloned.1.call-update) | async-done | bytes 196624 | tf_op jit(solution)/shard_map/psum | solution.py:9
  303.3 33.3 %all-reduce.1 = (f32[640]{0:T(1024)S(1)}, f32[384]{0:T(512)S(1)}) all-reduce(f32[640]{0:T(1024)S(1)} %get-tuple-element.161, f32[384]{0:T(512)S(1)} %reduce_sum.39), channel_id=1, replica_groups=mesh['state'=2,'member'=16] {'member'}, use_global_device_ids=true, to_apply=%region_16.0 | all-reduce | flops 1024 | bytes 8192 | tf_op jit(solution)/shard_map/psum | solution.py:39
  336.6 1.5 fusion.35
  338.2 2.0 fusion.20
  340.3 92.4 %all-reduce.12.cloned.1.call-done = (f32[384,640]{1,0:T(8,128)}, f32[384,384]{0,1:T(8,128)}) async-done(((f32[384,640]{1,0:T(8,128)}, f32[384,384]{0,1:T(8,128)}), (f32[384,640]{1,0:T(8,128)}, f32[384,384]{0,1:T(8,128)})) %all-reduce.12.cloned.1.call-update) | async-done | bytes 1572880 | tf_op jit(solution)/shard_map/psum | solution.py:44
  435.0 11.7 %cholesky.261 = f32[128,128]{1,0:T(8,128)S(1)} custom-call(f32[128,128]{1,0:T(8,128)S(1)} %cholesky.318), custom_call_target="Cholesky" | custom-call | tf_op jit(solution)/shard_map/jit(cholesky)/cholesky | solution.py:49
  446.8 9.8 %custom-call.38 = f32[1,128,128]{1,2,0:T(8,128)S(1)} custom-call(f32[1,128,128]{2,1,0:T(8,128)S(1)} %get-tuple-element.131), custom_call_target="InvertDiagBlocksLowerTriangular" | custom-call | tf_op jit(solution)/shard_map/jit(cholesky)/cholesky | solution.py:49
  457.2 11.9 %cholesky.280 = f32[128,128]{1,0:T(8,128)S(1)} custom-call(f32[128,128]{1,0:T(8,128)S(1)} %cholesky.322), custom_call_target="Cholesky" | custom-call | tf_op jit(solution)/shard_map/jit(cholesky)/cholesky | solution.py:49
  470.5 9.8 %custom-call.39 = f32[1,128,128]{1,2,0:T(8,128)S(1)} custom-call(f32[1,128,128]{2,1,0:T(8,128)S(1)} %get-tuple-element.128), custom_call_target="InvertDiagBlocksLowerTriangular" | custom-call | tf_op jit(solution)/shard_map/jit(cholesky)/cholesky | solution.py:49
  480.8 11.7 %cholesky.299 = f32[128,128]{1,0:T(8,128)S(1)} custom-call(f32[128,128]{1,0:T(8,128)S(1)} %convolution_subtract_fusion.6), custom_call_target="Cholesky" | custom-call | tf_op jit(solution)/shard_map/jit(cholesky)/cholesky | solution.py:49
  495.1 6.5 %while.17 = (s32[]{:T(128)}, f32[384,384]{1,0:T(8,128)S(1)}, s32[3,2]{0,1:T(2,128)S(1)}, f32[3,128,128]{2,1,0:T(8,128)S(1)}, s32[]{:T(128)}) while((s32[]{:T(128)}, f32[384,384]{1,0:T(8,128)S(1)}, s32[3,2]{0,1:T(2,128)S(1)}, f32[3,128,128]{2,1,0:T(8,128)S(1)}, s32[]{:T(128)}) %tuple.116), condition=%wide.while_cond.1.clone, body=%wide.while_body.1.clone.sunk | while | flops 2 | bytes 131181 | solution.py:18
  496.0 1.4 bitcast_dynamic-update-slice_fusion.5
  498.1 1.4 bitcast_dynamic-update-slice_fusion.5
  500.2 1.4 bitcast_dynamic-update-slice_fusion.5
  501.6 29.5 %custom-call.41 = f32[3,128,128]{1,2,0:T(8,128)S(1)} custom-call(f32[3,128,128]{2,1,0:T(8,128)S(1)} %get-tuple-element.72), custom_call_target="InvertDiagBlocksLowerTriangular" | custom-call | tf_op jit(solution)/shard_map/triangular_solve/custom-call.6 | solution.py:18
  536.4 1.6 fusion
  (166 shorter events, 40.5 us)
Async XLA Ops:
  6.5 34.1 %all-reduce.18.cloned.1.call-start = ((), (), s32[]{:S(2)}) async-start(), calls=%async_computation.3 | async-start | bytes 393216 | tf_op jit(solution)/shard_map/psum | solution.py:9
  7.3 1.2 copy-start.9
  12.5 2.8 copy-start
  15.2 156.5 %all-reduce.14.cloned.1.call-start = ((), (), s32[]{:S(2)}) async-start(), calls=%async_computation.1 | async-start | bytes 3145728 | tf_op jit(solution)/shard_map/psum | solution.py:44
  16.7 0.7 copy-start.10
  40.7 0.9 copy-start.6
  41.6 0.8 copy-start.5
  79.2 222.2 %all-reduce.16.cloned.1.call-start = ((), (), s32[]{:S(2)}) async-start(), calls=%async_computation.2 | async-start | bytes 393216 | tf_op jit(solution)/shard_map/psum | solution.py:9
  79.5 0.7 copy-start.11
  172.8 1.1 copy-start.3
  234.3 37.8 %copy-start.1 = (f32[384,640]{1,0:T(8,128)S(1)}, f32[384,640]{1,0:T(8,128)}, u32[]{:S(2)}) copy-start(f32[384,640]{1,0:T(8,128)} %get-tuple-element.101) | copy-start | bytes 2949124
  279.9 152.8 %all-reduce.12.cloned.1.call-start = ((), (), s32[]{:S(2)}) async-start(), calls=%async_computation | async-start | bytes 3145728 | tf_op jit(solution)/shard_map/psum | solution.py:44
  301.5 0.9 copy-start.8
  302.3 0.8 copy-start.7
  433.8 1.1 copy-start.4
  495.1 38.0 %copy-start.2 = (f32[384,640]{1,0:T(8,128)S(1)}, f32[384,640]{1,0:T(8,128)}, u32[]{:S(2)}) copy-start(f32[384,640]{1,0:T(8,128)} %get-tuple-element.99) | copy-start | bytes 2949124
Sparse Core Ops, SparseCore 0:
  15.4 25.2 all-reduce.17
  79.4 92.3 all-reduce.13
  280.0 21.4 all-reduce.15
  340.3 92.3 all-reduce.11
where the time goes:
time: 548 us; the launch traced here: 545 us
  waiting for transfers between devices  229 us (42%)
  other arithmetic  181 us (33%)
  blocking collectives  66.4 us (12%)
  local copies, waits for them, and re-layouts  24.8 us (5%)
  matrix products  22.1 us (4%)
  between operations  21.6 us (4%)
    psum x2, waiting for transfers between devices, analyse(): lax.psum((full_dot(obs_anom.T, row_anom), full_dot(obs_anom.T, obs_anom))...  184 us
    another operation x22, other arithmetic, analyse(): factor = jnp.linalg.cholesky(innov_cov)  114 us
    psum x2, blocking collectives, analyse(): lax.psum((jnp.sum(current, axis=0), jnp.sum(observed, axis=0)), 'member')  66.4 us
    another operation x5, other arithmetic, solve_gram(): lax.linalg.triangular_solve(factor, half, left_side=True, lower=True, tra...  59.1 us
    psum x2, waiting for transfers between devices, from_root(): return lax.psum(jnp.where(mine, x, jnp.zeros_like(x)), axis)  44.8 us
    another operation x21, local copies, waits for them, and re-layouts, solve_gram(): lax.linalg.triangular_solve(factor, half, left_side=True, lower=True, tra...  12.4 us
  transfers between devices with their start and end apart: 4, of which 4 were waited for; matrix products, arithmetic and copies ran while one was open for 0% of the time, Pallas kernels for 0%

commit v1 on v0

v1 whole, which is shorter than its diff:
```python
import jax
import jax.numpy as jnp
from jax import lax
from jax.sharding import PartitionSpec as P


def full_dot(left, right):
    return jnp.dot(left, right, precision=lax.Precision.HIGHEST, preferred_element_type=jnp.float32)


def tdot(left, right):
    return lax.dot_general(
        left, right, (((0,), (0,)), ((), ())),
        precision=lax.Precision.HIGHEST, preferred_element_type=jnp.float32,
    )


def solve_gram(factor, right):
    half = lax.linalg.triangular_solve(factor, right, left_side=True, lower=True)
    return lax.linalg.triangular_solve(factor, half, left_side=True, lower=True, transpose_a=True)


def exchange(cands, owners_block):
    n_state = lax.axis_size("state")
    obs = cands.shape[1]
    tile = obs // owners_block.shape[0]
    gathered = lax.all_gather(cands, "state", axis=0)
    own_each = jnp.repeat(owners_block, tile)
    pick = own_each[None, :] == jnp.arange(n_state, dtype=own_each.dtype)[:, None]
    return jnp.sum(jnp.where(pick[:, None, :], gathered, 0.0), axis=0)


def analyse(current, observed, target, noise):
    m_loc = current.shape[0]
    n_member = lax.axis_size("member")
    count = m_loc * n_member
    me = lax.axis_index("member")
    n_rows = current.shape[1]
    obs = observed.shape[1]

    row_loc = jnp.mean(current, axis=0)
    obs_loc = jnp.mean(observed, axis=0)
    row_c = current - row_loc[None, :]
    obs_c = observed - obs_loc[None, :]
    gram_loc = tdot(obs_c, obs_c)
    cross_loc = tdot(obs_c, row_c)

    slots = jnp.zeros((n_member, obs + n_rows), jnp.float32)
    slots = lax.dynamic_update_slice(slots, jnp.concatenate([obs_loc, row_loc])[None, :], (me, 0))
    gram_sum, slots = lax.psum((gram_loc, slots), "member")
    cross_loc, gram_sum, slots = lax.optimization_barrier((cross_loc, gram_sum, slots))
    cross_sum = lax.psum(cross_loc, "member")

    means = jnp.mean(slots, axis=0)
    dev = slots - means[None, :]
    obs_mean = means[:obs]
    dev_obs = dev[:, :obs]
    dev_row = dev[:, obs:]

    innov_cov = (gram_sum + m_loc * tdot(dev_obs, dev_obs)) / (count - 1.0) + jnp.diag(noise)
    factor = jnp.linalg.cholesky(innov_cov)
    obs_anom = observed - obs_mean[None, :]
    rhs = (target - obs_mean)[:, None] - 0.5 * obs_anom.T
    gain = solve_gram(factor, rhs)

    cross = (cross_sum + m_loc * tdot(dev_obs, dev_row)) / (count - 1.0)
    return gain, cross


def shards(state, obs_values, noise_var, obs_rows, owner):
    num_blocks = obs_rows.shape[0]
    current = state
    cands = jnp.take(current, obs_rows[0], axis=1)
    for block in range(num_blocks):
        observed = exchange(cands, owner[block])
        gain, cross = analyse(current, observed, obs_values[block], noise_var[block])
        if block + 1 < num_blocks:
            rows = obs_rows[block + 1]
            cands = jnp.take(current, rows, axis=1) + full_dot(gain.T, jnp.take(cross, rows, axis=1))
        current = current + full_dot(gain.T, cross)
    return current


def solution(mesh):
    placed = (P("member", "state"), P(), P(), P(), P())
    return jax.shard_map(
        shards, mesh=mesh, in_specs=placed, out_specs=P("member", "state"), check_vma=False
    )
```

time: 548 us -> 438 us (0.80)
  waiting for transfers between devices: 229 us -> 177 us
  blocking collectives: 66.4 us -> 15.8 us
  other arithmetic: 181 us -> 173 us
    psum x2 -> x0, blocking collectives: 66.4 us -> none  [analyse(): lax.psum((jnp.sum(current, axis=0), jnp.sum(observed, axis=0)), 'member')]
    psum x4, waiting for transfers between devices: 229 us -> 177 us  [the longest x2 177 us: analyse(): gram_sum, slots = lax.psum((gram_loc, slots), 'member')]
    all_gather x0 -> x2, blocking collectives: none -> 15.8 us  [exchange(): gathered = lax.all_gather(cands, 'state', axis=0)]
    dot_general x0 -> x8, matrix products: none -> 12.7 us  [tdot(): lax.dot_general(left, right, (((0,), (0,)), ((), ())), precision=lax.Prec...]
    dot_general x8 -> x3, matrix products: 10.9 us -> 3.35 us  [full_dot(): jnp.dot(left, right, precision=lax.Precision.HIGHEST, preferred_element_t...]
    another operation x22 -> x21, other arithmetic: 114 us -> 114 us  [analyse(): factor = jnp.linalg.cholesky(innov_cov)]
  transfers between devices with their start and end apart: 4 -> 4, of which waited for: 4 -> 2; matrix products, arithmetic and copies ran while one was open for 0% -> 46% of each run, Pallas kernels for 0% -> 0%
where the time goes in v1:
time: 438 us; the launch traced here: 434 us
  waiting for transfers between devices  177 us (40%)
  other arithmetic  173 us (39%)
  local copies, waits for them, and re-layouts  25.3 us (6%)
  matrix products  23.7 us (5%)
  between operations  17.9 us (4%)
  blocking collectives  15.8 us (4%)
    psum x2, waiting for transfers between devices, analyse(): gram_sum, slots = lax.psum((gram_loc, slots), 'member')  177 us
    another operation x21, other arithmetic, analyse(): factor = jnp.linalg.cholesky(innov_cov)  114 us
    another operation x5, other arithmetic, solve_gram(): lax.linalg.triangular_solve(factor, half, left_side=True, lower=True, tra...  59.1 us
    all_gather x2, blocking collectives, exchange(): gathered = lax.all_gather(cands, 'state', axis=0)  15.8 us
    dot_general x8, matrix products, tdot(): lax.dot_general(left, right, (((0,), (0,)), ((), ())), precision=lax.Prec...  12.7 us
    another operation x21, local copies, waits for them, and re-layouts, solve_gram(): lax.linalg.triangular_solve(factor, half, left_side=True, lower=True, tra...  12 us
  transfers between devices with their start and end apart: 4, of which 2 were waited for; matrix products, arithmetic and copies ran while one was open for 46% of the time, Pallas kernels for 0%

profile of v1, /device:TPU:0, one launch (start us, length us, event | category | flops | bytes accessed | tf_op | source)
XLA Modules:
  0.0 434.3 jit_solution(6324367499370617287)
XLA Ops:
  10.5 8.5 %all-gather = f32[256,384]{0,1:T(8,128)S(1)} all-gather(f32[128,384]{0,1:T(8,128)S(1)} %select_bitcast_fusion), channel_id=2, replica_groups=mesh['state'=2,'member'=16] {'state'}, dimensions={0}, use_global_device_ids=true | all-gather | bytes 589824 | tf_op jit(solution)/shard_map/all_gather | solution.py:27
  20.2 1.5 fusion.27
  25.3 1.9 fusion.15
  27.3 88.6 %all-reduce.14.cloned.1.call-done = (f32[384,384]{0,1:T(8,128)}, f32[16,1024]{1,0:T(8,128)}) async-done(((f32[384,384]{0,1:T(8,128)}, f32[16,1024]{1,0:T(8,128)}), (f32[384,384]{0,1:T(8,128)}, f32[16,1024]{1,0:T(8,128)})) %all-reduce.14.cloned.1.call-update) | async-done | bytes 655376 | tf_op jit(solution)/shard_map/psum | solution.py:50
  117.9 11.7 %cholesky.208 = f32[128,128]{1,0:T(8,128)S(1)} custom-call(f32[128,128]{1,0:T(8,128)S(1)} %cholesky.310), custom_call_target="Cholesky" | custom-call | tf_op jit(solution)/shard_map/jit(cholesky)/cholesky | solution.py:61
  129.7 9.8 %custom-call.24 = f32[1,128,128]{1,2,0:T(8,128)S(1)} custom-call(f32[1,128,128]{2,1,0:T(8,128)S(1)} %get-tuple-element.100), custom_call_target="InvertDiagBlocksLowerTriangular" | custom-call | tf_op jit(solution)/shard_map/jit(cholesky)/cholesky | solution.py:61
  140.1 11.7 %cholesky.227 = f32[128,128]{1,0:T(8,128)S(1)} custom-call(f32[128,128]{1,0:T(8,128)S(1)} %cholesky.314), custom_call_target="Cholesky" | custom-call | tf_op jit(solution)/shard_map/jit(cholesky)/cholesky | solution.py:61
  151.9 10.2 %custom-call.25 = f32[1,128,128]{1,2,0:T(8,128)S(1)} custom-call(f32[1,128,128]{2,1,0:T(8,128)S(1)} %get-tuple-element.97), custom_call_target="InvertDiagBlocksLowerTriangular" | custom-call | tf_op jit(solution)/shard_map/jit(cholesky)/cholesky | solution.py:61
  162.5 11.7 %cholesky.246 = f32[128,128]{1,0:T(8,128)S(1)} custom-call(f32[128,128]{1,0:T(8,128)S(1)} %convolution_subtract_fusion.11), custom_call_target="Cholesky" | custom-call | tf_op jit(solution)/shard_map/jit(cholesky)/cholesky | solution.py:61
  177.7 6.0 %while.8 = (s32[]{:T(128)}, f32[384,384]{1,0:T(8,128)S(1)}, s32[3,2]{0,1:T(2,128)S(1)}, f32[3,128,128]{2,1,0:T(8,128)S(1)}, s32[]{:T(128)}) while((s32[]{:T(128)}, f32[384,384]{1,0:T(8,128)S(1)}, s32[3,2]{0,1:T(2,128)S(1)}, f32[3,128,128]{2,1,0:T(8,128)S(1)}, s32[]{:T(128)}) %tuple.69), condition=%wide.while_cond.1, body=%wide.while_body.1.sunk | while | flops 2 | bytes 131189 | solution.py:20
  178.3 1.4 bitcast_dynamic-update-slice_fusion.4
  180.3 1.4 bitcast_dynamic-update-slice_fusion.4
  182.3 1.4 bitcast_dynamic-update-slice_fusion.4
  183.7 29.5 %custom-call.27 = f32[3,128,128]{1,2,0:T(8,128)S(1)} custom-call(f32[3,128,128]{2,1,0:T(8,128)S(1)} %get-tuple-element.50), custom_call_target="InvertDiagBlocksLowerTriangular" | custom-call | tf_op jit(solution)/shard_map/triangular_solve/custom-call.6 | solution.py:20
  216.1 2.2 fusion.3
  219.6 1.7 gather_fusion
  222.2 7.3 %all-gather.1 = f32[256,384]{1,0:T(8,128)S(1)} all-gather(f32[128,384]{1,0:T(8,128)S(1)} %convolution_add_fusion.2), channel_id=3, replica_groups=mesh['state'=2,'member'=16] {'state'}, dimensions={0}, use_global_device_ids=true | all-gather | bytes 589824 | tf_op jit(solution)/shard_map/all_gather | solution.py:27
  229.6 1.5 fusion.24
  232.1 1.9 fusion.13
  234.1 88.7 %all-reduce.12.cloned.1.call-done = (f32[384,384]{0,1:T(8,128)}, f32[16,1024]{1,0:T(8,128)}) async-done(((f32[384,384]{0,1:T(8,128)}, f32[16,1024]{1,0:T(8,128)}), (f32[384,384]{0,1:T(8,128)}, f32[16,1024]{1,0:T(8,128)})) %all-reduce.12.cloned.1.call-update) | async-done | bytes 655376 | tf_op jit(solution)/shard_map/psum | solution.py:50
  324.9 11.7 %cholesky.261 = f32[128,128]{1,0:T(8,128)S(1)} custom-call(f32[128,128]{1,0:T(8,128)S(1)} %cholesky.318), custom_call_target="Cholesky" | custom-call | tf_op jit(solution)/shard_map/jit(cholesky)/cholesky | solution.py:61
  336.7 9.8 %custom-call.28 = f32[1,128,128]{1,2,0:T(8,128)S(1)} custom-call(f32[1,128,128]{2,1,0:T(8,128)S(1)} %get-tuple-element.93), custom_call_target="InvertDiagBlocksLowerTriangular" | custom-call | tf_op jit(solution)/shard_map/jit(cholesky)/cholesky | solution.py:61
  347.0 11.7 %cholesky.280 = f32[128,128]{1,0:T(8,128)S(1)} custom-call(f32[128,128]{1,0:T(8,128)S(1)} %cholesky.322), custom_call_target="Cholesky" | custom-call | tf_op jit(solution)/shard_map/jit(cholesky)/cholesky | solution.py:61
  358.8 10.0 %custom-call.29 = f32[1,128,128]{1,2,0:T(8,128)S(1)} custom-call(f32[1,128,128]{2,1,0:T(8,128)S(1)} %get-tuple-element.90), custom_call_target="InvertDiagBlocksLowerTriangular" | custom-call | tf_op jit(solution)/shard_map/jit(cholesky)/cholesky | solution.py:61
  369.3 11.7 %cholesky.299 = f32[128,128]{1,0:T(8,128)S(1)} custom-call(f32[128,128]{1,0:T(8,128)S(1)} %convolution_subtract_fusion.6), custom_call_target="Cholesky" | custom-call | tf_op jit(solution)/shard_map/jit(cholesky)/cholesky | solution.py:61
  385.0 6.3 %while.9 = (s32[]{:T(128)}, f32[384,384]{1,0:T(8,128)S(1)}, s32[3,2]{0,1:T(2,128)S(1)}, f32[3,128,128]{2,1,0:T(8,128)S(1)}, s32[]{:T(128)}) while((s32[]{:T(128)}, f32[384,384]{1,0:T(8,128)S(1)}, s32[3,2]{0,1:T(2,128)S(1)}, f32[3,128,128]{2,1,0:T(8,128)S(1)}, s32[]{:T(128)}) %tuple.85), condition=%wide.while_cond.1.clone, body=%wide.while_body.1.clone.sunk | while | flops 2 | bytes 131189 | solution.py:20
  385.9 1.4 bitcast_dynamic-update-slice_fusion.5
  387.9 1.4 bitcast_dynamic-update-slice_fusion.5
  389.9 1.4 bitcast_dynamic-update-slice_fusion.5
  391.3 29.5 %custom-call.31 = f32[3,128,128]{1,2,0:T(8,128)S(1)} custom-call(f32[3,128,128]{2,1,0:T(8,128)S(1)} %get-tuple-element.52), custom_call_target="InvertDiagBlocksLowerTriangular" | custom-call | tf_op jit(solution)/shard_map/triangular_solve/custom-call.6 | solution.py:20
  423.7 2.2 fusion.1
  426.0 1.6 convolution_add_fusion
  (149 shorter events, 31.1 us)
Async XLA Ops:
  6.5 109.3 %all-reduce.14.cloned.1.call-start = ((), (), s32[]{:S(2)}) async-start(), calls=%async_computation.3 | async-start | bytes 1310720 | tf_op jit(solution)/shard_map/psum | solution.py:50
  7.3 0.7 copy-start.10
  19.0 1.0 copy-start
  21.8 0.6 copy-start.4
  21.8 0.7 copy-start.7
  22.5 193.7 %all-reduce.8.cloned.1.call-start = ((), (), s32[]{:S(2)}) async-start(), calls=%async_computation | async-start | bytes 1966080 | tf_op jit(solution)/shard_map/psum | solution.py:52
  22.6 0.7 copy-start.8
  23.2 0.7 copy-start.9
  115.8 0.8 copy-start.5
  115.8 1.1 copy-start.1
  115.8 206.9 %all-reduce.12.cloned.1.call-start = ((), (), s32[]{:S(2)}) async-start(), calls=%async_computation.2 | async-start | bytes 1310720 | tf_op jit(solution)/shard_map/psum | solution.py:50
  231.3 0.6 copy-start.3
  231.9 191.8 %all-reduce.10.cloned.1.call-start = ((), (), s32[]{:S(2)}) async-start(), calls=%async_computation.1 | async-start | bytes 1966080 | tf_op jit(solution)/shard_map/psum | solution.py:52
  322.7 0.8 copy-start.6
  322.7 1.1 copy-start.2
Sparse Core Ops, SparseCore 0:
  22.6 93.1 all-reduce.13
  119.2 94.2 all-reduce.7
  232.0 90.6 all-reduce.11
  326.0 94.4 all-reduce.9

commit v2 on v1

--- a/solution.py
+++ b/solution.py
@@ -15,19 +15,60 @@
     )
 
 
+def _pow2(n):
+    return n > 0 and (n & (n - 1)) == 0
+
+
+def tree_sum(x, axis):
+    n = lax.axis_size(axis)
+    if n == 1:
+        return x
+    if not _pow2(n) or x.shape[0] % n != 0:
+        return lax.psum(x, axis)
+    me = lax.axis_index(axis)
+    cur = x
+    k = 1
+    while k < n:
+        perm = [(i, i ^ k) for i in range(n)]
+        h = cur.shape[0] // 2
+        bit = (me // k) % 2
+        keep = lax.dynamic_slice_in_dim(cur, bit * h, h, axis=0)
+        send = lax.dynamic_slice_in_dim(cur, (1 - bit) * h, h, axis=0)
+        cur = keep + lax.ppermute(send, axis, perm)
+        k *= 2
+    k = n // 2
+    while k >= 1:
+        perm = [(i, i ^ k) for i in range(n)]
+        bit = (me // k) % 2
+        other = lax.ppermute(cur, axis, perm)
+        cur = jnp.where(bit == 0, jnp.concatenate([cur, other]), jnp.concatenate([other, cur]))
+        k //= 2
+    return cur
+
+
+def tree_sum_exact(x, axis):
+    n = lax.axis_size(axis)
+    if not _pow2(n):
+        return lax.psum(x, axis)
+    k = 1
+    while k < n:
+        perm = [(i, i ^ k) for i in range(n)]
+        x = x + lax.ppermute(x, axis, perm)
+        k *= 2
+    return x
+
+
 def solve_gram(factor, right):
     half = lax.linalg.triangular_solve(factor, right, left_side=True, lower=True)
     return lax.linalg.triangular_solve(factor, half, left_side=True, lower=True, transpose_a=True)
 
 
 def exchange(cands, owners_block):
-    n_state = lax.axis_size("state")
     obs = cands.shape[1]
     tile = obs // owners_block.shape[0]
-    gathered = lax.all_gather(cands, "state", axis=0)
     own_each = jnp.repeat(owners_block, tile)
-    pick = own_each[None, :] == jnp.arange(n_state, dtype=own_each.dtype)[:, None]
-    return jnp.sum(jnp.where(pick[:, None, :], gathered, 0.0), axis=0)
+    mine = own_each[None, :] == lax.axis_index("state")
+    return tree_sum_exact(jnp.where(mine, cands, 0.0), "state")
 
 
 def analyse(current, observed, target, noise):
@@ -45,11 +86,15 @@
     gram_loc = tdot(obs_c, obs_c)
     cross_loc = tdot(obs_c, row_c)
 
-    slots = jnp.zeros((n_member, obs + n_rows), jnp.float32)
+    width = -(-(obs + n_rows) // obs) * obs
+    slots = jnp.zeros((n_member, width), jnp.float32)
     slots = lax.dynamic_update_slice(slots, jnp.concatenate([obs_loc, row_loc])[None, :], (me, 0))
-    gram_sum, slots = lax.psum((gram_loc, slots), "member")
+    packed = jnp.concatenate([gram_loc, slots.reshape(-1, obs)], axis=0)
+    packed = tree_sum(packed, "member")
+    gram_sum = packed[:obs]
+    slots = packed[obs:].reshape(n_member, width)[:, : obs + n_rows]
     cross_loc, gram_sum, slots = lax.optimization_barrier((cross_loc, gram_sum, slots))
-    cross_sum = lax.psum(cross_loc, "member")
+    cross_sum = tree_sum(cross_loc, "member")
 
     means = jnp.mean(slots, axis=0)
     dev = slots - means[None, :]

time: 438 us -> 380 us (0.87)
  waiting for transfers between devices: 177 us -> 92.7 us
  starting transfers between devices: 0.47 us -> 52 us
  blocking collectives: 15.8 us -> 0 us
  between operations: 17.9 us -> 5.45 us
  other arithmetic: 173 us -> 180 us
  matrix products: 23.7 us -> 17.3 us
    psum x4 -> x0, waiting for transfers between devices: 177 us -> none  [the longest x2 177 us: analyse(): gram_sum, slots = lax.psum((gram_loc, slots), 'member')]
    ppermute x0 -> x34, waiting for transfers between devices: none -> 92.7 us  [the longest x16 42.2 us: tree_sum(): other = lax.ppermute(cur, axis, perm)]
    ppermute x0 -> x34, starting transfers between devices: none -> 52 us  [the longest x16 24.6 us: tree_sum(): cur = keep + lax.ppermute(send, axis, perm)]
    all_gather x2 -> x0, blocking collectives: 15.8 us -> none  [exchange(): gathered = lax.all_gather(cands, 'state', axis=0)]
    dot_general x8, matrix products: 12.7 us -> 6.8 us  [tdot(): lax.dot_general(left, right, (((0,), (0,)), ((), ())), precision=lax.Prec...]
  transfers between devices with their start and end apart: 4 -> 34, of which waited for: 2 -> 31; matrix products, arithmetic and copies ran while one was open for 46% -> 22% of each run, Pallas kernels for 0% -> 0%
where the time goes in v2:
time: 380 us; the launch traced here: 376 us
  other arithmetic  180 us (47%)
  waiting for transfers between devices  92.7 us (24%)
  starting transfers between devices  52 us (14%)
  local copies, waits for them, and re-layouts  28.6 us (8%)
  matrix products  17.3 us (5%)
  between operations  5.45 us (1%)
    another operation x21, other arithmetic, analyse(): factor = jnp.linalg.cholesky(innov_cov)  114 us
    another operation x5, other arithmetic, solve_gram(): lax.linalg.triangular_solve(factor, half, left_side=True, lower=True, tra...  60.2 us
    ppermute x16, waiting for transfers between devices, tree_sum(): other = lax.ppermute(cur, axis, perm)  42.2 us
    ppermute x16, waiting for transfers between devices, tree_sum(): cur = keep + lax.ppermute(send, axis, perm)  40.2 us
    ppermute x16, starting transfers between devices, tree_sum(): cur = keep + lax.ppermute(send, axis, perm)  24.6 us
    ppermute x16, starting transfers between devices, tree_sum(): other = lax.ppermute(cur, axis, perm)  22.8 us
    another operation x21, local copies, waits for them, and re-layouts, solve_gram(): lax.linalg.triangular_solve(factor, half, left_side=True, lower=True, tra...  12.4 us
    ppermute x2, waiting for transfers between devices, tree_sum_exact(): x = x + lax.ppermute(x, axis, perm)  10.3 us
  transfers between devices with their start and end apart: 34, of which 31 were waited for; matrix products, arithmetic and copies ran while one was open for 22% of the time, Pallas kernels for 0%

profile of v2, /device:TPU:0, one launch (start us, length us, event | category | flops | bytes accessed | tf_op | source)
XLA Modules:
  0.0 376.3 jit_solution(17773248566609353831)
XLA Ops:
  4.0 3.0 collective-permute-start
  7.1 4.8 %collective-permute-done = f32[128,384]{0,1:T(8,128)S(1)} collective-permute-done((f32[128,384]{0,1:T(8,128)S(1)}, f32[128,384]{0,1:T(8,128)S(1)}, u32[]{:S(2)}, u32[]{:S(2)}) %collective-permute-start) | collective-permute-done | bytes 196640 | tf_op jit(solution)/shard_map/ppermute | solution.py:56
  17.6 4.2 %collective-permute-done.2 = f32[108,384]{1,0:T(8,128)S(1)} collective-permute-done((f32[108,384]{1,0:T(8,128)S(1)}, f32[108,384]{1,0:T(8,128)S(1)}, u32[]{:S(2)}, u32[]{:S(2)}) %collective-permute-start.2) | collective-permute-done | bytes 165920 | tf_op jit(solution)/shard_map/ppermute | solution.py:37
  26.4 2.9 collective-permute-start.4
  31.5 2.9 collective-permute-start.5
  38.8 3.8 %collective-permute-done.6 = f32[54,384]{0,1:T(8,128)S(1)} collective-permute-done((f32[54,384]{0,1:T(8,128)S(1)}, f32[54,384]{0,1:T(8,128)S(1)}, u32[]{:S(2)}, u32[]{:S(2)}) %collective-permute-start.6) | collective-permute-done | bytes 82976 | tf_op jit(solution)/shard_map/ppermute | solution.py:43
  54.8 11.7 %cholesky.208 = f32[128,128]{1,0:T(8,128)S(1)} custom-call(f32[128,128]{1,0:T(8,128)S(1)} %cholesky.310), custom_call_target="Cholesky" | custom-call | tf_op jit(solution)/shard_map/jit(cholesky)/cholesky | solution.py:106
  66.6 9.8 %custom-call.24 = f32[1,128,128]{1,2,0:T(8,128)S(1)} custom-call(f32[1,128,128]{2,1,0:T(8,128)S(1)} %get-tuple-element.100), custom_call_target="InvertDiagBlocksLowerTriangular" | custom-call | tf_op jit(solution)/shard_map/jit(cholesky)/cholesky | solution.py:106
  77.0 12.1 %cholesky.227 = f32[128,128]{1,0:T(8,128)S(1)} custom-call(f32[128,128]{1,0:T(8,128)S(1)} %cholesky.314), custom_call_target="Cholesky" | custom-call | tf_op jit(solution)/shard_map/jit(cholesky)/cholesky | solution.py:106
  89.1 9.8 %custom-call.25 = f32[1,128,128]{1,2,0:T(8,128)S(1)} custom-call(f32[1,128,128]{2,1,0:T(8,128)S(1)} %get-tuple-element.97), custom_call_target="InvertDiagBlocksLowerTriangular" | custom-call | tf_op jit(solution)/shard_map/jit(cholesky)/cholesky | solution.py:106
  99.4 11.7 %cholesky.246 = f32[128,128]{1,0:T(8,128)S(1)} custom-call(f32[128,128]{1,0:T(8,128)S(1)} %convolution_subtract_fusion.11), custom_call_target="Cholesky" | custom-call | tf_op jit(solution)/shard_map/jit(cholesky)/cholesky | solution.py:106
  115.6 6.5 %while.8 = (s32[]{:T(128)}, f32[384,384]{1,0:T(8,128)S(1)}, s32[3,2]{0,1:T(2,128)S(1)}, f32[3,128,128]{2,1,0:T(8,128)S(1)}, s32[]{:T(128)}) while((s32[]{:T(128)}, f32[384,384]{1,0:T(8,128)S(1)}, s32[3,2]{0,1:T(2,128)S(1)}, f32[3,128,128]{2,1,0:T(8,128)S(1)}, s32[]{:T(128)}) %tuple.71), condition=%wide.while_cond.1, body=%wide.while_body.1.sunk | while | flops 2 | bytes 131181 | solution.py:63
  125.3 30.3 %custom-call.27 = f32[3,128,128]{1,2,0:T(8,128)S(1)} custom-call(f32[3,128,128]{2,1,0:T(8,128)} %copy-done.5), custom_call_target="InvertDiagBlocksLowerTriangular" | custom-call | tf_op jit(solution)/shard_map/triangular_solve/custom-call.6 | solution.py:63
  157.9 3.6 collective-permute-done.11
  161.5 3.2 collective-permute-start.12
  174.5 2.8 collective-permute-done.14
  178.5 5.2 %collective-permute-done.15 = f32[96,640]{1,0:T(8,128)S(1)} collective-permute-done((f32[96,640]{1,0:T(8,128)S(1)}, f32[96,640]{1,0:T(8,128)S(1)}, u32[]{:S(2)}, u32[]{:S(2)}) %collective-permute-start.15) | collective-permute-done | bytes 245792 | tf_op jit(solution)/shard_map/ppermute | solution.py:43
  191.9 5.4 %collective-permute-done.17 = f32[128,384]{0,1:T(8,128)S(1)} collective-permute-done((f32[128,384]{0,1:T(8,128)S(1)}, f32[128,384]{0,1:T(8,128)S(1)}, u32[]{:S(2)}, u32[]{:S(2)}) %collective-permute-start.17) | collective-permute-done | bytes 196640 | tf_op jit(solution)/shard_map/ppermute | solution.py:56
  201.3 5.9 %collective-permute-done.19 = f32[108,384]{1,0:T(8,128)S(1)} collective-permute-done((f32[108,384]{1,0:T(8,128)S(1)}, f32[108,384]{1,0:T(8,128)S(1)}, u32[]{:S(2)}, u32[]{:S(2)}) %collective-permute-start.19) | collective-permute-done | bytes 165920 | tf_op jit(solution)/shard_map/ppermute | solution.py:37
  224.2 3.9 %collective-permute-done.23 = f32[54,384]{0,1:T(8,128)S(1)} collective-permute-done((f32[54,384]{0,1:T(8,128)S(1)}, f32[54,384]{0,1:T(8,128)S(1)}, u32[]{:S(2)}, u32[]{:S(2)}) %collective-permute-start.23) | collective-permute-done | bytes 82976 | tf_op jit(solution)/shard_map/ppermute | solution.py:43
  228.9 5.1 %collective-permute-done.24 = f32[108,384]{0,1:T(8,128)S(1)} collective-permute-done((f32[108,384]{0,1:T(8,128)S(1)}, f32[108,384]{0,1:T(8,128)S(1)}, u32[]{:S(2)}, u32[]{:S(2)}) %collective-permute-start.24) | collective-permute-done | bytes 165920 | tf_op jit(solution)/shard_map/ppermute | solution.py:43
  239.4 11.7 %cholesky.261 = f32[128,128]{1,0:T(8,128)S(1)} custom-call(f32[128,128]{1,0:T(8,128)S(1)} %cholesky.318), custom_call_target="Cholesky" | custom-call | tf_op jit(solution)/shard_map/jit(cholesky)/cholesky | solution.py:106
  251.2 9.8 %custom-call.28 = f32[1,128,128]{1,2,0:T(8,128)S(1)} custom-call(f32[1,128,128]{2,1,0:T(8,128)S(1)} %get-tuple-element.93), custom_call_target="InvertDiagBlocksLowerTriangular" | custom-call | tf_op jit(solution)/shard_map/jit(cholesky)/cholesky | solution.py:106
  261.6 11.9 %cholesky.280 = f32[128,128]{1,0:T(8,128)S(1)} custom-call(f32[128,128]{1,0:T(8,128)S(1)} %cholesky.322), custom_call_target="Cholesky" | custom-call | tf_op jit(solution)/shard_map/jit(cholesky)/cholesky | solution.py:106
  274.9 9.8 %custom-call.29 = f32[1,128,128]{1,2,0:T(8,128)S(1)} custom-call(f32[1,128,128]{2,1,0:T(8,128)S(1)} %get-tuple-element.90), custom_call_target="InvertDiagBlocksLowerTriangular" | custom-call | tf_op jit(solution)/shard_map/jit(cholesky)/cholesky | solution.py:106
  285.2 11.7 %cholesky.299 = f32[128,128]{1,0:T(8,128)S(1)} custom-call(f32[128,128]{1,0:T(8,128)S(1)} %convolution_subtract_fusion.6), custom_call_target="Cholesky" | custom-call | tf_op jit(solution)/shard_map/jit(cholesky)/cholesky | solution.py:106
  299.8 6.0 %while.9 = (s32[]{:T(128)}, f32[384,384]{1,0:T(8,128)S(1)}, s32[3,2]{0,1:T(2,128)S(1)}, f32[3,128,128]{2,1,0:T(8,128)S(1)}, s32[]{:T(128)}) while((s32[]{:T(128)}, f32[384,384]{1,0:T(8,128)S(1)}, s32[3,2]{0,1:T(2,128)S(1)}, f32[3,128,128]{2,1,0:T(8,128)S(1)}, s32[]{:T(128)}) %tuple.77), condition=%wide.while_cond.1.clone, body=%wide.while_body.1.clone.sunk | while | flops 2 | bytes 131181 | solution.py:63
  305.8 29.7 %custom-call.31 = f32[3,128,128]{1,2,0:T(8,128)S(1)} custom-call(f32[3,128,128]{2,1,0:T(8,128)S(1)} %get-tuple-element.52), custom_call_target="InvertDiagBlocksLowerTriangular" | custom-call | tf_op jit(solution)/shard_map/triangular_solve/custom-call.6 | solution.py:63
  338.0 7.2 %collective-permute-done.27 = f32[96,640]{1,0:T(8,128)S(1)} collective-permute-done((f32[96,640]{1,0:T(8,128)S(1)}, f32[96,640]{1,0:T(8,128)S(1)}, u32[]{:S(2)}, u32[]{:S(2)}) %collective-permute-start.27) | collective-permute-done | bytes 245792 | tf_op jit(solution)/shard_map/ppermute | solution.py:37
  350.2 3.3 collective-permute-start.29
  355.7 3.0 collective-permute-start.30
  367.2 5.2 %collective-permute-done.32 = f32[96,640]{1,0:T(8,128)S(1)} collective-permute-done((f32[96,640]{1,0:T(8,128)S(1)}, f32[96,640]{1,0:T(8,128)S(1)}, u32[]{:S(2)}, u32[]{:S(2)}) %collective-permute-start.32) | collective-permute-done | bytes 245792 | tf_op jit(solution)/shard_map/ppermute | solution.py:43
  (267 shorter events, 125.1 us)
Async XLA Ops:
  4.0 7.9 %collective-permute-start = (f32[128,384]{0,1:T(8,128)S(1)}, f32[128,384]{0,1:T(8,128)S(1)}, u32[]{:S(2)}, u32[]{:S(2)}) collective-permute-start(f32[128,384]{0,1:T(8,128)S(1)} %bitcast_select_fusion), channel_id=1, source_target_pairs={{0,16},{16,0},{1,17},{17,1},{2,18},{18,2},{3,19},{19,3},{4,20},{20... | collective-permute-start | bytes 589832 | tf_op jit(solution)/shard_map/ppermute | solution.py:56
  15.3 6.5 %collective-permute-start.2 = (f32[108,384]{1,0:T(8,128)S(1)}, f32[108,384]{1,0:T(8,128)S(1)}, u32[]{:S(2)}, u32[]{:S(2)}) collective-permute-start(f32[108,384]{1,0:T(8,128)S(1)} %constant_dynamic-slice_fusion.15), channel_id=1, source_target_pairs={{0,2},{1,3},{2,0},{3,1},{4,6},{5,7},{6,4},{7,5},{8,10},{9,11},{10,... | collective-permute-start | bytes 497672 | tf_op jit(solution)/shard_map/ppermute | solution.py:37
  21.8 4.6 %collective-permute-start.3 = (f32[54,384]{1,0:T(8,128)S(1)}, f32[54,384]{1,0:T(8,128)S(1)}, u32[]{:S(2)}, u32[]{:S(2)}) collective-permute-start(f32[54,384]{1,0:T(8,128)S(1)} %constant_dynamic-slice_fusion.14), channel_id=1, source_target_pairs={{0,4},{1,5},{2,6},{3,7},{4,0},{5,1},{6,2},{7,3},{8,12},{9,13},{10,... | collective-permute-start | bytes 248840 | tf_op jit(solution)/shard_map/ppermute | solution.py:37
  26.4 5.1 %collective-permute-start.4 = (f32[27,384]{1,0:T(8,128)S(1)}, f32[27,384]{1,0:T(8,128)S(1)}, u32[]{:S(2)}, u32[]{:S(2)}) collective-permute-start(f32[27,384]{1,0:T(8,128)S(1)} %constant_dynamic-slice_fusion.13), channel_id=1, source_target_pairs={{0,8},{1,9},{2,10},{3,11},{4,12},{5,13},{6,14},{7,15},{8,0},{9,1},... | collective-permute-start | bytes 124424 | tf_op jit(solution)/shard_map/ppermute | solution.py:37
  31.5 5.1 %collective-permute-start.5 = (f32[27,384]{1,0:T(8,128)S(1)}, f32[27,384]{1,0:T(8,128)S(1)}, u32[]{:S(2)}, u32[]{:S(2)}) collective-permute-start(f32[27,384]{1,0:T(8,128)S(1)} %dynamic-slice_add_fusion.13), channel_id=1, source_target_pairs={{0,8},{1,9},{2,10},{3,11},{4,12},{5,13},{6,14},{7,15},{8,0},{9,1},... | collective-permute-start | bytes 124424 | tf_op jit(solution)/shard_map/ppermute | solution.py:43
  36.9 5.7 %collective-permute-start.6 = (f32[54,384]{0,1:T(8,128)S(1)}, f32[54,384]{0,1:T(8,128)S(1)}, u32[]{:S(2)}, u32[]{:S(2)}) collective-permute-start(f32[54,384]{0,1:T(8,128)S(1)} %broadcast_select_fusion.1), channel_id=1, source_target_pairs={{0,4},{1,5},{2,6},{3,7},{4,0},{5,1},{6,2},{7,3},{8,12},{9,13},{10,... | collective-permute-start | bytes 248840 | tf_op jit(solution)/shard_map/ppermute | solution.py:43
  42.8 5.7 %collective-permute-start.7 = (f32[108,384]{0,1:T(8,128)S(1)}, f32[108,384]{0,1:T(8,128)S(1)}, u32[]{:S(2)}, u32[]{:S(2)}) collective-permute-start(f32[108,384]{0,1:T(8,128)S(1)} %maximum_select_fusion.10), channel_id=1, source_target_pairs={{0,2},{1,3},{2,0},{3,1},{4,6},{5,7},{6,4},{7,5},{8,10},{9,11},{10,... | collective-permute-start | bytes 497672 | tf_op jit(solution)/shard_map/ppermute | solution.py:43
  48.8 1.8 collective-permute-start.8
  112.7 9.4 %collective-permute-start.9 = (f32[192,640]{1,0:T(8,128)}, f32[192,640]{1,0:T(8,128)}, u32[]{:S(2)}, u32[]{:S(2)}) collective-permute-start(f32[192,640]{1,0:T(8,128)} %constant_dynamic-slice_fusion.12), channel_id=1, source_target_pairs={{0,1},{1,0},{2,3},{3,2},{4,5},{5,4},{6,7},{7,6},{8,9},{9,8},{10,11... | collective-permute-start | bytes 1474568 | tf_op jit(solution)/shard_map/ppermute | solution.py:37
  123.3 32.6 %collective-permute-start.10 = (f32[96,640]{1,0:T(8,128)S(1)}, f32[96,640]{1,0:T(8,128)S(1)}, u32[]{:S(2)}, u32[]{:S(2)}) collective-permute-start(f32[96,640]{1,0:T(8,128)S(1)} %constant_dynamic-slice_fusion.11), channel_id=1, source_target_pairs={{0,2},{1,3},{2,0},{3,1},{4,6},{5,7},{6,4},{7,5},{8,10},{9,11},{10,... | collective-permute-start | bytes 737288 | tf_op jit(solution)/shard_map/ppermute | solution.py:37
  156.0 5.4 %collective-permute-start.11 = (f32[48,640]{1,0:T(8,128)S(1)}, f32[48,640]{1,0:T(8,128)S(1)}, u32[]{:S(2)}, u32[]{:S(2)}) collective-permute-start(f32[48,640]{1,0:T(8,128)S(1)} %constant_dynamic-slice_fusion.10), channel_id=1, source_target_pairs={{0,4},{1,5},{2,6},{3,7},{4,0},{5,1},{6,2},{7,3},{8,12},{9,13},{10,... | collective-permute-start | bytes 368648 | tf_op jit(solution)/shard_map/ppermute | solution.py:37
  161.5 5.8 %collective-permute-start.12 = (f32[24,640]{1,0:T(8,128)S(1)}, f32[24,640]{1,0:T(8,128)S(1)}, u32[]{:S(2)}, u32[]{:S(2)}) collective-permute-start(f32[24,640]{1,0:T(8,128)S(1)} %constant_dynamic-slice_fusion.9), channel_id=1, source_target_pairs={{0,8},{1,9},{2,10},{3,11},{4,12},{5,13},{6,14},{7,15},{8,0},{9,1},... | collective-permute-start | bytes 184328 | tf_op jit(solution)/shard_map/ppermute | solution.py:37
  167.2 5.2 %collective-permute-start.13 = (f32[24,640]{1,0:T(8,128)S(1)}, f32[24,640]{1,0:T(8,128)S(1)}, u32[]{:S(2)}, u32[]{:S(2)}) collective-permute-start(f32[24,640]{1,0:T(8,128)S(1)} %dynamic-slice_add_fusion.11), channel_id=1, source_target_pairs={{0,8},{1,9},{2,10},{3,11},{4,12},{5,13},{6,14},{7,15},{8,0},{9,1},... | collective-permute-start | bytes 184328 | tf_op jit(solution)/shard_map/ppermute | solution.py:43
  172.4 4.9 %collective-permute-start.14 = (f32[48,640]{1,0:T(8,128)S(1)}, f32[48,640]{1,0:T(8,128)S(1)}, u32[]{:S(2)}, u32[]{:S(2)}) collective-permute-start(f32[48,640]{1,0:T(8,128)S(1)} %maximum_select_fusion.12), channel_id=1, source_target_pairs={{0,4},{1,5},{2,6},{3,7},{4,0},{5,1},{6,2},{7,3},{8,12},{9,13},{10,... | collective-permute-start | bytes 368648 | tf_op jit(solution)/shard_map/ppermute | solution.py:43
  177.4 6.3 %collective-permute-start.15 = (f32[96,640]{1,0:T(8,128)S(1)}, f32[96,640]{1,0:T(8,128)S(1)}, u32[]{:S(2)}, u32[]{:S(2)}) collective-permute-start(f32[96,640]{1,0:T(8,128)S(1)} %maximum_select_fusion.8), channel_id=1, source_target_pairs={{0,2},{1,3},{2,0},{3,1},{4,6},{5,7},{6,4},{7,5},{8,10},{9,11},{10,... | collective-permute-start | bytes 737288 | tf_op jit(solution)/shard_map/ppermute | solution.py:43
  183.7 1.9 collective-permute-start.16
  190.4 7.0 %collective-permute-start.17 = (f32[128,384]{0,1:T(8,128)S(1)}, f32[128,384]{0,1:T(8,128)S(1)}, u32[]{:S(2)}, u32[]{:S(2)}) collective-permute-start(f32[128,384]{0,1:T(8,128)S(1)} %fusion.6), channel_id=1, source_target_pairs={{0,16},{16,0},{1,17},{17,1},{2,18},{18,2},{3,19},{19,3},{4,20},{20... | collective-permute-start | bytes 589832 | tf_op jit(solution)/shard_map/ppermute | solution.py:56
  200.7 6.5 %collective-permute-start.19 = (f32[108,384]{1,0:T(8,128)S(1)}, f32[108,384]{1,0:T(8,128)S(1)}, u32[]{:S(2)}, u32[]{:S(2)}) collective-permute-start(f32[108,384]{1,0:T(8,128)S(1)} %constant_dynamic-slice_fusion.8), channel_id=1, source_target_pairs={{0,2},{1,3},{2,0},{3,1},{4,6},{5,7},{6,4},{7,5},{8,10},{9,11},{10,... | collective-permute-start | bytes 497672 | tf_op jit(solution)/shard_map/ppermute | solution.py:37
  207.3 4.6 %collective-permute-start.20 = (f32[54,384]{1,0:T(8,128)S(1)}, f32[54,384]{1,0:T(8,128)S(1)}, u32[]{:S(2)}, u32[]{:S(2)}) collective-permute-start(f32[54,384]{1,0:T(8,128)S(1)} %constant_dynamic-slice_fusion.7), channel_id=1, source_target_pairs={{0,4},{1,5},{2,6},{3,7},{4,0},{5,1},{6,2},{7,3},{8,12},{9,13},{10,... | collective-permute-start | bytes 248840 | tf_op jit(solution)/shard_map/ppermute | solution.py:37
  211.9 5.1 %collective-permute-start.21 = (f32[27,384]{1,0:T(8,128)S(1)}, f32[27,384]{1,0:T(8,128)S(1)}, u32[]{:S(2)}, u32[]{:S(2)}) collective-permute-start(f32[27,384]{1,0:T(8,128)S(1)} %constant_dynamic-slice_fusion.6), channel_id=1, source_target_pairs={{0,8},{1,9},{2,10},{3,11},{4,12},{5,13},{6,14},{7,15},{8,0},{9,1},... | collective-permute-start | bytes 124424 | tf_op jit(solution)/shard_map/ppermute | solution.py:37
  216.9 5.1 %collective-permute-start.22 = (f32[27,384]{1,0:T(8,128)S(1)}, f32[27,384]{1,0:T(8,128)S(1)}, u32[]{:S(2)}, u32[]{:S(2)}) collective-permute-start(f32[27,384]{1,0:T(8,128)S(1)} %dynamic-slice_add_fusion.12), channel_id=1, source_target_pairs={{0,8},{1,9},{2,10},{3,11},{4,12},{5,13},{6,14},{7,15},{8,0},{9,1},... | collective-permute-start | bytes 124424 | tf_op jit(solution)/shard_map/ppermute | solution.py:43
  222.4 5.7 %collective-permute-start.23 = (f32[54,384]{0,1:T(8,128)S(1)}, f32[54,384]{0,1:T(8,128)S(1)}, u32[]{:S(2)}, u32[]{:S(2)}) collective-permute-start(f32[54,384]{0,1:T(8,128)S(1)} %broadcast_select_fusion), channel_id=1, source_target_pairs={{0,4},{1,5},{2,6},{3,7},{4,0},{5,1},{6,2},{7,3},{8,12},{9,13},{10,... | collective-permute-start | bytes 248840 | tf_op jit(solution)/shard_map/ppermute | solution.py:43
  228.3 5.7 %collective-permute-start.24 = (f32[108,384]{0,1:T(8,128)S(1)}, f32[108,384]{0,1:T(8,128)S(1)}, u32[]{:S(2)}, u32[]{:S(2)}) collective-permute-start(f32[108,384]{0,1:T(8,128)S(1)} %maximum_select_fusion.11), channel_id=1, source_target_pairs={{0,2},{1,3},{2,0},{3,1},{4,6},{5,7},{6,4},{7,5},{8,10},{9,11},{10,... | collective-permute-start | bytes 497672 | tf_op jit(solution)/shard_map/ppermute | solution.py:43
  234.3 1.8 collective-permute-start.25
  297.6 38.1 %collective-permute-start.26 = (f32[192,640]{1,0:T(8,128)S(1)}, f32[192,640]{1,0:T(8,128)}, u32[]{:S(2)}, u32[]{:S(2)}) collective-permute-start(f32[192,640]{1,0:T(8,128)S(1)} %constant_dynamic-slice_fusion.5), channel_id=1, source_target_pairs={{0,1},{1,0},{2,3},{3,2},{4,5},{5,4},{6,7},{7,6},{8,9},{9,8},{10,11... | collective-permute-start | bytes 1474568 | tf_op jit(solution)/shard_map/ppermute | solution.py:37
  336.9 8.3 %collective-permute-start.27 = (f32[96,640]{1,0:T(8,128)S(1)}, f32[96,640]{1,0:T(8,128)S(1)}, u32[]{:S(2)}, u32[]{:S(2)}) collective-permute-start(f32[96,640]{1,0:T(8,128)S(1)} %constant_dynamic-slice_fusion.4), channel_id=1, source_target_pairs={{0,2},{1,3},{2,0},{3,1},{4,6},{5,7},{6,4},{7,5},{8,10},{9,11},{10,... | collective-permute-start | bytes 737288 | tf_op jit(solution)/shard_map/ppermute | solution.py:37
  345.2 4.9 %collective-permute-start.28 = (f32[48,640]{1,0:T(8,128)S(1)}, f32[48,640]{1,0:T(8,128)S(1)}, u32[]{:S(2)}, u32[]{:S(2)}) collective-permute-start(f32[48,640]{1,0:T(8,128)S(1)} %constant_dynamic-slice_fusion.3), channel_id=1, source_target_pairs={{0,4},{1,5},{2,6},{3,7},{4,0},{5,1},{6,2},{7,3},{8,12},{9,13},{10,... | collective-permute-start | bytes 368648 | tf_op jit(solution)/shard_map/ppermute | solution.py:37
  350.2 5.5 %collective-permute-start.29 = (f32[24,640]{1,0:T(8,128)S(1)}, f32[24,640]{1,0:T(8,128)S(1)}, u32[]{:S(2)}, u32[]{:S(2)}) collective-permute-start(f32[24,640]{1,0:T(8,128)S(1)} %constant_dynamic-slice_fusion.2), channel_id=1, source_target_pairs={{0,8},{1,9},{2,10},{3,11},{4,12},{5,13},{6,14},{7,15},{8,0},{9,1},... | collective-permute-start | bytes 184328 | tf_op jit(solution)/shard_map/ppermute | solution.py:37
  355.7 5.4 %collective-permute-start.30 = (f32[24,640]{1,0:T(8,128)S(1)}, f32[24,640]{1,0:T(8,128)S(1)}, u32[]{:S(2)}, u32[]{:S(2)}) collective-permute-start(f32[24,640]{1,0:T(8,128)S(1)} %dynamic-slice_add_fusion.10), channel_id=1, source_target_pairs={{0,8},{1,9},{2,10},{3,11},{4,12},{5,13},{6,14},{7,15},{8,0},{9,1},... | collective-permute-start | bytes 184328 | tf_op jit(solution)/shard_map/ppermute | solution.py:43
  361.1 4.9 %collective-permute-start.31 = (f32[48,640]{1,0:T(8,128)S(1)}, f32[48,640]{1,0:T(8,128)S(1)}, u32[]{:S(2)}, u32[]{:S(2)}) collective-permute-start(f32[48,640]{1,0:T(8,128)S(1)} %maximum_select_fusion.13), channel_id=1, source_target_pairs={{0,4},{1,5},{2,6},{3,7},{4,0},{5,1},{6,2},{7,3},{8,12},{9,13},{10,... | collective-permute-start | bytes 368648 | tf_op jit(solution)/shard_map/ppermute | solution.py:43
  366.1 6.3 %collective-permute-start.32 = (f32[96,640]{1,0:T(8,128)S(1)}, f32[96,640]{1,0:T(8,128)S(1)}, u32[]{:S(2)}, u32[]{:S(2)}) collective-permute-start(f32[96,640]{1,0:T(8,128)S(1)} %maximum_select_fusion.9), channel_id=1, source_target_pairs={{0,2},{1,3},{2,0},{3,1},{4,6},{5,7},{6,4},{7,5},{8,10},{9,11},{10,... | collective-permute-start | bytes 737288 | tf_op jit(solution)/shard_map/ppermute | solution.py:43
  372.4 1.9 collective-permute-start.33
  (16 other events, 47.0 us)

commit v3 on v2

--- a/solution.py
+++ b/solution.py
@@ -63,6 +63,36 @@
     return lax.linalg.triangular_solve(factor, half, left_side=True, lower=True, transpose_a=True)
 
 
+def block_solve(cov, right, size):
+    nb = cov.shape[0] // size
+    if nb * size != cov.shape[0]:
+        return solve_gram(jnp.linalg.cholesky(cov), right)
+    cov = 0.5 * (cov + cov.T)
+    eye = jnp.eye(size, dtype=cov.dtype)
+    blk = [[cov[i * size:(i + 1) * size, j * size:(j + 1) * size] for j in range(nb)] for i in range(nb)]
+    rhs = [right[i * size:(i + 1) * size] for i in range(nb)]
+    low = [[None] * nb for _ in range(nb)]
+    inv = [None] * nb
+    fwd = [None] * nb
+    for k in range(nb):
+        diag = jnp.linalg.cholesky(blk[k][k], symmetrize_input=False)
+        inv[k] = lax.linalg.triangular_solve(diag, eye, left_side=True, lower=True)
+        fwd[k] = full_dot(inv[k], rhs[k])
+        for i in range(k + 1, nb):
+            low[i][k] = full_dot(blk[i][k], inv[k].T)
+        for i in range(k + 1, nb):
+            for j in range(k + 1, i + 1):
+                blk[i][j] = blk[i][j] - full_dot(low[i][k], low[j][k].T)
+            rhs[i] = rhs[i] - full_dot(low[i][k], fwd[k])
+    out = [None] * nb
+    for k in reversed(range(nb)):
+        acc = fwd[k]
+        for j in range(k + 1, nb):
+            acc = acc - tdot(low[j][k], out[j])
+        out[k] = tdot(inv[k], acc)
+    return jnp.concatenate(out, axis=0)
+
+
 def exchange(cands, owners_block):
     obs = cands.shape[1]
     tile = obs // owners_block.shape[0]
@@ -103,10 +133,9 @@
     dev_row = dev[:, obs:]
 
     innov_cov = (gram_sum + m_loc * tdot(dev_obs, dev_obs)) / (count - 1.0) + jnp.diag(noise)
-    factor = jnp.linalg.cholesky(innov_cov)
     obs_anom = observed - obs_mean[None, :]
     rhs = (target - obs_mean)[:, None] - 0.5 * obs_anom.T
-    gain = solve_gram(factor, rhs)
+    gain = block_solve(innov_cov, rhs, 128)
 
     cross = (cross_sum + m_loc * tdot(dev_obs, dev_row)) / (count - 1.0)
     return gain, cross

time: 380 us -> 328 us (0.86)
  other arithmetic: 180 us -> 142 us
  local copies, waits for them, and re-layouts: 28.6 us -> 15.4 us
  matrix products: 17.3 us -> 25.7 us
  waiting for transfers between devices: 92.7 us -> 84.5 us
    another operation x26 -> x30, other arithmetic: 174 us -> 138 us  [the longest x18 75 us: block_solve(): diag = jnp.linalg.cholesky(blk[k][k], symmetrize_input=False)]
    another operation x29 -> x2, local copies, waits for them, and re-layouts: 12.5 us -> 0.01 us  [the longest x21 12.4 us: solve_gram(): lax.linalg.triangular_solve(factor, half, left_side=True, lower=True, tra...]
    dot_general x3 -> x29, matrix products: 3.23 us -> 13.6 us  [full_dot(): jnp.dot(left, right, precision=lax.Precision.HIGHEST, preferred_element_t...]
    ppermute x16, waiting for transfers between devices: 40.2 us -> 34.4 us  [tree_sum(): cur = keep + lax.ppermute(send, axis, perm)]
    another operation x28 -> x6, matrix products: 7.23 us -> 1.7 us  [block_solve(): inv[k] = lax.linalg.triangular_solve(diag, eye, left_side=True, lower=True)]
    dot_general x8 -> x20, matrix products: 6.8 us -> 10.4 us  [tdot(): lax.dot_general(left, right, (((0,), (0,)), ((), ())), precision=lax.Prec...]
  transfers between devices with their start and end apart: 34 -> 34, of which waited for: 31 -> 32; matrix products, arithmetic and copies ran while one was open for 22% -> 10% of each run, Pallas kernels for 0% -> 0%
where the time goes in v3:
time: 328 us; the launch traced here: 324 us
  other arithmetic  142 us (43%)
  waiting for transfers between devices  84.5 us (26%)
  starting transfers between devices  54.7 us (17%)
  matrix products  25.7 us (8%)
  local copies, waits for them, and re-layouts  15.4 us (5%)
    another operation x18, other arithmetic, block_solve(): diag = jnp.linalg.cholesky(blk[k][k], symmetrize_input=False)  75 us
    another operation x12, other arithmetic, block_solve(): inv[k] = lax.linalg.triangular_solve(diag, eye, left_side=True, lower=True)  63 us
    ppermute x16, waiting for transfers between devices, tree_sum(): other = lax.ppermute(cur, axis, perm)  39.8 us
    ppermute x16, waiting for transfers between devices, tree_sum(): cur = keep + lax.ppermute(send, axis, perm)  34.4 us
    ppermute x16, starting transfers between devices, tree_sum(): cur = keep + lax.ppermute(send, axis, perm)  25.5 us
    ppermute x16, starting transfers between devices, tree_sum(): other = lax.ppermute(cur, axis, perm)  24.6 us
    dot_general x29, matrix products, full_dot(): jnp.dot(left, right, precision=lax.Precision.HIGHEST, preferred_element_t...  13.6 us
    dot_general x20, matrix products, tdot(): lax.dot_general(left, right, (((0,), (0,)), ((), ())), precision=lax.Prec...  10.4 us
  transfers between devices with their start and end apart: 34, of which 32 were waited for; matrix products, arithmetic and copies ran while one was open for 10% of the time, Pallas kernels for 0%

profile of v3, /device:TPU:0, one launch (start us, length us, event | category | flops | bytes accessed | tf_op | source)
XLA Modules:
  0.0 323.8 jit_solution(12180867643813201116)
XLA Ops:
  4.0 3.0 collective-permute-start
  7.1 4.8 %collective-permute-done = f32[128,384]{0,1:T(8,128)S(1)} collective-permute-done((f32[128,384]{0,1:T(8,128)S(1)}, f32[128,384]{0,1:T(8,128)S(1)}, u32[]{:S(2)}, u32[]{:S(2)}) %collective-permute-start) | collective-permute-done | bytes 196640 | tf_op jit(solution)/shard_map/ppermute | solution.py:56
  17.1 4.7 %collective-permute-done.2 = f32[108,384]{1,0:T(8,128)S(1)} collective-permute-done((f32[108,384]{1,0:T(8,128)S(1)}, f32[108,384]{1,0:T(8,128)S(1)}, u32[]{:S(2)}, u32[]{:S(2)}) %collective-permute-start.2) | collective-permute-done | bytes 165920 | tf_op jit(solution)/shard_map/ppermute | solution.py:37
  26.4 2.9 collective-permute-start.4
  31.5 2.9 collective-permute-start.5
  38.8 3.8 %collective-permute-done.6 = f32[54,384]{0,1:T(8,128)S(1)} collective-permute-done((f32[54,384]{0,1:T(8,128)S(1)}, f32[54,384]{0,1:T(8,128)S(1)}, u32[]{:S(2)}, u32[]{:S(2)}) %collective-permute-start.6) | collective-permute-done | bytes 82976 | tf_op jit(solution)/shard_map/ppermute | solution.py:43
  54.8 11.7 %cholesky.105 = f32[128,128]{1,0:T(8,128)S(1)} custom-call(f32[128,128]{1,0:T(8,128)S(1)} %slice.168), custom_call_target="Cholesky" | custom-call | tf_op jit(solution)/shard_map/jit(cholesky)/cholesky | solution.py:78
  67.9 9.8 %custom-call.10 = f32[1,128,128]{1,2,0:T(8,128)S(1)} custom-call(f32[1,128,128]{2,1,0:T(8,128)S(1)} %fusion.62), custom_call_target="InvertDiagBlocksLowerTriangular" | custom-call | tf_op jit(solution)/shard_map/triangular_solve/custom-call.0 | solution.py:79
  83.9 12.2 %cholesky.116 = f32[128,128]{1,0:T(8,128)S(1)} custom-call(f32[128,128]{1,0:T(8,128)S(1)} %convolution_subtract_fusion.19), custom_call_target="Cholesky" | custom-call | tf_op jit(solution)/shard_map/jit(cholesky)/cholesky | solution.py:78
  97.4 9.8 %custom-call.11 = f32[1,128,128]{1,2,0:T(8,128)S(1)} custom-call(f32[1,128,128]{2,1,0:T(8,128)S(1)} %fusion.63), custom_call_target="InvertDiagBlocksLowerTriangular" | custom-call | tf_op jit(solution)/shard_map/triangular_solve/custom-call.0 | solution.py:79
  108.1 11.7 %cholesky.127 = f32[128,128]{1,0:T(8,128)S(1)} custom-call(f32[128,128]{1,0:T(8,128)S(1)} %convolution_subtract_fusion.15), custom_call_target="Cholesky" | custom-call | tf_op jit(solution)/shard_map/jit(cholesky)/cholesky | solution.py:78
  124.4 9.8 %custom-call.12 = f32[1,128,128]{1,2,0:T(8,128)S(1)} custom-call(f32[1,128,128]{2,1,0:T(8,128)S(1)} %fusion.64), custom_call_target="InvertDiagBlocksLowerTriangular" | custom-call | tf_op jit(solution)/shard_map/triangular_solve/custom-call.0 | solution.py:79
  136.3 3.3 %collective-permute-done.11 = f32[48,640]{1,0:T(8,128)S(1)} collective-permute-done((f32[48,640]{1,0:T(8,128)S(1)}, f32[48,640]{1,0:T(8,128)S(1)}, u32[]{:S(2)}, u32[]{:S(2)}) %collective-permute-start.11) | collective-permute-done | bytes 122912 | tf_op jit(solution)/shard_map/ppermute | solution.py:37
  139.7 3.2 collective-permute-start.12
  145.2 2.9 collective-permute-start.13
  156.7 4.9 %collective-permute-done.15 = f32[96,640]{1,0:T(8,128)S(1)} collective-permute-done((f32[96,640]{1,0:T(8,128)S(1)}, f32[96,640]{1,0:T(8,128)S(1)}, u32[]{:S(2)}, u32[]{:S(2)}) %collective-permute-start.15) | collective-permute-done | bytes 245792 | tf_op jit(solution)/shard_map/ppermute | solution.py:43
  169.9 5.4 %collective-permute-done.17 = f32[128,384]{0,1:T(8,128)S(1)} collective-permute-done((f32[128,384]{0,1:T(8,128)S(1)}, f32[128,384]{0,1:T(8,128)S(1)}, u32[]{:S(2)}, u32[]{:S(2)}) %collective-permute-start.17) | collective-permute-done | bytes 196640 | tf_op jit(solution)/shard_map/ppermute | solution.py:56
  179.1 5.9 %collective-permute-done.19 = f32[108,384]{1,0:T(8,128)S(1)} collective-permute-done((f32[108,384]{1,0:T(8,128)S(1)}, f32[108,384]{1,0:T(8,128)S(1)}, u32[]{:S(2)}, u32[]{:S(2)}) %collective-permute-start.19) | collective-permute-done | bytes 165920 | tf_op jit(solution)/shard_map/ppermute | solution.py:37
  189.7 3.2 collective-permute-start.21
  194.9 3.0 collective-permute-start.22
  202.4 3.7 %collective-permute-done.23 = f32[54,384]{0,1:T(8,128)S(1)} collective-permute-done((f32[54,384]{0,1:T(8,128)S(1)}, f32[54,384]{0,1:T(8,128)S(1)}, u32[]{:S(2)}, u32[]{:S(2)}) %collective-permute-start.23) | collective-permute-done | bytes 82976 | tf_op jit(solution)/shard_map/ppermute | solution.py:43
  206.9 5.2 %collective-permute-done.24 = f32[108,384]{0,1:T(8,128)S(1)} collective-permute-done((f32[108,384]{0,1:T(8,128)S(1)}, f32[108,384]{0,1:T(8,128)S(1)}, u32[]{:S(2)}, u32[]{:S(2)}) %collective-permute-start.24) | collective-permute-done | bytes 165920 | tf_op jit(solution)/shard_map/ppermute | solution.py:43
  217.7 11.7 %cholesky.138 = f32[128,128]{1,0:T(8,128)S(1)} custom-call(f32[128,128]{1,0:T(8,128)S(1)} %slice.182), custom_call_target="Cholesky" | custom-call | tf_op jit(solution)/shard_map/jit(cholesky)/cholesky | solution.py:78
  230.8 9.8 %custom-call.13 = f32[1,128,128]{1,2,0:T(8,128)S(1)} custom-call(f32[1,128,128]{2,1,0:T(8,128)S(1)} %fusion.65), custom_call_target="InvertDiagBlocksLowerTriangular" | custom-call | tf_op jit(solution)/shard_map/triangular_solve/custom-call.0 | solution.py:79
  242.9 11.9 %cholesky.149 = f32[128,128]{1,0:T(8,128)S(1)} custom-call(f32[128,128]{1,0:T(8,128)S(1)} %convolution_subtract_fusion.9), custom_call_target="Cholesky" | custom-call | tf_op jit(solution)/shard_map/jit(cholesky)/cholesky | solution.py:78
  256.1 9.8 %custom-call.14 = f32[1,128,128]{1,2,0:T(8,128)S(1)} custom-call(f32[1,128,128]{2,1,0:T(8,128)S(1)} %fusion.66), custom_call_target="InvertDiagBlocksLowerTriangular" | custom-call | tf_op jit(solution)/shard_map/triangular_solve/custom-call.0 | solution.py:79
  266.8 11.7 %cholesky.160 = f32[128,128]{1,0:T(8,128)S(1)} custom-call(f32[128,128]{1,0:T(8,128)S(1)} %convolution_subtract_fusion.5), custom_call_target="Cholesky" | custom-call | tf_op jit(solution)/shard_map/jit(cholesky)/cholesky | solution.py:78
  281.8 10.0 %custom-call.15 = f32[1,128,128]{1,2,0:T(8,128)S(1)} custom-call(f32[1,128,128]{2,1,0:T(8,128)S(1)} %fusion.67), custom_call_target="InvertDiagBlocksLowerTriangular" | custom-call | tf_op jit(solution)/shard_map/triangular_solve/custom-call.0 | solution.py:79
  294.5 3.1 collective-permute-done.28
  297.6 3.3 %collective-permute-start.29 = (f32[24,640]{1,0:T(8,128)S(1)}, f32[24,640]{1,0:T(8,128)S(1)}, u32[]{:S(2)}, u32[]{:S(2)}) collective-permute-start(f32[24,640]{1,0:T(8,128)S(1)} %constant_dynamic-slice_fusion), channel_id=1, source_target_pairs={{0,8},{1,9},{2,10},{3,11},{4,12},{5,13},{6,14},{7,15},{8,0},{9,1},... | collective-permute-start | bytes 184328 | tf_op jit(solution)/shard_map/ppermute | solution.py:37
  303.3 2.9 collective-permute-start.30
  315.6 4.1 %collective-permute-done.32 = f32[96,640]{1,0:T(8,128)S(1)} collective-permute-done((f32[96,640]{1,0:T(8,128)S(1)}, f32[96,640]{1,0:T(8,128)S(1)}, u32[]{:S(2)}, u32[]{:S(2)}) %collective-permute-start.32) | collective-permute-done | bytes 245792 | tf_op jit(solution)/shard_map/ppermute | solution.py:43
  (256 shorter events, 115.9 us)
Async XLA Ops:
  4.0 7.9 %collective-permute-start = (f32[128,384]{0,1:T(8,128)S(1)}, f32[128,384]{0,1:T(8,128)S(1)}, u32[]{:S(2)}, u32[]{:S(2)}) collective-permute-start(f32[128,384]{0,1:T(8,128)S(1)} %bitcast_select_fusion), channel_id=1, source_target_pairs={{0,16},{16,0},{1,17},{17,1},{2,18},{18,2},{3,19},{19,3},{4,20},{20... | collective-permute-start | bytes 589832 | tf_op jit(solution)/shard_map/ppermute | solution.py:56
  15.3 6.5 %collective-permute-start.2 = (f32[108,384]{1,0:T(8,128)S(1)}, f32[108,384]{1,0:T(8,128)S(1)}, u32[]{:S(2)}, u32[]{:S(2)}) collective-permute-start(f32[108,384]{1,0:T(8,128)S(1)} %constant_dynamic-slice_fusion.13), channel_id=1, source_target_pairs={{0,2},{1,3},{2,0},{3,1},{4,6},{5,7},{6,4},{7,5},{8,10},{9,11},{10,... | collective-permute-start | bytes 497672 | tf_op jit(solution)/shard_map/ppermute | solution.py:37
  21.8 4.6 %collective-permute-start.3 = (f32[54,384]{1,0:T(8,128)S(1)}, f32[54,384]{1,0:T(8,128)S(1)}, u32[]{:S(2)}, u32[]{:S(2)}) collective-permute-start(f32[54,384]{1,0:T(8,128)S(1)} %constant_dynamic-slice_fusion.12), channel_id=1, source_target_pairs={{0,4},{1,5},{2,6},{3,7},{4,0},{5,1},{6,2},{7,3},{8,12},{9,13},{10,... | collective-permute-start | bytes 248840 | tf_op jit(solution)/shard_map/ppermute | solution.py:37
  26.4 5.1 %collective-permute-start.4 = (f32[27,384]{1,0:T(8,128)S(1)}, f32[27,384]{1,0:T(8,128)S(1)}, u32[]{:S(2)}, u32[]{:S(2)}) collective-permute-start(f32[27,384]{1,0:T(8,128)S(1)} %constant_dynamic-slice_fusion.11), channel_id=1, source_target_pairs={{0,8},{1,9},{2,10},{3,11},{4,12},{5,13},{6,14},{7,15},{8,0},{9,1},... | collective-permute-start | bytes 124424 | tf_op jit(solution)/shard_map/ppermute | solution.py:37
  31.5 5.1 %collective-permute-start.5 = (f32[27,384]{1,0:T(8,128)S(1)}, f32[27,384]{1,0:T(8,128)S(1)}, u32[]{:S(2)}, u32[]{:S(2)}) collective-permute-start(f32[27,384]{1,0:T(8,128)S(1)} %dynamic-slice_add_fusion.13), channel_id=1, source_target_pairs={{0,8},{1,9},{2,10},{3,11},{4,12},{5,13},{6,14},{7,15},{8,0},{9,1},... | collective-permute-start | bytes 124424 | tf_op jit(solution)/shard_map/ppermute | solution.py:43
  36.9 5.7 %collective-permute-start.6 = (f32[54,384]{0,1:T(8,128)S(1)}, f32[54,384]{0,1:T(8,128)S(1)}, u32[]{:S(2)}, u32[]{:S(2)}) collective-permute-start(f32[54,384]{0,1:T(8,128)S(1)} %broadcast_select_fusion.1), channel_id=1, source_target_pairs={{0,4},{1,5},{2,6},{3,7},{4,0},{5,1},{6,2},{7,3},{8,12},{9,13},{10,... | collective-permute-start | bytes 248840 | tf_op jit(solution)/shard_map/ppermute | solution.py:43
  42.8 5.7 %collective-permute-start.7 = (f32[108,384]{0,1:T(8,128)S(1)}, f32[108,384]{0,1:T(8,128)S(1)}, u32[]{:S(2)}, u32[]{:S(2)}) collective-permute-start(f32[108,384]{0,1:T(8,128)S(1)} %maximum_select_fusion.10), channel_id=1, source_target_pairs={{0,2},{1,3},{2,0},{3,1},{4,6},{5,7},{6,4},{7,5},{8,10},{9,11},{10,... | collective-permute-start | bytes 497672 | tf_op jit(solution)/shard_map/ppermute | solution.py:43
  48.8 1.8 collective-permute-start.8
  119.9 1.9 collective-permute-start.9
  121.9 12.6 %collective-permute-start.10 = (f32[96,640]{1,0:T(8,128)S(1)}, f32[96,640]{1,0:T(8,128)S(1)}, u32[]{:S(2)}, u32[]{:S(2)}) collective-permute-start(f32[96,640]{1,0:T(8,128)S(1)} %constant_dynamic-slice_fusion.9), channel_id=1, source_target_pairs={{0,2},{1,3},{2,0},{3,1},{4,6},{5,7},{6,4},{7,5},{8,10},{9,11},{10,... | collective-permute-start | bytes 737288 | tf_op jit(solution)/shard_map/ppermute | solution.py:37
  134.5 5.1 %collective-permute-start.11 = (f32[48,640]{1,0:T(8,128)S(1)}, f32[48,640]{1,0:T(8,128)S(1)}, u32[]{:S(2)}, u32[]{:S(2)}) collective-permute-start(f32[48,640]{1,0:T(8,128)S(1)} %constant_dynamic-slice_fusion.8), channel_id=1, source_target_pairs={{0,4},{1,5},{2,6},{3,7},{4,0},{5,1},{6,2},{7,3},{8,12},{9,13},{10,... | collective-permute-start | bytes 368648 | tf_op jit(solution)/shard_map/ppermute | solution.py:37
  139.7 5.5 %collective-permute-start.12 = (f32[24,640]{1,0:T(8,128)S(1)}, f32[24,640]{1,0:T(8,128)S(1)}, u32[]{:S(2)}, u32[]{:S(2)}) collective-permute-start(f32[24,640]{1,0:T(8,128)S(1)} %constant_dynamic-slice_fusion.7), channel_id=1, source_target_pairs={{0,8},{1,9},{2,10},{3,11},{4,12},{5,13},{6,14},{7,15},{8,0},{9,1},... | collective-permute-start | bytes 184328 | tf_op jit(solution)/shard_map/ppermute | solution.py:37
  145.2 5.2 %collective-permute-start.13 = (f32[24,640]{1,0:T(8,128)S(1)}, f32[24,640]{1,0:T(8,128)S(1)}, u32[]{:S(2)}, u32[]{:S(2)}) collective-permute-start(f32[24,640]{1,0:T(8,128)S(1)} %dynamic-slice_add_fusion.11), channel_id=1, source_target_pairs={{0,8},{1,9},{2,10},{3,11},{4,12},{5,13},{6,14},{7,15},{8,0},{9,1},... | collective-permute-start | bytes 184328 | tf_op jit(solution)/shard_map/ppermute | solution.py:43
  150.4 4.9 %collective-permute-start.14 = (f32[48,640]{1,0:T(8,128)S(1)}, f32[48,640]{1,0:T(8,128)S(1)}, u32[]{:S(2)}, u32[]{:S(2)}) collective-permute-start(f32[48,640]{1,0:T(8,128)S(1)} %maximum_select_fusion.12), channel_id=1, source_target_pairs={{0,4},{1,5},{2,6},{3,7},{4,0},{5,1},{6,2},{7,3},{8,12},{9,13},{10,... | collective-permute-start | bytes 368648 | tf_op jit(solution)/shard_map/ppermute | solution.py:43
  155.4 6.3 %collective-permute-start.15 = (f32[96,640]{1,0:T(8,128)S(1)}, f32[96,640]{1,0:T(8,128)S(1)}, u32[]{:S(2)}, u32[]{:S(2)}) collective-permute-start(f32[96,640]{1,0:T(8,128)S(1)} %maximum_select_fusion.8), channel_id=1, source_target_pairs={{0,2},{1,3},{2,0},{3,1},{4,6},{5,7},{6,4},{7,5},{8,10},{9,11},{10,... | collective-permute-start | bytes 737288 | tf_op jit(solution)/shard_map/ppermute | solution.py:43
  161.7 1.9 collective-permute-start.16
  168.4 7.0 %collective-permute-start.17 = (f32[128,384]{0,1:T(8,128)S(1)}, f32[128,384]{0,1:T(8,128)S(1)}, u32[]{:S(2)}, u32[]{:S(2)}) collective-permute-start(f32[128,384]{0,1:T(8,128)S(1)} %fusion.6), channel_id=1, source_target_pairs={{0,16},{16,0},{1,17},{17,1},{2,18},{18,2},{3,19},{19,3},{4,20},{20... | collective-permute-start | bytes 589832 | tf_op jit(solution)/shard_map/ppermute | solution.py:56
  178.5 6.5 %collective-permute-start.19 = (f32[108,384]{1,0:T(8,128)S(1)}, f32[108,384]{1,0:T(8,128)S(1)}, u32[]{:S(2)}, u32[]{:S(2)}) collective-permute-start(f32[108,384]{1,0:T(8,128)S(1)} %constant_dynamic-slice_fusion.6), channel_id=1, source_target_pairs={{0,2},{1,3},{2,0},{3,1},{4,6},{5,7},{6,4},{7,5},{8,10},{9,11},{10,... | collective-permute-start | bytes 497672 | tf_op jit(solution)/shard_map/ppermute | solution.py:37
  185.1 4.6 %collective-permute-start.20 = (f32[54,384]{1,0:T(8,128)S(1)}, f32[54,384]{1,0:T(8,128)S(1)}, u32[]{:S(2)}, u32[]{:S(2)}) collective-permute-start(f32[54,384]{1,0:T(8,128)S(1)} %constant_dynamic-slice_fusion.5), channel_id=1, source_target_pairs={{0,4},{1,5},{2,6},{3,7},{4,0},{5,1},{6,2},{7,3},{8,12},{9,13},{10,... | collective-permute-start | bytes 248840 | tf_op jit(solution)/shard_map/ppermute | solution.py:37
  189.7 5.3 %collective-permute-start.21 = (f32[27,384]{1,0:T(8,128)S(1)}, f32[27,384]{1,0:T(8,128)S(1)}, u32[]{:S(2)}, u32[]{:S(2)}) collective-permute-start(f32[27,384]{1,0:T(8,128)S(1)} %constant_dynamic-slice_fusion.4), channel_id=1, source_target_pairs={{0,8},{1,9},{2,10},{3,11},{4,12},{5,13},{6,14},{7,15},{8,0},{9,1},... | collective-permute-start | bytes 124424 | tf_op jit(solution)/shard_map/ppermute | solution.py:37
  194.9 5.1 %collective-permute-start.22 = (f32[27,384]{1,0:T(8,128)S(1)}, f32[27,384]{1,0:T(8,128)S(1)}, u32[]{:S(2)}, u32[]{:S(2)}) collective-permute-start(f32[27,384]{1,0:T(8,128)S(1)} %dynamic-slice_add_fusion.12), channel_id=1, source_target_pairs={{0,8},{1,9},{2,10},{3,11},{4,12},{5,13},{6,14},{7,15},{8,0},{9,1},... | collective-permute-start | bytes 124424 | tf_op jit(solution)/shard_map/ppermute | solution.py:43
  200.4 5.7 %collective-permute-start.23 = (f32[54,384]{0,1:T(8,128)S(1)}, f32[54,384]{0,1:T(8,128)S(1)}, u32[]{:S(2)}, u32[]{:S(2)}) collective-permute-start(f32[54,384]{0,1:T(8,128)S(1)} %broadcast_select_fusion), channel_id=1, source_target_pairs={{0,4},{1,5},{2,6},{3,7},{4,0},{5,1},{6,2},{7,3},{8,12},{9,13},{10,... | collective-permute-start | bytes 248840 | tf_op jit(solution)/shard_map/ppermute | solution.py:43
  206.3 5.7 %collective-permute-start.24 = (f32[108,384]{0,1:T(8,128)S(1)}, f32[108,384]{0,1:T(8,128)S(1)}, u32[]{:S(2)}, u32[]{:S(2)}) collective-permute-start(f32[108,384]{0,1:T(8,128)S(1)} %maximum_select_fusion.11), channel_id=1, source_target_pairs={{0,2},{1,3},{2,0},{3,1},{4,6},{5,7},{6,4},{7,5},{8,10},{9,11},{10,... | collective-permute-start | bytes 497672 | tf_op jit(solution)/shard_map/ppermute | solution.py:43
  212.3 1.8 collective-permute-start.25
  278.6 1.9 collective-permute-start.26
  280.6 11.5 %collective-permute-start.27 = (f32[96,640]{1,0:T(8,128)S(1)}, f32[96,640]{1,0:T(8,128)S(1)}, u32[]{:S(2)}, u32[]{:S(2)}) collective-permute-start(f32[96,640]{1,0:T(8,128)S(1)} %constant_dynamic-slice_fusion.2), channel_id=1, source_target_pairs={{0,2},{1,3},{2,0},{3,1},{4,6},{5,7},{6,4},{7,5},{8,10},{9,11},{10,... | collective-permute-start | bytes 737288 | tf_op jit(solution)/shard_map/ppermute | solution.py:37
  292.2 5.4 %collective-permute-start.28 = (f32[48,640]{1,0:T(8,128)S(1)}, f32[48,640]{1,0:T(8,128)S(1)}, u32[]{:S(2)}, u32[]{:S(2)}) collective-permute-start(f32[48,640]{1,0:T(8,128)S(1)} %constant_dynamic-slice_fusion.1), channel_id=1, source_target_pairs={{0,4},{1,5},{2,6},{3,7},{4,0},{5,1},{6,2},{7,3},{8,12},{9,13},{10,... | collective-permute-start | bytes 368648 | tf_op jit(solution)/shard_map/ppermute | solution.py:37
  297.6 5.7 %collective-permute-start.29 = (f32[24,640]{1,0:T(8,128)S(1)}, f32[24,640]{1,0:T(8,128)S(1)}, u32[]{:S(2)}, u32[]{:S(2)}) collective-permute-start(f32[24,640]{1,0:T(8,128)S(1)} %constant_dynamic-slice_fusion), channel_id=1, source_target_pairs={{0,8},{1,9},{2,10},{3,11},{4,12},{5,13},{6,14},{7,15},{8,0},{9,1},... | collective-permute-start | bytes 184328 | tf_op jit(solution)/shard_map/ppermute | solution.py:37
  303.3 5.2 %collective-permute-start.30 = (f32[24,640]{1,0:T(8,128)S(1)}, f32[24,640]{1,0:T(8,128)S(1)}, u32[]{:S(2)}, u32[]{:S(2)}) collective-permute-start(f32[24,640]{1,0:T(8,128)S(1)} %dynamic-slice_add_fusion.10), channel_id=1, source_target_pairs={{0,8},{1,9},{2,10},{3,11},{4,12},{5,13},{6,14},{7,15},{8,0},{9,1},... | collective-permute-start | bytes 184328 | tf_op jit(solution)/shard_map/ppermute | solution.py:43
  308.5 4.9 %collective-permute-start.31 = (f32[48,640]{1,0:T(8,128)S(1)}, f32[48,640]{1,0:T(8,128)S(1)}, u32[]{:S(2)}, u32[]{:S(2)}) collective-permute-start(f32[48,640]{1,0:T(8,128)S(1)} %maximum_select_fusion.13), channel_id=1, source_target_pairs={{0,4},{1,5},{2,6},{3,7},{4,0},{5,1},{6,2},{7,3},{8,12},{9,13},{10,... | collective-permute-start | bytes 368648 | tf_op jit(solution)/shard_map/ppermute | solution.py:43
  313.4 6.3 %collective-permute-start.32 = (f32[96,640]{1,0:T(8,128)S(1)}, f32[96,640]{1,0:T(8,128)S(1)}, u32[]{:S(2)}, u32[]{:S(2)}) collective-permute-start(f32[96,640]{1,0:T(8,128)S(1)} %maximum_select_fusion.9), channel_id=1, source_target_pairs={{0,2},{1,3},{2,0},{3,1},{4,6},{5,7},{6,4},{7,5},{8,10},{9,11},{10,... | collective-permute-start | bytes 737288 | tf_op jit(solution)/shard_map/ppermute | solution.py:43
  319.7 1.9 collective-permute-start.33
  (13 other events, 20.9 us)

commit v4 on v3

--- a/solution.py
+++ b/solution.py
@@ -33,8 +33,8 @@
         h = cur.shape[0] // 2
         bit = (me // k) % 2
         keep = lax.dynamic_slice_in_dim(cur, bit * h, h, axis=0)
-        send = lax.dynamic_slice_in_dim(cur, (1 - bit) * h, h, axis=0)
-        cur = keep + lax.ppermute(send, axis, perm)
+        away = lax.dynamic_slice_in_dim(cur, (1 - bit) * h, h, axis=0)
+        cur = keep + lax.ppermute(away, axis, perm)
         k *= 2
     k = n // 2
     while k >= 1:
@@ -58,24 +58,15 @@
     return x
 
 
-def solve_gram(factor, right):
-    half = lax.linalg.triangular_solve(factor, right, left_side=True, lower=True)
-    return lax.linalg.triangular_solve(factor, half, left_side=True, lower=True, transpose_a=True)
-
-
-def block_solve(cov, right, size):
-    nb = cov.shape[0] // size
-    if nb * size != cov.shape[0]:
-        return solve_gram(jnp.linalg.cholesky(cov), right)
-    cov = 0.5 * (cov + cov.T)
-    eye = jnp.eye(size, dtype=cov.dtype)
-    blk = [[cov[i * size:(i + 1) * size, j * size:(j + 1) * size] for j in range(nb)] for i in range(nb)]
+def block_solve(blk, right, size):
+    nb = len(blk)
+    eye = jnp.eye(size, dtype=right.dtype)
     rhs = [right[i * size:(i + 1) * size] for i in range(nb)]
     low = [[None] * nb for _ in range(nb)]
     inv = [None] * nb
     fwd = [None] * nb
     for k in range(nb):
-        diag = jnp.linalg.cholesky(blk[k][k], symmetrize_input=False)
+        diag = lax.linalg.cholesky(blk[k][k], symmetrize_input=False)
         inv[k] = lax.linalg.triangular_solve(diag, eye, left_side=True, lower=True)
         fwd[k] = full_dot(inv[k], rhs[k])
         for i in range(k + 1, nb):
@@ -116,15 +107,26 @@
     gram_loc = tdot(obs_c, obs_c)
     cross_loc = tdot(obs_c, row_c)
 
-    width = -(-(obs + n_rows) // obs) * obs
+    size = 128 if obs % 128 == 0 else obs
+    nb = obs // size
+    pairs = [(i, j) for i in range(nb) for j in range(i + 1)]
+    width = -(-(obs + n_rows) // size) * size
     slots = jnp.zeros((n_member, width), jnp.float32)
     slots = lax.dynamic_update_slice(slots, jnp.concatenate([obs_loc, row_loc])[None, :], (me, 0))
-    packed = jnp.concatenate([gram_loc, slots.reshape(-1, obs)], axis=0)
+    pieces = [gram_loc[i * size:(i + 1) * size, j * size:(j + 1) * size] for i, j in pairs]
+    n_gram = len(pairs) * size
+    n_slot = n_member * width // size
+    cross_pad = -(-n_rows // size) * size
+    cross_wide = jnp.pad(cross_loc, ((0, 0), (0, cross_pad - n_rows)))
+    cross_parts = [cross_wide[:, c * size:(c + 1) * size] for c in range(cross_pad // size)]
+    packed = jnp.concatenate(pieces + [slots.reshape(-1, size)] + cross_parts, axis=0)
     packed = tree_sum(packed, "member")
-    gram_sum = packed[:obs]
-    slots = packed[obs:].reshape(n_member, width)[:, : obs + n_rows]
-    cross_loc, gram_sum, slots = lax.optimization_barrier((cross_loc, gram_sum, slots))
-    cross_sum = tree_sum(cross_loc, "member")
+    gram_blocks = packed[:n_gram]
+    slots = packed[n_gram:n_gram + n_slot].reshape(n_member, width)[:, : obs + n_rows]
+    tail = packed[n_gram + n_slot:]
+    cross_sum = jnp.concatenate(
+        [tail[c * obs:(c + 1) * obs] for c in range(cross_pad // size)], axis=1
+    )[:, :n_rows]
 
     means = jnp.mean(slots, axis=0)
     dev = slots - means[None, :]
@@ -132,10 +134,17 @@
     dev_obs = dev[:, :obs]
     dev_row = dev[:, obs:]
 
-    innov_cov = (gram_sum + m_loc * tdot(dev_obs, dev_obs)) / (count - 1.0) + jnp.diag(noise)
+    corr = m_loc * tdot(dev_obs, dev_obs)
+    blk = [[None] * nb for _ in range(nb)]
+    for p, (i, j) in enumerate(pairs):
+        part = gram_blocks[p * size:(p + 1) * size] + corr[i * size:(i + 1) * size, j * size:(j + 1) * size]
+        part = part / (count - 1.0)
+        if i == j:
+            part = 0.5 * (part + part.T) + jnp.diag(noise[i * size:(i + 1) * size])
+        blk[i][j] = part
     obs_anom = observed - obs_mean[None, :]
     rhs = (target - obs_mean)[:, None] - 0.5 * obs_anom.T
-    gain = block_solve(innov_cov, rhs, 128)
+    gain = block_solve(blk, rhs, size)
 
     cross = (cross_sum + m_loc * tdot(dev_obs, dev_row)) / (count - 1.0)
     return gain, cross

time: 328 us -> 320 us (0.976)
  starting transfers between devices: 54.7 us -> 28 us
  matrix products: 25.7 us -> 32.5 us
  other arithmetic: 142 us -> 147 us
  local copies, waits for them, and re-layouts: 15.4 us -> 20.2 us
    ppermute x16 -> x8, starting transfers between devices: 24.6 us -> 10.1 us  [tree_sum(): other = lax.ppermute(cur, axis, perm)]
    ppermute x16 -> x8, starting transfers between devices: 25.5 us -> 13.3 us  [tree_sum(): cur = keep + lax.ppermute(away, axis, perm)]
    ppermute x16 -> x8, waiting for transfers between devices: 39.8 us -> 31.8 us  [tree_sum(): other = lax.ppermute(cur, axis, perm)]
    ppermute x16 -> x8, waiting for transfers between devices: 34.4 us -> 42.2 us  [tree_sum(): cur = keep + lax.ppermute(away, axis, perm)]
    dot_general x29, matrix products: 13.6 us -> 17.2 us  [full_dot(): jnp.dot(left, right, precision=lax.Precision.HIGHEST, preferred_element_t...]
    unnamed x19 -> x59, local copies, waits for them, and re-layouts: 5.03 us -> 6.91 us
    another operation x18 -> x19, other arithmetic: 75 us -> 75.7 us  [block_solve(): diag = lax.linalg.cholesky(blk[k][k], symmetrize_input=False)]
  transfers between devices with their start and end apart: 34 -> 18, of which waited for: 32 -> 17; matrix products, arithmetic and copies ran while one was open for 10% -> 1% of each run, Pallas kernels for 0% -> 0%
where the time goes in v4:
time: 320 us; the launch traced here: 315 us
  other arithmetic  147 us (46%)
  waiting for transfers between devices  84.7 us (26%)
  matrix products  32.5 us (10%)
  starting transfers between devices  28 us (9%)
  local copies, waits for them, and re-layouts  20.2 us (6%)
    another operation x19, other arithmetic, block_solve(): diag = lax.linalg.cholesky(blk[k][k], symmetrize_input=False)  75.7 us
    another operation x12, other arithmetic, block_solve(): inv[k] = lax.linalg.triangular_solve(diag, eye, left_side=True, lower=True)  65.1 us
    ppermute x8, waiting for transfers between devices, tree_sum(): cur = keep + lax.ppermute(away, axis, perm)  42.2 us
    ppermute x8, waiting for transfers between devices, tree_sum(): other = lax.ppermute(cur, axis, perm)  31.8 us
    dot_general x29, matrix products, full_dot(): jnp.dot(left, right, precision=lax.Precision.HIGHEST, preferred_element_t...  17.2 us
    ppermute x8, starting transfers between devices, tree_sum(): cur = keep + lax.ppermute(away, axis, perm)  13.3 us
    dot_general x20, matrix products, tdot(): lax.dot_general(left, right, (((0,), (0,)), ((), ())), precision=lax.Prec...  12.7 us
    ppermute x2, waiting for transfers between devices, tree_sum_exact(): x = x + lax.ppermute(x, axis, perm)  10.6 us
  transfers between devices with their start and end apart: 18, of which 17 were waited for; matrix products, arithmetic and copies ran while one was open for 1% of the time, Pallas kernels for 0%

profile of v4, /device:TPU:0, one launch (start us, length us, event | category | flops | bytes accessed | tf_op | source)
XLA Modules:
  0.0 314.6 jit_solution(11432965370553069453)
XLA Ops:
  3.4 3.0 collective-permute-start
  6.5 4.8 %collective-permute-done = f32[128,384]{1,0:T(8,128)S(1)} collective-permute-done((f32[128,384]{1,0:T(8,128)S(1)}, f32[128,384]{1,0:T(8,128)S(1)}, u32[]{:S(2)}, u32[]{:S(2)}) %collective-permute-start) | collective-permute-done | bytes 196640 | tf_op jit(solution)/shard_map/ppermute | solution.py:56
  19.1 9.4 %collective-permute-done.2 = f32[704,128]{0,1:T(8,128)S(1)} collective-permute-done((f32[704,128]{0,1:T(8,128)S(1)}, f32[704,128]{0,1:T(8,128)S(1)}, u32[]{:S(2)}, u32[]{:S(2)}) %collective-permute-start.2) | collective-permute-done | bytes 360480 | tf_op jit(solution)/shard_map/ppermute | solution.py:37
  30.8 4.4 %collective-permute-done.3 = f32[352,128]{0,1:T(8,128)S(1)} collective-permute-done((f32[352,128]{0,1:T(8,128)S(1)}, f32[352,128]{0,1:T(8,128)S(1)}, u32[]{:S(2)}, u32[]{:S(2)}) %collective-permute-start.3) | collective-permute-done | bytes 180256 | tf_op jit(solution)/shard_map/ppermute | solution.py:37
  35.4 2.8 collective-permute-start.4
  38.2 4.9 %collective-permute-done.4 = f32[176,128]{0,1:T(8,128)S(1)} collective-permute-done((f32[176,128]{0,1:T(8,128)S(1)}, f32[176,128]{0,1:T(8,128)S(1)}, u32[]{:S(2)}, u32[]{:S(2)}) %collective-permute-start.4) | collective-permute-done | bytes 90144 | tf_op jit(solution)/shard_map/ppermute | solution.py:37
  44.3 5.0 %collective-permute-done.5 = f32[176,128]{0,1:T(8,128)S(1)} collective-permute-done((f32[176,128]{0,1:T(8,128)S(1)}, f32[176,128]{0,1:T(8,128)S(1)}, u32[]{:S(2)}, u32[]{:S(2)}) %collective-permute-start.5) | collective-permute-done | bytes 90144 | tf_op jit(solution)/shard_map/ppermute | solution.py:43
  49.5 2.4 collective-permute-start.6
  52.5 3.1 collective-permute-done.6
  57.4 6.2 %collective-permute-done.7 = f32[704,128]{0,1:T(8,128)S(1)} collective-permute-done((f32[704,128]{0,1:T(8,128)S(1)}, f32[704,128]{0,1:T(8,128)S(1)}, u32[]{:S(2)}, u32[]{:S(2)}) %collective-permute-start.7) | collective-permute-done | bytes 360480 | tf_op jit(solution)/shard_map/ppermute | solution.py:43
  71.3 11.7 %custom-call.16 = f32[128,128]{1,0:T(8,128)S(1)} custom-call(f32[128,128]{1,0:T(8,128)S(1)} %copy.75), custom_call_target="Cholesky" | custom-call | tf_op jit(solution)/shard_map/cholesky/custom-call.1 | solution.py:69
  84.3 9.8 %custom-call.17 = f32[1,128,128]{1,2,0:T(8,128)S(1)} custom-call(f32[1,128,128]{2,1,0:T(8,128)S(1)} %fusion.41), custom_call_target="InvertDiagBlocksLowerTriangular" | custom-call | tf_op jit(solution)/shard_map/triangular_solve/custom-call.0 | solution.py:70
  106.5 13.0 %custom-call.18 = f32[128,128]{1,0:T(8,128)S(1)} custom-call(f32[128,128]{1,0:T(8,128)} %copy.81), custom_call_target="Cholesky" | custom-call | tf_op jit(solution)/shard_map/cholesky/custom-call.1 | solution.py:69
  121.6 11.3 %custom-call.19 = f32[1,128,128]{1,2,0:T(8,128)} custom-call(f32[1,128,128]{2,1,0:T(8,128)} %fusion.42), custom_call_target="InvertDiagBlocksLowerTriangular" | custom-call | tf_op jit(solution)/shard_map/triangular_solve/custom-call.0 | solution.py:70
  136.4 11.7 %custom-call.20 = f32[128,128]{1,0:T(8,128)S(1)} custom-call(f32[128,128]{1,0:T(8,128)S(1)} %copy.88), custom_call_target="Cholesky" | custom-call | tf_op jit(solution)/shard_map/cholesky/custom-call.1 | solution.py:69
  149.5 9.8 %custom-call.21 = f32[1,128,128]{1,2,0:T(8,128)S(1)} custom-call(f32[1,128,128]{2,1,0:T(8,128)S(1)} %fusion.43), custom_call_target="InvertDiagBlocksLowerTriangular" | custom-call | tf_op jit(solution)/shard_map/triangular_solve/custom-call.0 | solution.py:70
  168.7 5.8 %collective-permute-done.9 = f32[128,384]{1,0:T(8,128)S(1)} collective-permute-done((f32[128,384]{1,0:T(8,128)S(1)}, f32[128,384]{1,0:T(8,128)S(1)}, u32[]{:S(2)}, u32[]{:S(2)}) %collective-permute-start.9) | collective-permute-done | bytes 196640 | tf_op jit(solution)/shard_map/ppermute | solution.py:56
  180.8 9.7 %collective-permute-done.11 = f32[704,128]{0,1:T(8,128)S(1)} collective-permute-done((f32[704,128]{0,1:T(8,128)S(1)}, f32[704,128]{0,1:T(8,128)S(1)}, u32[]{:S(2)}, u32[]{:S(2)}) %collective-permute-start.11) | collective-permute-done | bytes 360480 | tf_op jit(solution)/shard_map/ppermute | solution.py:37
  192.9 4.4 %collective-permute-done.12 = f32[352,128]{0,1:T(8,128)S(1)} collective-permute-done((f32[352,128]{0,1:T(8,128)S(1)}, f32[352,128]{0,1:T(8,128)S(1)}, u32[]{:S(2)}, u32[]{:S(2)}) %collective-permute-start.12) | collective-permute-done | bytes 180256 | tf_op jit(solution)/shard_map/ppermute | solution.py:37
  197.5 3.0 collective-permute-start.13
  200.4 5.1 %collective-permute-done.13 = f32[176,128]{0,1:T(8,128)S(1)} collective-permute-done((f32[176,128]{0,1:T(8,128)S(1)}, f32[176,128]{0,1:T(8,128)S(1)}, u32[]{:S(2)}, u32[]{:S(2)}) %collective-permute-start.13) | collective-permute-done | bytes 90144 | tf_op jit(solution)/shard_map/ppermute | solution.py:37
  206.6 5.3 %collective-permute-done.14 = f32[176,128]{0,1:T(8,128)S(1)} collective-permute-done((f32[176,128]{0,1:T(8,128)S(1)}, f32[176,128]{0,1:T(8,128)S(1)}, u32[]{:S(2)}, u32[]{:S(2)}) %collective-permute-start.14) | collective-permute-done | bytes 90144 | tf_op jit(solution)/shard_map/ppermute | solution.py:43
  212.0 2.3 collective-permute-start.15
  214.3 3.6 %collective-permute-done.15 = f32[352,128]{0,1:T(8,128)S(1)} collective-permute-done((f32[352,128]{0,1:T(8,128)S(1)}, f32[352,128]{0,1:T(8,128)S(1)}, u32[]{:S(2)}, u32[]{:S(2)}) %collective-permute-start.15) | collective-permute-done | bytes 180256 | tf_op jit(solution)/shard_map/ppermute | solution.py:43
  219.8 6.4 %collective-permute-done.16 = f32[704,128]{0,1:T(8,128)S(1)} collective-permute-done((f32[704,128]{0,1:T(8,128)S(1)}, f32[704,128]{0,1:T(8,128)S(1)}, u32[]{:S(2)}, u32[]{:S(2)}) %collective-permute-start.16) | collective-permute-done | bytes 360480 | tf_op jit(solution)/shard_map/ppermute | solution.py:43
  230.6 11.7 %custom-call.22 = f32[128,128]{1,0:T(8,128)S(1)} custom-call(f32[128,128]{1,0:T(8,128)S(1)} %fusion.87), custom_call_target="Cholesky" | custom-call | tf_op jit(solution)/shard_map/cholesky/custom-call.1 | solution.py:69
  243.7 9.8 %custom-call.23 = f32[1,128,128]{1,2,0:T(8,128)S(1)} custom-call(f32[1,128,128]{2,1,0:T(8,128)S(1)} %fusion.44), custom_call_target="InvertDiagBlocksLowerTriangular" | custom-call | tf_op jit(solution)/shard_map/triangular_solve/custom-call.0 | solution.py:70
  258.3 2.4 fusion.1
  261.4 11.7 %custom-call.24 = f32[128,128]{1,0:T(8,128)S(1)} custom-call(f32[128,128]{1,0:T(8,128)S(1)} %convolution_subtract_fusion.8), custom_call_target="Cholesky" | custom-call | tf_op jit(solution)/shard_map/cholesky/custom-call.1 | solution.py:69
  274.5 9.8 %custom-call.25 = f32[1,128,128]{1,2,0:T(8,128)S(1)} custom-call(f32[1,128,128]{2,1,0:T(8,128)S(1)} %fusion.45), custom_call_target="InvertDiagBlocksLowerTriangular" | custom-call | tf_op jit(solution)/shard_map/triangular_solve/custom-call.0 | solution.py:70
  286.3 11.7 %custom-call.26 = f32[128,128]{1,0:T(8,128)S(1)} custom-call(f32[128,128]{1,0:T(8,128)S(1)} %convolution_subtract_fusion.5), custom_call_target="Cholesky" | custom-call | tf_op jit(solution)/shard_map/cholesky/custom-call.1 | solution.py:69
  299.4 10.0 %custom-call.27 = f32[1,128,128]{1,2,0:T(8,128)S(1)} custom-call(f32[1,128,128]{2,1,0:T(8,128)S(1)} %fusion.46), custom_call_target="InvertDiagBlocksLowerTriangular" | custom-call | tf_op jit(solution)/shard_map/triangular_solve/custom-call.0 | solution.py:70
  (247 shorter events, 86.7 us)
Async XLA Ops:
  0.0 3.2 %copy-start.13 = (s32[2,3]{1,0:T(2,128)S(1)}, s32[2,3]{1,0:T(2,128)}, u32[]{:S(2)}) copy-start(s32[2,3]{1,0:T(2,128)} %param.14) | copy-start | bytes 76
  1.9 4.5 %copy-start = (f32[128,640]{1,0:T(8,128)S(1)}, f32[128,640]{1,0:T(8,128)}, u32[]{:S(2)}) copy-start(f32[128,640]{1,0:T(8,128)} %param.10) | copy-start | bytes 983044
  3.4 7.9 %collective-permute-start = (f32[128,384]{1,0:T(8,128)S(1)}, f32[128,384]{1,0:T(8,128)S(1)}, u32[]{:S(2)}, u32[]{:S(2)}) collective-permute-start(f32[128,384]{1,0:T(8,128)S(1)} %bitcast_select_fusion), channel_id=1, source_target_pairs={{0,16},{16,0},{1,17},{17,1},{2,18},{18,2},{3,19},{19,3},{4,20},{20... | collective-permute-start | bytes 589832 | tf_op jit(solution)/shard_map/ppermute | solution.py:56
  13.6 2.4 collective-permute-start.1
  17.3 11.3 %collective-permute-start.2 = (f32[704,128]{0,1:T(8,128)S(1)}, f32[704,128]{0,1:T(8,128)S(1)}, u32[]{:S(2)}, u32[]{:S(2)}) collective-permute-start(f32[704,128]{0,1:T(8,128)S(1)} %constant_dynamic-slice_fusion.6), channel_id=1, source_target_pairs={{0,2},{1,3},{2,0},{3,1},{4,6},{5,7},{6,4},{7,5},{8,10},{9,11},{10,... | collective-permute-start | bytes 1081352 | tf_op jit(solution)/shard_map/ppermute | solution.py:37
  19.1 32.8 %copy-start.7 = (f32[2,384]{1,0:T(2,128)S(1)}, f32[2,384]{1,0:T(2,128)}, u32[]{:S(2)}) copy-start(f32[2,384]{1,0:T(2,128)} %param.11) | copy-start | bytes 9220
  28.8 28.6 %copy-start.6 = (s32[2,384]{1,0:T(2,128)S(1)}, s32[2,384]{1,0:T(2,128)}, u32[]{:S(2)}) copy-start(s32[2,384]{1,0:T(2,128)} %param.13) | copy-start | bytes 9220
  28.9 6.2 %collective-permute-start.3 = (f32[352,128]{0,1:T(8,128)S(1)}, f32[352,128]{0,1:T(8,128)S(1)}, u32[]{:S(2)}, u32[]{:S(2)}) collective-permute-start(f32[352,128]{0,1:T(8,128)S(1)} %constant_dynamic-slice_fusion.5), channel_id=1, source_target_pairs={{0,4},{1,5},{2,6},{3,7},{4,0},{5,1},{6,2},{7,3},{8,12},{9,13},{10,... | collective-permute-start | bytes 540680 | tf_op jit(solution)/shard_map/ppermute | solution.py:37
  35.4 7.7 %collective-permute-start.4 = (f32[176,128]{0,1:T(8,128)S(1)}, f32[176,128]{0,1:T(8,128)S(1)}, u32[]{:S(2)}, u32[]{:S(2)}) collective-permute-start(f32[176,128]{0,1:T(8,128)S(1)} %constant_dynamic-slice_fusion.4), channel_id=1, source_target_pairs={{0,8},{1,9},{2,10},{3,11},{4,12},{5,13},{6,14},{7,15},{8,0},{9,1},... | collective-permute-start | bytes 270344 | tf_op jit(solution)/shard_map/ppermute | solution.py:37
  43.2 6.2 %collective-permute-start.5 = (f32[176,128]{0,1:T(8,128)S(1)}, f32[176,128]{0,1:T(8,128)S(1)}, u32[]{:S(2)}, u32[]{:S(2)}) collective-permute-start(f32[176,128]{0,1:T(8,128)S(1)} %dynamic-slice_add_fusion.7), channel_id=1, source_target_pairs={{0,8},{1,9},{2,10},{3,11},{4,12},{5,13},{6,14},{7,15},{8,0},{9,1},... | collective-permute-start | bytes 270344 | tf_op jit(solution)/shard_map/ppermute | solution.py:43
  49.5 6.1 %collective-permute-start.6 = (f32[352,128]{0,1:T(8,128)S(1)}, f32[352,128]{0,1:T(8,128)S(1)}, u32[]{:S(2)}, u32[]{:S(2)}) collective-permute-start(f32[352,128]{0,1:T(8,128)S(1)} %maximum_select_fusion.6), channel_id=1, source_target_pairs={{0,4},{1,5},{2,6},{3,7},{4,0},{5,1},{6,2},{7,3},{8,12},{9,13},{10,... | collective-permute-start | bytes 540680 | tf_op jit(solution)/shard_map/ppermute | solution.py:43
  55.8 7.8 %collective-permute-start.7 = (f32[704,128]{0,1:T(8,128)S(1)}, f32[704,128]{0,1:T(8,128)S(1)}, u32[]{:S(2)}, u32[]{:S(2)}) collective-permute-start(f32[704,128]{0,1:T(8,128)S(1)} %maximum_select_fusion.4), channel_id=1, source_target_pairs={{0,2},{1,3},{2,0},{3,1},{4,6},{5,7},{6,4},{7,5},{8,10},{9,11},{10,... | collective-permute-start | bytes 1081352 | tf_op jit(solution)/shard_map/ppermute | solution.py:43
  63.9 3.5 %copy-start.8 = (f32[2,384]{1,0:T(2,128)S(1)}, f32[2,384]{1,0:T(2,128)}, u32[]{:S(2)}) copy-start(f32[2,384]{1,0:T(2,128)} %param.12) | copy-start | bytes 9220
  63.9 4.1 %collective-permute-start.8 = (f32[1408,128]{0,1:T(8,128)S(1)}, f32[1408,128]{0,1:T(8,128)}, u32[]{:S(2)}, u32[]{:S(2)}) collective-permute-start(f32[1408,128]{0,1:T(8,128)S(1)} %maximum_select_fusion.2), channel_id=1, source_target_pairs={{0,1},{1,0},{2,3},{3,2},{4,5},{5,4},{6,7},{7,6},{8,9},{9,8},{10,11... | collective-permute-start | bytes 2162696 | tf_op jit(solution)/shard_map/ppermute | solution.py:43
  71.0 25.5 %copy-start.2 = (f32[384,384]{0,1:T(8,128)}, f32[384,384]{0,1:T(8,128)S(1)}, u32[]{:S(2)}) copy-start(f32[384,384]{0,1:T(8,128)S(1)} %convolution_multiply_fusion.3) | copy-start | bytes 1769476
  102.4 57.2 %copy-start.3 = (f32[128,128]{0,1:T(8,128)S(1)}, f32[128,128]{0,1:T(8,128)}, u32[]{:S(2)}) copy-start(f32[128,128]{0,1:T(8,128)} %convolution_subtract_fusion.16) | copy-start | bytes 196612
  161.8 2.6 copy-start.4
  164.4 1.8 copy-start.12
  164.4 1.8 copy-start.14
  167.1 7.4 %collective-permute-start.9 = (f32[128,384]{1,0:T(8,128)S(1)}, f32[128,384]{1,0:T(8,128)S(1)}, u32[]{:S(2)}, u32[]{:S(2)}) collective-permute-start(f32[128,384]{1,0:T(8,128)S(1)} %fusion.4), channel_id=1, source_target_pairs={{0,16},{16,0},{1,17},{17,1},{2,18},{18,2},{3,19},{19,3},{4,20},{20... | collective-permute-start | bytes 589832 | tf_op jit(solution)/shard_map/ppermute | solution.py:56
  176.7 2.3 collective-permute-start.10
  179.2 11.2 %collective-permute-start.11 = (f32[704,128]{0,1:T(8,128)S(1)}, f32[704,128]{0,1:T(8,128)S(1)}, u32[]{:S(2)}, u32[]{:S(2)}) collective-permute-start(f32[704,128]{0,1:T(8,128)S(1)} %constant_dynamic-slice_fusion.2), channel_id=1, source_target_pairs={{0,2},{1,3},{2,0},{3,1},{4,6},{5,7},{6,4},{7,5},{8,10},{9,11},{10,... | collective-permute-start | bytes 1081352 | tf_op jit(solution)/shard_map/ppermute | solution.py:37
  190.8 6.4 %collective-permute-start.12 = (f32[352,128]{0,1:T(8,128)S(1)}, f32[352,128]{0,1:T(8,128)S(1)}, u32[]{:S(2)}, u32[]{:S(2)}) collective-permute-start(f32[352,128]{0,1:T(8,128)S(1)} %constant_dynamic-slice_fusion.1), channel_id=1, source_target_pairs={{0,4},{1,5},{2,6},{3,7},{4,0},{5,1},{6,2},{7,3},{8,12},{9,13},{10,... | collective-permute-start | bytes 540680 | tf_op jit(solution)/shard_map/ppermute | solution.py:37
  197.5 8.0 %collective-permute-start.13 = (f32[176,128]{0,1:T(8,128)S(1)}, f32[176,128]{0,1:T(8,128)S(1)}, u32[]{:S(2)}, u32[]{:S(2)}) collective-permute-start(f32[176,128]{0,1:T(8,128)S(1)} %constant_dynamic-slice_fusion), channel_id=1, source_target_pairs={{0,8},{1,9},{2,10},{3,11},{4,12},{5,13},{6,14},{7,15},{8,0},{9,1},... | collective-permute-start | bytes 270344 | tf_op jit(solution)/shard_map/ppermute | solution.py:37
  205.6 6.3 %collective-permute-start.14 = (f32[176,128]{0,1:T(8,128)S(1)}, f32[176,128]{0,1:T(8,128)S(1)}, u32[]{:S(2)}, u32[]{:S(2)}) collective-permute-start(f32[176,128]{0,1:T(8,128)S(1)} %dynamic-slice_add_fusion.6), channel_id=1, source_target_pairs={{0,8},{1,9},{2,10},{3,11},{4,12},{5,13},{6,14},{7,15},{8,0},{9,1},... | collective-permute-start | bytes 270344 | tf_op jit(solution)/shard_map/ppermute | solution.py:43
  212.0 5.9 %collective-permute-start.15 = (f32[352,128]{0,1:T(8,128)S(1)}, f32[352,128]{0,1:T(8,128)S(1)}, u32[]{:S(2)}, u32[]{:S(2)}) collective-permute-start(f32[352,128]{0,1:T(8,128)S(1)} %maximum_select_fusion.7), channel_id=1, source_target_pairs={{0,4},{1,5},{2,6},{3,7},{4,0},{5,1},{6,2},{7,3},{8,12},{9,13},{10,... | collective-permute-start | bytes 540680 | tf_op jit(solution)/shard_map/ppermute | solution.py:43
  218.2 7.9 %collective-permute-start.16 = (f32[704,128]{0,1:T(8,128)S(1)}, f32[704,128]{0,1:T(8,128)S(1)}, u32[]{:S(2)}, u32[]{:S(2)}) collective-permute-start(f32[704,128]{0,1:T(8,128)S(1)} %maximum_select_fusion.5), channel_id=1, source_target_pairs={{0,2},{1,3},{2,0},{3,1},{4,6},{5,7},{6,4},{7,5},{8,10},{9,11},{10,... | collective-permute-start | bytes 1081352 | tf_op jit(solution)/shard_map/ppermute | solution.py:43
  226.4 2.3 collective-permute-start.17
  229.5 24.8 %copy-start.5 = (f32[384]{0:T(512)S(1)}, f32[384]{0:T(512)}, u32[]{:S(2)}) copy-start(f32[384]{0:T(512)} %get-tuple-element.6) | copy-start | bytes 4612
  230.4 25.2 %copy-start.1 = (f32[384,384]{0,1:T(8,128)}, f32[384,384]{0,1:T(8,128)S(1)}, u32[]{:S(2)}) copy-start(f32[384,384]{0,1:T(8,128)S(1)} %convolution_multiply_fusion.2) | copy-start | bytes 1769476
  258.3 2.9 copy-start.10
  258.3 26.3 %copy-start.9 = (f32[128]{0:T(128)S(1)}, f32[128]{0:T(128)}, u32[]{:S(2)}) copy-start(f32[128]{0:T(128)} %get-tuple-element.31) | copy-start | bytes 1540
  (1 other events, 1.7 us)

commit v5 on v4

--- a/solution.py
+++ b/solution.py
@@ -114,19 +114,12 @@
     slots = jnp.zeros((n_member, width), jnp.float32)
     slots = lax.dynamic_update_slice(slots, jnp.concatenate([obs_loc, row_loc])[None, :], (me, 0))
     pieces = [gram_loc[i * size:(i + 1) * size, j * size:(j + 1) * size] for i, j in pairs]
-    n_gram = len(pairs) * size
-    n_slot = n_member * width // size
-    cross_pad = -(-n_rows // size) * size
-    cross_wide = jnp.pad(cross_loc, ((0, 0), (0, cross_pad - n_rows)))
-    cross_parts = [cross_wide[:, c * size:(c + 1) * size] for c in range(cross_pad // size)]
-    packed = jnp.concatenate(pieces + [slots.reshape(-1, size)] + cross_parts, axis=0)
+    packed = jnp.concatenate(pieces + [slots.reshape(-1, size)], axis=0)
     packed = tree_sum(packed, "member")
-    gram_blocks = packed[:n_gram]
-    slots = packed[n_gram:n_gram + n_slot].reshape(n_member, width)[:, : obs + n_rows]
-    tail = packed[n_gram + n_slot:]
-    cross_sum = jnp.concatenate(
-        [tail[c * obs:(c + 1) * obs] for c in range(cross_pad // size)], axis=1
-    )[:, :n_rows]
+    gram_blocks = packed[: len(pairs) * size]
+    slots = packed[len(pairs) * size:].reshape(n_member, width)[:, : obs + n_rows]
+    cross_loc, gram_blocks, slots = lax.optimization_barrier((cross_loc, gram_blocks, slots))
+    cross_sum = tree_sum(cross_loc, "member")
 
     means = jnp.mean(slots, axis=0)
     dev = slots - means[None, :]
@@ -159,7 +152,8 @@
         gain, cross = analyse(current, observed, obs_values[block], noise_var[block])
         if block + 1 < num_blocks:
             rows = obs_rows[block + 1]
-            cands = jnp.take(current, rows, axis=1) + full_dot(gain.T, jnp.take(cross, rows, axis=1))
+            picked = jnp.take(current, rows, axis=1)
+            cands = picked + full_dot(gain.T, jnp.take(cross, rows, axis=1))
         current = current + full_dot(gain.T, cross)
     return current
 

time: 320 us -> 320 us (level)
  starting transfers between devices: 28 us -> 52.9 us
  matrix products: 32.5 us -> 23 us
  waiting for transfers between devices: 84.7 us -> 78 us
  other arithmetic: 147 us -> 143 us
    ppermute x8 -> x16, starting transfers between devices: 10.1 us -> 23.4 us  [tree_sum(): other = lax.ppermute(cur, axis, perm)]
    ppermute x8 -> x16, starting transfers between devices: 13.3 us -> 24.9 us  [tree_sum(): cur = keep + lax.ppermute(away, axis, perm)]
    ppermute x8 -> x16, waiting for transfers between devices: 42.2 us -> 31.2 us  [tree_sum(): cur = keep + lax.ppermute(away, axis, perm)]
    dot_general x29, matrix products: 17.2 us -> 11.2 us  [full_dot(): jnp.dot(left, right, precision=lax.Precision.HIGHEST, preferred_element_t...]
    ppermute x8 -> x16, waiting for transfers between devices: 31.8 us -> 36.5 us  [tree_sum(): other = lax.ppermute(cur, axis, perm)]
    unnamed x59 -> x41, local copies, waits for them, and re-layouts: 6.91 us -> 6.02 us
  transfers between devices with their start and end apart: 18 -> 34, of which waited for: 17 -> 29; matrix products, arithmetic and copies ran while one was open for 1% -> 35% of each run, Pallas kernels for 0% -> 0%
where the time goes in v5:
time: 320 us; the launch traced here: 316 us
  other arithmetic  143 us (45%)
  waiting for transfers between devices  78 us (24%)
  starting transfers between devices  52.9 us (17%)
  matrix products  23 us (7%)
  local copies, waits for them, and re-layouts  17 us (5%)
    another operation x19, other arithmetic, block_solve(): diag = lax.linalg.cholesky(blk[k][k], symmetrize_input=False)  75.3 us
    another operation x12, other arithmetic, block_solve(): inv[k] = lax.linalg.triangular_solve(diag, eye, left_side=True, lower=True)  63.1 us
    ppermute x16, waiting for transfers between devices, tree_sum(): other = lax.ppermute(cur, axis, perm)  36.5 us
    ppermute x16, waiting for transfers between devices, tree_sum(): cur = keep + lax.ppermute(away, axis, perm)  31.2 us
    ppermute x16, starting transfers between devices, tree_sum(): cur = keep + lax.ppermute(away, axis, perm)  24.9 us
    ppermute x16, starting transfers between devices, tree_sum(): other = lax.ppermute(cur, axis, perm)  23.4 us
    dot_general x29, matrix products, full_dot(): jnp.dot(left, right, precision=lax.Precision.HIGHEST, preferred_element_t...  11.2 us
    ppermute x2, waiting for transfers between devices, tree_sum_exact(): x = x + lax.ppermute(x, axis, perm)  10.3 us
  transfers between devices with their start and end apart: 34, of which 29 were waited for; matrix products, arithmetic and copies ran while one was open for 35% of the time, Pallas kernels for 0%

profile of v5, /device:TPU:0, one launch (start us, length us, event | category | flops | bytes accessed | tf_op | source)
XLA Modules:
  0.0 316.4 jit_solution(11417678450690201935)
XLA Ops:
  4.0 3.0 collective-permute-start
  7.1 4.8 %collective-permute-done = f32[128,384]{1,0:T(8,128)S(1)} collective-permute-done((f32[128,384]{1,0:T(8,128)S(1)}, f32[128,384]{1,0:T(8,128)S(1)}, u32[]{:S(2)}, u32[]{:S(2)}) %collective-permute-start) | collective-permute-done | bytes 196640 | tf_op jit(solution)/shard_map/ppermute | solution.py:56
  16.9 3.8 %collective-permute-done.2 = f32[224,128]{0,1:T(8,128)S(1)} collective-permute-done((f32[224,128]{0,1:T(8,128)S(1)}, f32[224,128]{0,1:T(8,128)S(1)}, u32[]{:S(2)}, u32[]{:S(2)}) %collective-permute-start.2) | collective-permute-done | bytes 114720 | tf_op jit(solution)/shard_map/ppermute | solution.py:37
  25.4 2.8 collective-permute-start.4
  30.7 2.9 collective-permute-start.5
  49.5 11.7 %custom-call.16 = f32[128,128]{1,0:T(8,128)S(1)} custom-call(f32[128,128]{1,0:T(8,128)S(1)} %copy.60), custom_call_target="Cholesky" | custom-call | tf_op jit(solution)/shard_map/cholesky/custom-call.1 | solution.py:69
  62.7 9.8 %custom-call.17 = f32[1,128,128]{1,2,0:T(8,128)S(1)} custom-call(f32[1,128,128]{2,1,0:T(8,128)S(1)} %fusion.49), custom_call_target="InvertDiagBlocksLowerTriangular" | custom-call | tf_op jit(solution)/shard_map/triangular_solve/custom-call.0 | solution.py:70
  77.0 12.2 %custom-call.18 = f32[128,128]{1,0:T(8,128)S(1)} custom-call(f32[128,128]{1,0:T(8,128)S(1)} %copy.66), custom_call_target="Cholesky" | custom-call | tf_op jit(solution)/shard_map/cholesky/custom-call.1 | solution.py:69
  90.6 9.8 %custom-call.19 = f32[1,128,128]{1,2,0:T(8,128)S(1)} custom-call(f32[1,128,128]{2,1,0:T(8,128)S(1)} %fusion.50), custom_call_target="InvertDiagBlocksLowerTriangular" | custom-call | tf_op jit(solution)/shard_map/triangular_solve/custom-call.0 | solution.py:70
  102.8 11.7 %custom-call.20 = f32[128,128]{1,0:T(8,128)S(1)} custom-call(f32[128,128]{1,0:T(8,128)S(1)} %copy.73), custom_call_target="Cholesky" | custom-call | tf_op jit(solution)/shard_map/cholesky/custom-call.1 | solution.py:69
  119.6 9.8 %custom-call.21 = f32[1,128,128]{1,2,0:T(8,128)S(1)} custom-call(f32[1,128,128]{2,1,0:T(8,128)S(1)} %fusion.51), custom_call_target="InvertDiagBlocksLowerTriangular" | custom-call | tf_op jit(solution)/shard_map/triangular_solve/custom-call.0 | solution.py:70
  132.0 3.3 %collective-permute-done.11 = f32[48,640]{1,0:T(8,128)S(1)} collective-permute-done((f32[48,640]{1,0:T(8,128)S(1)}, f32[48,640]{1,0:T(8,128)S(1)}, u32[]{:S(2)}, u32[]{:S(2)}) %collective-permute-start.11) | collective-permute-done | bytes 122912 | tf_op jit(solution)/shard_map/ppermute | solution.py:37
  135.4 3.2 %collective-permute-start.12 = (f32[24,640]{1,0:T(8,128)S(1)}, f32[24,640]{1,0:T(8,128)S(1)}, u32[]{:S(2)}, u32[]{:S(2)}) collective-permute-start(f32[24,640]{1,0:T(8,128)S(1)} %constant_dynamic-slice_fusion.8), channel_id=1, source_target_pairs={{0,8},{1,9},{2,10},{3,11},{4,12},{5,13},{6,14},{7,15},{8,0},{9,1},... | collective-permute-start | bytes 184328 | tf_op jit(solution)/shard_map/ppermute | solution.py:37
  141.2 2.6 collective-permute-start.13
  148.5 2.9 collective-permute-done.14
  152.6 5.1 %collective-permute-done.15 = f32[96,640]{1,0:T(8,128)S(1)} collective-permute-done((f32[96,640]{1,0:T(8,128)S(1)}, f32[96,640]{1,0:T(8,128)S(1)}, u32[]{:S(2)}, u32[]{:S(2)}) %collective-permute-start.15) | collective-permute-done | bytes 245792 | tf_op jit(solution)/shard_map/ppermute | solution.py:43
  166.2 5.4 %collective-permute-done.17 = f32[128,384]{1,0:T(8,128)S(1)} collective-permute-done((f32[128,384]{1,0:T(8,128)S(1)}, f32[128,384]{1,0:T(8,128)S(1)}, u32[]{:S(2)}, u32[]{:S(2)}) %collective-permute-start.17) | collective-permute-done | bytes 196640 | tf_op jit(solution)/shard_map/ppermute | solution.py:56
  175.4 5.0 %collective-permute-done.19 = f32[224,128]{0,1:T(8,128)S(1)} collective-permute-done((f32[224,128]{0,1:T(8,128)S(1)}, f32[224,128]{0,1:T(8,128)S(1)}, u32[]{:S(2)}, u32[]{:S(2)}) %collective-permute-start.19) | collective-permute-done | bytes 114720 | tf_op jit(solution)/shard_map/ppermute | solution.py:37
  185.1 2.7 collective-permute-start.21
  190.4 2.8 collective-permute-start.22
  200.8 4.5 %collective-permute-done.24 = f32[224,128]{0,1:T(8,128)S(1)} collective-permute-done((f32[224,128]{0,1:T(8,128)S(1)}, f32[224,128]{0,1:T(8,128)S(1)}, u32[]{:S(2)}, u32[]{:S(2)}) %collective-permute-start.24) | collective-permute-done | bytes 114720 | tf_op jit(solution)/shard_map/ppermute | solution.py:43
  208.4 11.7 %custom-call.22 = f32[128,128]{1,0:T(8,128)S(1)} custom-call(f32[128,128]{1,0:T(8,128)S(1)} %fusion.83), custom_call_target="Cholesky" | custom-call | tf_op jit(solution)/shard_map/cholesky/custom-call.1 | solution.py:69
  221.6 9.8 %custom-call.23 = f32[1,128,128]{1,2,0:T(8,128)S(1)} custom-call(f32[1,128,128]{2,1,0:T(8,128)S(1)} %fusion.52), custom_call_target="InvertDiagBlocksLowerTriangular" | custom-call | tf_op jit(solution)/shard_map/triangular_solve/custom-call.0 | solution.py:70
  233.5 11.9 %custom-call.24 = f32[128,128]{1,0:T(8,128)S(1)} custom-call(f32[128,128]{1,0:T(8,128)S(1)} %convolution_subtract_fusion.9), custom_call_target="Cholesky" | custom-call | tf_op jit(solution)/shard_map/cholesky/custom-call.1 | solution.py:69
  246.8 9.8 %custom-call.25 = f32[1,128,128]{1,2,0:T(8,128)S(1)} custom-call(f32[1,128,128]{2,1,0:T(8,128)S(1)} %fusion.53), custom_call_target="InvertDiagBlocksLowerTriangular" | custom-call | tf_op jit(solution)/shard_map/triangular_solve/custom-call.0 | solution.py:70
  257.7 11.7 %custom-call.26 = f32[128,128]{1,0:T(8,128)S(1)} custom-call(f32[128,128]{1,0:T(8,128)S(1)} %convolution_subtract_fusion.5), custom_call_target="Cholesky" | custom-call | tf_op jit(solution)/shard_map/cholesky/custom-call.1 | solution.py:69
  273.7 10.0 %custom-call.27 = f32[1,128,128]{1,2,0:T(8,128)S(1)} custom-call(f32[1,128,128]{2,1,0:T(8,128)S(1)} %fusion.54), custom_call_target="InvertDiagBlocksLowerTriangular" | custom-call | tf_op jit(solution)/shard_map/triangular_solve/custom-call.0 | solution.py:70
  286.3 3.3 %collective-permute-done.28 = f32[48,640]{1,0:T(8,128)S(1)} collective-permute-done((f32[48,640]{1,0:T(8,128)S(1)}, f32[48,640]{1,0:T(8,128)S(1)}, u32[]{:S(2)}, u32[]{:S(2)}) %collective-permute-start.28) | collective-permute-done | bytes 122912 | tf_op jit(solution)/shard_map/ppermute | solution.py:37
  289.6 3.3 %collective-permute-start.29 = (f32[24,640]{1,0:T(8,128)S(1)}, f32[24,640]{1,0:T(8,128)S(1)}, u32[]{:S(2)}, u32[]{:S(2)}) collective-permute-start(f32[24,640]{1,0:T(8,128)S(1)} %constant_dynamic-slice_fusion), channel_id=1, source_target_pairs={{0,8},{1,9},{2,10},{3,11},{4,12},{5,13},{6,14},{7,15},{8,0},{9,1},... | collective-permute-start | bytes 184328 | tf_op jit(solution)/shard_map/ppermute | solution.py:37
  295.6 2.6 collective-permute-start.30
  302.8 2.9 collective-permute-done.31
  307.9 4.1 %collective-permute-done.32 = f32[96,640]{1,0:T(8,128)S(1)} collective-permute-done((f32[96,640]{1,0:T(8,128)S(1)}, f32[96,640]{1,0:T(8,128)S(1)}, u32[]{:S(2)}, u32[]{:S(2)}) %collective-permute-start.32) | collective-permute-done | bytes 245792 | tf_op jit(solution)/shard_map/ppermute | solution.py:43
  (284 shorter events, 113.3 us)
Async XLA Ops:
  4.0 7.9 %collective-permute-start = (f32[128,384]{1,0:T(8,128)S(1)}, f32[128,384]{1,0:T(8,128)S(1)}, u32[]{:S(2)}, u32[]{:S(2)}) collective-permute-start(f32[128,384]{1,0:T(8,128)S(1)} %bitcast_select_fusion), channel_id=1, source_target_pairs={{0,16},{16,0},{1,17},{17,1},{2,18},{18,2},{3,19},{19,3},{4,20},{20... | collective-permute-start | bytes 589832 | tf_op jit(solution)/shard_map/ppermute | solution.py:56
  15.1 5.6 %collective-permute-start.2 = (f32[224,128]{0,1:T(8,128)S(1)}, f32[224,128]{0,1:T(8,128)S(1)}, u32[]{:S(2)}, u32[]{:S(2)}) collective-permute-start(f32[224,128]{0,1:T(8,128)S(1)} %constant_dynamic-slice_fusion.14), channel_id=1, source_target_pairs={{0,2},{1,3},{2,0},{3,1},{4,6},{5,7},{6,4},{7,5},{8,10},{9,11},{10,... | collective-permute-start | bytes 344072 | tf_op jit(solution)/shard_map/ppermute | solution.py:37
  20.9 4.3 %collective-permute-start.3 = (f32[112,128]{0,1:T(8,128)S(1)}, f32[112,128]{0,1:T(8,128)S(1)}, u32[]{:S(2)}, u32[]{:S(2)}) collective-permute-start(f32[112,128]{0,1:T(8,128)S(1)} %constant_dynamic-slice_fusion.13), channel_id=1, source_target_pairs={{0,4},{1,5},{2,6},{3,7},{4,0},{5,1},{6,2},{7,3},{8,12},{9,13},{10,... | collective-permute-start | bytes 172040 | tf_op jit(solution)/shard_map/ppermute | solution.py:37
  25.4 5.2 %collective-permute-start.4 = (f32[56,128]{0,1:T(8,128)S(1)}, f32[56,128]{0,1:T(8,128)S(1)}, u32[]{:S(2)}, u32[]{:S(2)}) collective-permute-start(f32[56,128]{0,1:T(8,128)S(1)} %constant_dynamic-slice_fusion.12), channel_id=1, source_target_pairs={{0,8},{1,9},{2,10},{3,11},{4,12},{5,13},{6,14},{7,15},{8,0},{9,1},... | collective-permute-start | bytes 86024 | tf_op jit(solution)/shard_map/ppermute | solution.py:37
  30.7 5.3 %collective-permute-start.5 = (f32[56,128]{0,1:T(8,128)S(1)}, f32[56,128]{0,1:T(8,128)S(1)}, u32[]{:S(2)}, u32[]{:S(2)}) collective-permute-start(f32[56,128]{0,1:T(8,128)S(1)} %dynamic-slice_add_fusion.12), channel_id=1, source_target_pairs={{0,8},{1,9},{2,10},{3,11},{4,12},{5,13},{6,14},{7,15},{8,0},{9,1},... | collective-permute-start | bytes 86024 | tf_op jit(solution)/shard_map/ppermute | solution.py:43
  36.2 4.4 %collective-permute-start.6 = (f32[112,128]{0,1:T(8,128)S(1)}, f32[112,128]{0,1:T(8,128)S(1)}, u32[]{:S(2)}, u32[]{:S(2)}) collective-permute-start(f32[112,128]{0,1:T(8,128)S(1)} %maximum_select_fusion.14), channel_id=1, source_target_pairs={{0,4},{1,5},{2,6},{3,7},{4,0},{5,1},{6,2},{7,3},{8,12},{9,13},{10,... | collective-permute-start | bytes 172040 | tf_op jit(solution)/shard_map/ppermute | solution.py:43
  40.7 5.0 %collective-permute-start.7 = (f32[224,128]{0,1:T(8,128)S(1)}, f32[224,128]{0,1:T(8,128)S(1)}, u32[]{:S(2)}, u32[]{:S(2)}) collective-permute-start(f32[224,128]{0,1:T(8,128)S(1)} %maximum_select_fusion.10), channel_id=1, source_target_pairs={{0,2},{1,3},{2,0},{3,1},{4,6},{5,7},{6,4},{7,5},{8,10},{9,11},{10,... | collective-permute-start | bytes 344072 | tf_op jit(solution)/shard_map/ppermute | solution.py:43
  45.9 1.6 collective-permute-start.8
  73.5 42.6 %collective-permute-start.9 = (f32[192,640]{1,0:T(8,128)S(1)}, f32[192,640]{1,0:T(8,128)}, u32[]{:S(2)}, u32[]{:S(2)}) collective-permute-start(f32[192,640]{1,0:T(8,128)S(1)} %constant_dynamic-slice_fusion.11), channel_id=1, source_target_pairs={{0,1},{1,0},{2,3},{3,2},{4,5},{5,4},{6,7},{7,6},{8,9},{9,8},{10,11... | collective-permute-start | bytes 1474568 | tf_op jit(solution)/shard_map/ppermute | solution.py:37
  117.2 12.5 %collective-permute-start.10 = (f32[96,640]{1,0:T(8,128)S(1)}, f32[96,640]{1,0:T(8,128)S(1)}, u32[]{:S(2)}, u32[]{:S(2)}) collective-permute-start(f32[96,640]{1,0:T(8,128)S(1)} %constant_dynamic-slice_fusion.10), channel_id=1, source_target_pairs={{0,2},{1,3},{2,0},{3,1},{4,6},{5,7},{6,4},{7,5},{8,10},{9,11},{10,... | collective-permute-start | bytes 737288 | tf_op jit(solution)/shard_map/ppermute | solution.py:37
  129.8 5.6 %collective-permute-start.11 = (f32[48,640]{1,0:T(8,128)S(1)}, f32[48,640]{1,0:T(8,128)S(1)}, u32[]{:S(2)}, u32[]{:S(2)}) collective-permute-start(f32[48,640]{1,0:T(8,128)S(1)} %constant_dynamic-slice_fusion.9), channel_id=1, source_target_pairs={{0,4},{1,5},{2,6},{3,7},{4,0},{5,1},{6,2},{7,3},{8,12},{9,13},{10,... | collective-permute-start | bytes 368648 | tf_op jit(solution)/shard_map/ppermute | solution.py:37
  135.4 5.8 %collective-permute-start.12 = (f32[24,640]{1,0:T(8,128)S(1)}, f32[24,640]{1,0:T(8,128)S(1)}, u32[]{:S(2)}, u32[]{:S(2)}) collective-permute-start(f32[24,640]{1,0:T(8,128)S(1)} %constant_dynamic-slice_fusion.8), channel_id=1, source_target_pairs={{0,8},{1,9},{2,10},{3,11},{4,12},{5,13},{6,14},{7,15},{8,0},{9,1},... | collective-permute-start | bytes 184328 | tf_op jit(solution)/shard_map/ppermute | solution.py:37
  141.2 5.2 %collective-permute-start.13 = (f32[24,640]{1,0:T(8,128)S(1)}, f32[24,640]{1,0:T(8,128)S(1)}, u32[]{:S(2)}, u32[]{:S(2)}) collective-permute-start(f32[24,640]{1,0:T(8,128)S(1)} %dynamic-slice_add_fusion.15), channel_id=1, source_target_pairs={{0,8},{1,9},{2,10},{3,11},{4,12},{5,13},{6,14},{7,15},{8,0},{9,1},... | collective-permute-start | bytes 184328 | tf_op jit(solution)/shard_map/ppermute | solution.py:43
  146.4 4.9 %collective-permute-start.14 = (f32[48,640]{1,0:T(8,128)S(1)}, f32[48,640]{1,0:T(8,128)S(1)}, u32[]{:S(2)}, u32[]{:S(2)}) collective-permute-start(f32[48,640]{1,0:T(8,128)S(1)} %maximum_select_fusion.12), channel_id=1, source_target_pairs={{0,4},{1,5},{2,6},{3,7},{4,0},{5,1},{6,2},{7,3},{8,12},{9,13},{10,... | collective-permute-start | bytes 368648 | tf_op jit(solution)/shard_map/ppermute | solution.py:43
  151.5 6.3 %collective-permute-start.15 = (f32[96,640]{1,0:T(8,128)S(1)}, f32[96,640]{1,0:T(8,128)S(1)}, u32[]{:S(2)}, u32[]{:S(2)}) collective-permute-start(f32[96,640]{1,0:T(8,128)S(1)} %maximum_select_fusion.8), channel_id=1, source_target_pairs={{0,2},{1,3},{2,0},{3,1},{4,6},{5,7},{6,4},{7,5},{8,10},{9,11},{10,... | collective-permute-start | bytes 737288 | tf_op jit(solution)/shard_map/ppermute | solution.py:43
  157.8 1.9 collective-permute-start.16
  164.7 7.0 %collective-permute-start.17 = (f32[128,384]{1,0:T(8,128)S(1)}, f32[128,384]{1,0:T(8,128)S(1)}, u32[]{:S(2)}, u32[]{:S(2)}) collective-permute-start(f32[128,384]{1,0:T(8,128)S(1)} %fusion), channel_id=1, source_target_pairs={{0,16},{16,0},{1,17},{17,1},{2,18},{18,2},{3,19},{19,3},{4,20},{20... | collective-permute-start | bytes 589832 | tf_op jit(solution)/shard_map/ppermute | solution.py:56
  172.9 1.6 collective-permute-start.18
  174.8 5.6 %collective-permute-start.19 = (f32[224,128]{0,1:T(8,128)S(1)}, f32[224,128]{0,1:T(8,128)S(1)}, u32[]{:S(2)}, u32[]{:S(2)}) collective-permute-start(f32[224,128]{0,1:T(8,128)S(1)} %constant_dynamic-slice_fusion.6), channel_id=1, source_target_pairs={{0,2},{1,3},{2,0},{3,1},{4,6},{5,7},{6,4},{7,5},{8,10},{9,11},{10,... | collective-permute-start | bytes 344072 | tf_op jit(solution)/shard_map/ppermute | solution.py:37
  180.6 4.3 %collective-permute-start.20 = (f32[112,128]{0,1:T(8,128)S(1)}, f32[112,128]{0,1:T(8,128)S(1)}, u32[]{:S(2)}, u32[]{:S(2)}) collective-permute-start(f32[112,128]{0,1:T(8,128)S(1)} %constant_dynamic-slice_fusion.5), channel_id=1, source_target_pairs={{0,4},{1,5},{2,6},{3,7},{4,0},{5,1},{6,2},{7,3},{8,12},{9,13},{10,... | collective-permute-start | bytes 172040 | tf_op jit(solution)/shard_map/ppermute | solution.py:37
  185.1 5.2 %collective-permute-start.21 = (f32[56,128]{0,1:T(8,128)S(1)}, f32[56,128]{0,1:T(8,128)S(1)}, u32[]{:S(2)}, u32[]{:S(2)}) collective-permute-start(f32[56,128]{0,1:T(8,128)S(1)} %constant_dynamic-slice_fusion.4), channel_id=1, source_target_pairs={{0,8},{1,9},{2,10},{3,11},{4,12},{5,13},{6,14},{7,15},{8,0},{9,1},... | collective-permute-start | bytes 86024 | tf_op jit(solution)/shard_map/ppermute | solution.py:37
  190.4 5.3 %collective-permute-start.22 = (f32[56,128]{0,1:T(8,128)S(1)}, f32[56,128]{0,1:T(8,128)S(1)}, u32[]{:S(2)}, u32[]{:S(2)}) collective-permute-start(f32[56,128]{0,1:T(8,128)S(1)} %dynamic-slice_add_fusion.10), channel_id=1, source_target_pairs={{0,8},{1,9},{2,10},{3,11},{4,12},{5,13},{6,14},{7,15},{8,0},{9,1},... | collective-permute-start | bytes 86024 | tf_op jit(solution)/shard_map/ppermute | solution.py:43
  195.8 4.3 %collective-permute-start.23 = (f32[112,128]{0,1:T(8,128)S(1)}, f32[112,128]{0,1:T(8,128)S(1)}, u32[]{:S(2)}, u32[]{:S(2)}) collective-permute-start(f32[112,128]{0,1:T(8,128)S(1)} %maximum_select_fusion.15), channel_id=1, source_target_pairs={{0,4},{1,5},{2,6},{3,7},{4,0},{5,1},{6,2},{7,3},{8,12},{9,13},{10,... | collective-permute-start | bytes 172040 | tf_op jit(solution)/shard_map/ppermute | solution.py:43
  200.3 5.0 %collective-permute-start.24 = (f32[224,128]{0,1:T(8,128)S(1)}, f32[224,128]{0,1:T(8,128)S(1)}, u32[]{:S(2)}, u32[]{:S(2)}) collective-permute-start(f32[224,128]{0,1:T(8,128)S(1)} %maximum_select_fusion.11), channel_id=1, source_target_pairs={{0,2},{1,3},{2,0},{3,1},{4,6},{5,7},{6,4},{7,5},{8,10},{9,11},{10,... | collective-permute-start | bytes 344072 | tf_op jit(solution)/shard_map/ppermute | solution.py:43
  232.4 38.9 %collective-permute-start.26 = (f32[192,640]{1,0:T(8,128)S(1)}, f32[192,640]{1,0:T(8,128)}, u32[]{:S(2)}, u32[]{:S(2)}) collective-permute-start(f32[192,640]{1,0:T(8,128)S(1)} %constant_dynamic-slice_fusion.3), channel_id=1, source_target_pairs={{0,1},{1,0},{2,3},{3,2},{4,5},{5,4},{6,7},{7,6},{8,9},{9,8},{10,11... | collective-permute-start | bytes 1474568 | tf_op jit(solution)/shard_map/ppermute | solution.py:37
  272.4 11.6 %collective-permute-start.27 = (f32[96,640]{1,0:T(8,128)S(1)}, f32[96,640]{1,0:T(8,128)S(1)}, u32[]{:S(2)}, u32[]{:S(2)}) collective-permute-start(f32[96,640]{1,0:T(8,128)S(1)} %constant_dynamic-slice_fusion.2), channel_id=1, source_target_pairs={{0,2},{1,3},{2,0},{3,1},{4,6},{5,7},{6,4},{7,5},{8,10},{9,11},{10,... | collective-permute-start | bytes 737288 | tf_op jit(solution)/shard_map/ppermute | solution.py:37
  284.1 5.5 %collective-permute-start.28 = (f32[48,640]{1,0:T(8,128)S(1)}, f32[48,640]{1,0:T(8,128)S(1)}, u32[]{:S(2)}, u32[]{:S(2)}) collective-permute-start(f32[48,640]{1,0:T(8,128)S(1)} %constant_dynamic-slice_fusion.1), channel_id=1, source_target_pairs={{0,4},{1,5},{2,6},{3,7},{4,0},{5,1},{6,2},{7,3},{8,12},{9,13},{10,... | collective-permute-start | bytes 368648 | tf_op jit(solution)/shard_map/ppermute | solution.py:37
  289.6 5.9 %collective-permute-start.29 = (f32[24,640]{1,0:T(8,128)S(1)}, f32[24,640]{1,0:T(8,128)S(1)}, u32[]{:S(2)}, u32[]{:S(2)}) collective-permute-start(f32[24,640]{1,0:T(8,128)S(1)} %constant_dynamic-slice_fusion), channel_id=1, source_target_pairs={{0,8},{1,9},{2,10},{3,11},{4,12},{5,13},{6,14},{7,15},{8,0},{9,1},... | collective-permute-start | bytes 184328 | tf_op jit(solution)/shard_map/ppermute | solution.py:37
  295.6 5.2 %collective-permute-start.30 = (f32[24,640]{1,0:T(8,128)S(1)}, f32[24,640]{1,0:T(8,128)S(1)}, u32[]{:S(2)}, u32[]{:S(2)}) collective-permute-start(f32[24,640]{1,0:T(8,128)S(1)} %dynamic-slice_add_fusion.14), channel_id=1, source_target_pairs={{0,8},{1,9},{2,10},{3,11},{4,12},{5,13},{6,14},{7,15},{8,0},{9,1},... | collective-permute-start | bytes 184328 | tf_op jit(solution)/shard_map/ppermute | solution.py:43
  300.8 4.9 %collective-permute-start.31 = (f32[48,640]{1,0:T(8,128)S(1)}, f32[48,640]{1,0:T(8,128)S(1)}, u32[]{:S(2)}, u32[]{:S(2)}) collective-permute-start(f32[48,640]{1,0:T(8,128)S(1)} %maximum_select_fusion.13), channel_id=1, source_target_pairs={{0,4},{1,5},{2,6},{3,7},{4,0},{5,1},{6,2},{7,3},{8,12},{9,13},{10,... | collective-permute-start | bytes 368648 | tf_op jit(solution)/shard_map/ppermute | solution.py:43
  305.7 6.3 %collective-permute-start.32 = (f32[96,640]{1,0:T(8,128)S(1)}, f32[96,640]{1,0:T(8,128)S(1)}, u32[]{:S(2)}, u32[]{:S(2)}) collective-permute-start(f32[96,640]{1,0:T(8,128)S(1)} %maximum_select_fusion.9), channel_id=1, source_target_pairs={{0,2},{1,3},{2,0},{3,1},{4,6},{5,7},{6,4},{7,5},{8,10},{9,11},{10,... | collective-permute-start | bytes 737288 | tf_op jit(solution)/shard_map/ppermute | solution.py:43
  312.0 2.2 collective-permute-start.33
  (17 other events, 20.4 us)

commit v6 on v5

--- a/solution.py
+++ b/solution.py
@@ -133,7 +133,7 @@
         part = gram_blocks[p * size:(p + 1) * size] + corr[i * size:(i + 1) * size, j * size:(j + 1) * size]
         part = part / (count - 1.0)
         if i == j:
-            part = 0.5 * (part + part.T) + jnp.diag(noise[i * size:(i + 1) * size])
+            part = part + jnp.eye(size, dtype=part.dtype) * noise[i * size:(i + 1) * size][None, :]
         blk[i][j] = part
     obs_anom = observed - obs_mean[None, :]
     rhs = (target - obs_mean)[:, None] - 0.5 * obs_anom.T
@@ -152,8 +152,7 @@
         gain, cross = analyse(current, observed, obs_values[block], noise_var[block])
         if block + 1 < num_blocks:
             rows = obs_rows[block + 1]
-            picked = jnp.take(current, rows, axis=1)
-            cands = picked + full_dot(gain.T, jnp.take(cross, rows, axis=1))
+            cands = jnp.take(current, rows, axis=1) + full_dot(gain.T, jnp.take(cross, rows, axis=1))
         current = current + full_dot(gain.T, cross)
     return current
 

time: 320 us -> 308 us (0.963)
  local copies, waits for them, and re-layouts: 17 us -> 9.54 us
    another operation x19 -> x18, other arithmetic: 75.3 us -> 76 us  [block_solve(): diag = lax.linalg.cholesky(blk[k][k], symmetrize_input=False)]
  transfers between devices with their start and end apart: 34 -> 34, of which waited for: 29 -> 29; matrix products, arithmetic and copies ran while one was open for 35% -> 36% of each run, Pallas kernels for 0% -> 0%
where the time goes in v6:
time: 308 us; the launch traced here: 304 us
  other arithmetic  142 us (46%)
  waiting for transfers between devices  77.8 us (25%)
  starting transfers between devices  50.6 us (16%)
  matrix products  23.1 us (8%)
  local copies, waits for them, and re-layouts  9.54 us (3%)
    another operation x18, other arithmetic, block_solve(): diag = lax.linalg.cholesky(blk[k][k], symmetrize_input=False)  76 us
    another operation x12, other arithmetic, block_solve(): inv[k] = lax.linalg.triangular_solve(diag, eye, left_side=True, lower=True)  62.8 us
    ppermute x16, waiting for transfers between devices, tree_sum(): other = lax.ppermute(cur, axis, perm)  35.6 us
    ppermute x16, waiting for transfers between devices, tree_sum(): cur = keep + lax.ppermute(away, axis, perm)  31.8 us
    ppermute x16, starting transfers between devices, tree_sum(): cur = keep + lax.ppermute(away, axis, perm)  23.5 us
    ppermute x16, starting transfers between devices, tree_sum(): other = lax.ppermute(cur, axis, perm)  22.5 us
    dot_general x29, matrix products, full_dot(): jnp.dot(left, right, precision=lax.Precision.HIGHEST, preferred_element_t...  11.2 us
    ppermute x2, waiting for transfers between devices, tree_sum_exact(): x = x + lax.ppermute(x, axis, perm)  10.4 us
  transfers between devices with their start and end apart: 34, of which 29 were waited for; matrix products, arithmetic and copies ran while one was open for 36% of the time, Pallas kernels for 0%

profile of v6, /device:TPU:0, one launch (start us, length us, event | category | flops | bytes accessed | tf_op | source)
XLA Modules:
  0.0 304.5 jit_solution(3822394722578025869)
XLA Ops:
  4.0 3.0 collective-permute-start
  7.1 4.8 %collective-permute-done = f32[128,384]{1,0:T(8,128)S(1)} collective-permute-done((f32[128,384]{1,0:T(8,128)S(1)}, f32[128,384]{1,0:T(8,128)S(1)}, u32[]{:S(2)}, u32[]{:S(2)}) %collective-permute-start) | collective-permute-done | bytes 196640 | tf_op jit(solution)/shard_map/ppermute | solution.py:56
  16.4 3.4 %collective-permute-done.2 = f32[224,128]{1,0:T(8,128)S(1)} collective-permute-done((f32[224,128]{1,0:T(8,128)S(1)}, f32[224,128]{1,0:T(8,128)S(1)}, u32[]{:S(2)}, u32[]{:S(2)}) %collective-permute-start.2) | collective-permute-done | bytes 114720 | tf_op jit(solution)/shard_map/ppermute | solution.py:37
  24.2 2.9 collective-permute-start.4
  29.0 2.8 collective-permute-start.5
  45.5 11.7 %custom-call.16 = f32[128,128]{1,0:T(8,128)S(1)} custom-call(f32[128,128]{1,0:T(8,128)S(1)} %fusion.84), custom_call_target="Cholesky" | custom-call | tf_op jit(solution)/shard_map/cholesky/custom-call.1 | solution.py:69
  58.7 9.8 %custom-call.17 = f32[1,128,128]{1,2,0:T(8,128)S(1)} custom-call(f32[1,128,128]{2,1,0:T(8,128)S(1)} %fusion.49), custom_call_target="InvertDiagBlocksLowerTriangular" | custom-call | tf_op jit(solution)/shard_map/triangular_solve/custom-call.0 | solution.py:70
  71.0 12.9 %custom-call.18 = f32[128,128]{1,0:T(8,128)S(1)} custom-call(f32[128,128]{1,0:T(8,128)} %convolution_subtract_fusion.19), custom_call_target="Cholesky" | custom-call | tf_op jit(solution)/shard_map/cholesky/custom-call.1 | solution.py:69
  85.3 9.8 %custom-call.19 = f32[1,128,128]{1,2,0:T(8,128)S(1)} custom-call(f32[1,128,128]{2,1,0:T(8,128)S(1)} %fusion.50), custom_call_target="InvertDiagBlocksLowerTriangular" | custom-call | tf_op jit(solution)/shard_map/triangular_solve/custom-call.0 | solution.py:70
  96.0 11.7 %custom-call.20 = f32[128,128]{1,0:T(8,128)S(1)} custom-call(f32[128,128]{1,0:T(8,128)S(1)} %convolution_subtract_fusion.15), custom_call_target="Cholesky" | custom-call | tf_op jit(solution)/shard_map/cholesky/custom-call.1 | solution.py:69
  112.7 9.8 %custom-call.21 = f32[1,128,128]{1,2,0:T(8,128)S(1)} custom-call(f32[1,128,128]{2,1,0:T(8,128)S(1)} %fusion.51), custom_call_target="InvertDiagBlocksLowerTriangular" | custom-call | tf_op jit(solution)/shard_map/triangular_solve/custom-call.0 | solution.py:70
  125.2 3.3 %collective-permute-done.11 = f32[48,640]{1,0:T(8,128)S(1)} collective-permute-done((f32[48,640]{1,0:T(8,128)S(1)}, f32[48,640]{1,0:T(8,128)S(1)}, u32[]{:S(2)}, u32[]{:S(2)}) %collective-permute-start.11) | collective-permute-done | bytes 122912 | tf_op jit(solution)/shard_map/ppermute | solution.py:37
  131.3 2.5 collective-permute-done.12
  136.5 2.5 collective-permute-done.13
  141.0 3.0 collective-permute-done.14
  145.2 5.1 %collective-permute-done.15 = f32[96,640]{1,0:T(8,128)S(1)} collective-permute-done((f32[96,640]{1,0:T(8,128)S(1)}, f32[96,640]{1,0:T(8,128)S(1)}, u32[]{:S(2)}, u32[]{:S(2)}) %collective-permute-start.15) | collective-permute-done | bytes 245792 | tf_op jit(solution)/shard_map/ppermute | solution.py:43
  158.8 5.6 %collective-permute-done.17 = f32[128,384]{1,0:T(8,128)S(1)} collective-permute-done((f32[128,384]{1,0:T(8,128)S(1)}, f32[128,384]{1,0:T(8,128)S(1)}, u32[]{:S(2)}, u32[]{:S(2)}) %collective-permute-start.17) | collective-permute-done | bytes 196640 | tf_op jit(solution)/shard_map/ppermute | solution.py:56
  167.5 4.7 %collective-permute-done.19 = f32[224,128]{1,0:T(8,128)S(1)} collective-permute-done((f32[224,128]{1,0:T(8,128)S(1)}, f32[224,128]{1,0:T(8,128)S(1)}, u32[]{:S(2)}, u32[]{:S(2)}) %collective-permute-start.19) | collective-permute-done | bytes 114720 | tf_op jit(solution)/shard_map/ppermute | solution.py:37
  173.9 2.6 collective-permute-done.20
  176.5 2.5 collective-permute-start.21
  190.9 4.3 %collective-permute-done.24 = f32[224,128]{1,0:T(8,128)S(1)} collective-permute-done((f32[224,128]{1,0:T(8,128)S(1)}, f32[224,128]{1,0:T(8,128)S(1)}, u32[]{:S(2)}, u32[]{:S(2)}) %collective-permute-start.24) | collective-permute-done | bytes 114720 | tf_op jit(solution)/shard_map/ppermute | solution.py:43
  197.7 11.7 %custom-call.22 = f32[128,128]{1,0:T(8,128)S(1)} custom-call(f32[128,128]{1,0:T(8,128)S(1)} %fusion.69), custom_call_target="Cholesky" | custom-call | tf_op jit(solution)/shard_map/cholesky/custom-call.1 | solution.py:69
  210.9 9.8 %custom-call.23 = f32[1,128,128]{1,2,0:T(8,128)S(1)} custom-call(f32[1,128,128]{2,1,0:T(8,128)S(1)} %fusion.52), custom_call_target="InvertDiagBlocksLowerTriangular" | custom-call | tf_op jit(solution)/shard_map/triangular_solve/custom-call.0 | solution.py:70
  222.6 11.9 %custom-call.24 = f32[128,128]{1,0:T(8,128)S(1)} custom-call(f32[128,128]{1,0:T(8,128)S(1)} %convolution_subtract_fusion.9), custom_call_target="Cholesky" | custom-call | tf_op jit(solution)/shard_map/cholesky/custom-call.1 | solution.py:69
  235.9 9.8 %custom-call.25 = f32[1,128,128]{1,2,0:T(8,128)S(1)} custom-call(f32[1,128,128]{2,1,0:T(8,128)S(1)} %fusion.53), custom_call_target="InvertDiagBlocksLowerTriangular" | custom-call | tf_op jit(solution)/shard_map/triangular_solve/custom-call.0 | solution.py:70
  246.5 11.7 %custom-call.26 = f32[128,128]{1,0:T(8,128)S(1)} custom-call(f32[128,128]{1,0:T(8,128)S(1)} %convolution_subtract_fusion.5), custom_call_target="Cholesky" | custom-call | tf_op jit(solution)/shard_map/cholesky/custom-call.1 | solution.py:69
  262.4 9.8 %custom-call.27 = f32[1,128,128]{1,2,0:T(8,128)S(1)} custom-call(f32[1,128,128]{2,1,0:T(8,128)S(1)} %fusion.54), custom_call_target="InvertDiagBlocksLowerTriangular" | custom-call | tf_op jit(solution)/shard_map/triangular_solve/custom-call.0 | solution.py:70
  275.0 3.3 %collective-permute-done.28 = f32[48,640]{1,0:T(8,128)S(1)} collective-permute-done((f32[48,640]{1,0:T(8,128)S(1)}, f32[48,640]{1,0:T(8,128)S(1)}, u32[]{:S(2)}, u32[]{:S(2)}) %collective-permute-start.28) | collective-permute-done | bytes 122912 | tf_op jit(solution)/shard_map/ppermute | solution.py:37
  278.3 2.8 collective-permute-start.29
  283.8 2.5 collective-permute-start.30
  291.0 3.0 collective-permute-done.31
  296.2 4.1 %collective-permute-done.32 = f32[96,640]{1,0:T(8,128)S(1)} collective-permute-done((f32[96,640]{1,0:T(8,128)S(1)}, f32[96,640]{1,0:T(8,128)S(1)}, u32[]{:S(2)}, u32[]{:S(2)}) %collective-permute-start.32) | collective-permute-done | bytes 245792 | tf_op jit(solution)/shard_map/ppermute | solution.py:43
  (251 shorter events, 103.6 us)
Async XLA Ops:
  4.0 7.9 %collective-permute-start = (f32[128,384]{1,0:T(8,128)S(1)}, f32[128,384]{1,0:T(8,128)S(1)}, u32[]{:S(2)}, u32[]{:S(2)}) collective-permute-start(f32[128,384]{1,0:T(8,128)S(1)} %bitcast_select_fusion), channel_id=1, source_target_pairs={{0,16},{16,0},{1,17},{17,1},{2,18},{18,2},{3,19},{19,3},{4,20},{20... | collective-permute-start | bytes 589832 | tf_op jit(solution)/shard_map/ppermute | solution.py:56
  13.0 1.6 collective-permute-start.1
  14.6 5.3 %collective-permute-start.2 = (f32[224,128]{1,0:T(8,128)S(1)}, f32[224,128]{1,0:T(8,128)S(1)}, u32[]{:S(2)}, u32[]{:S(2)}) collective-permute-start(f32[224,128]{1,0:T(8,128)S(1)} %constant_dynamic-slice_fusion.14), channel_id=1, source_target_pairs={{0,2},{1,3},{2,0},{3,1},{4,6},{5,7},{6,4},{7,5},{8,10},{9,11},{10,... | collective-permute-start | bytes 344072 | tf_op jit(solution)/shard_map/ppermute | solution.py:37
  19.9 4.2 %collective-permute-start.3 = (f32[112,128]{1,0:T(8,128)S(1)}, f32[112,128]{1,0:T(8,128)S(1)}, u32[]{:S(2)}, u32[]{:S(2)}) collective-permute-start(f32[112,128]{1,0:T(8,128)S(1)} %constant_dynamic-slice_fusion.13), channel_id=1, source_target_pairs={{0,4},{1,5},{2,6},{3,7},{4,0},{5,1},{6,2},{7,3},{8,12},{9,13},{10,... | collective-permute-start | bytes 172040 | tf_op jit(solution)/shard_map/ppermute | solution.py:37
  24.2 4.8 %collective-permute-start.4 = (f32[56,128]{1,0:T(8,128)S(1)}, f32[56,128]{1,0:T(8,128)S(1)}, u32[]{:S(2)}, u32[]{:S(2)}) collective-permute-start(f32[56,128]{1,0:T(8,128)S(1)} %constant_dynamic-slice_fusion.12), channel_id=1, source_target_pairs={{0,8},{1,9},{2,10},{3,11},{4,12},{5,13},{6,14},{7,15},{8,0},{9,1},... | collective-permute-start | bytes 86024 | tf_op jit(solution)/shard_map/ppermute | solution.py:37
  29.0 4.8 %collective-permute-start.5 = (f32[56,128]{1,0:T(8,128)S(1)}, f32[56,128]{1,0:T(8,128)S(1)}, u32[]{:S(2)}, u32[]{:S(2)}) collective-permute-start(f32[56,128]{1,0:T(8,128)S(1)} %dynamic-slice_add_fusion.15), channel_id=1, source_target_pairs={{0,8},{1,9},{2,10},{3,11},{4,12},{5,13},{6,14},{7,15},{8,0},{9,1},... | collective-permute-start | bytes 86024 | tf_op jit(solution)/shard_map/ppermute | solution.py:43
  33.8 4.4 %collective-permute-start.6 = (f32[112,128]{1,0:T(8,128)S(1)}, f32[112,128]{1,0:T(8,128)S(1)}, u32[]{:S(2)}, u32[]{:S(2)}) collective-permute-start(f32[112,128]{1,0:T(8,128)S(1)} %maximum_select_fusion.14), channel_id=1, source_target_pairs={{0,4},{1,5},{2,6},{3,7},{4,0},{5,1},{6,2},{7,3},{8,12},{9,13},{10,... | collective-permute-start | bytes 172040 | tf_op jit(solution)/shard_map/ppermute | solution.py:43
  38.2 4.9 %collective-permute-start.7 = (f32[224,128]{1,0:T(8,128)S(1)}, f32[224,128]{1,0:T(8,128)S(1)}, u32[]{:S(2)}, u32[]{:S(2)}) collective-permute-start(f32[224,128]{1,0:T(8,128)S(1)} %maximum_select_fusion.12), channel_id=1, source_target_pairs={{0,2},{1,3},{2,0},{3,1},{4,6},{5,7},{6,4},{7,5},{8,10},{9,11},{10,... | collective-permute-start | bytes 344072 | tf_op jit(solution)/shard_map/ppermute | solution.py:43
  69.4 39.8 %collective-permute-start.9 = (f32[192,640]{1,0:T(8,128)S(1)}, f32[192,640]{1,0:T(8,128)}, u32[]{:S(2)}, u32[]{:S(2)}) collective-permute-start(f32[192,640]{1,0:T(8,128)S(1)} %constant_dynamic-slice_fusion.11), channel_id=1, source_target_pairs={{0,1},{1,0},{2,3},{3,2},{4,5},{5,4},{6,7},{7,6},{8,9},{9,8},{10,11... | collective-permute-start | bytes 1474568 | tf_op jit(solution)/shard_map/ppermute | solution.py:37
  110.4 12.4 %collective-permute-start.10 = (f32[96,640]{1,0:T(8,128)S(1)}, f32[96,640]{1,0:T(8,128)S(1)}, u32[]{:S(2)}, u32[]{:S(2)}) collective-permute-start(f32[96,640]{1,0:T(8,128)S(1)} %constant_dynamic-slice_fusion.10), channel_id=1, source_target_pairs={{0,2},{1,3},{2,0},{3,1},{4,6},{5,7},{6,4},{7,5},{8,10},{9,11},{10,... | collective-permute-start | bytes 737288 | tf_op jit(solution)/shard_map/ppermute | solution.py:37
  122.9 5.6 %collective-permute-start.11 = (f32[48,640]{1,0:T(8,128)S(1)}, f32[48,640]{1,0:T(8,128)S(1)}, u32[]{:S(2)}, u32[]{:S(2)}) collective-permute-start(f32[48,640]{1,0:T(8,128)S(1)} %constant_dynamic-slice_fusion.9), channel_id=1, source_target_pairs={{0,4},{1,5},{2,6},{3,7},{4,0},{5,1},{6,2},{7,3},{8,12},{9,13},{10,... | collective-permute-start | bytes 368648 | tf_op jit(solution)/shard_map/ppermute | solution.py:37
  128.5 5.3 %collective-permute-start.12 = (f32[24,640]{1,0:T(8,128)S(1)}, f32[24,640]{1,0:T(8,128)S(1)}, u32[]{:S(2)}, u32[]{:S(2)}) collective-permute-start(f32[24,640]{1,0:T(8,128)S(1)} %constant_dynamic-slice_fusion.8), channel_id=1, source_target_pairs={{0,8},{1,9},{2,10},{3,11},{4,12},{5,13},{6,14},{7,15},{8,0},{9,1},... | collective-permute-start | bytes 184328 | tf_op jit(solution)/shard_map/ppermute | solution.py:37
  133.8 5.2 %collective-permute-start.13 = (f32[24,640]{1,0:T(8,128)S(1)}, f32[24,640]{1,0:T(8,128)S(1)}, u32[]{:S(2)}, u32[]{:S(2)}) collective-permute-start(f32[24,640]{1,0:T(8,128)S(1)} %dynamic-slice_add_fusion.11), channel_id=1, source_target_pairs={{0,8},{1,9},{2,10},{3,11},{4,12},{5,13},{6,14},{7,15},{8,0},{9,1},... | collective-permute-start | bytes 184328 | tf_op jit(solution)/shard_map/ppermute | solution.py:43
  139.1 4.9 %collective-permute-start.14 = (f32[48,640]{1,0:T(8,128)S(1)}, f32[48,640]{1,0:T(8,128)S(1)}, u32[]{:S(2)}, u32[]{:S(2)}) collective-permute-start(f32[48,640]{1,0:T(8,128)S(1)} %maximum_select_fusion.10), channel_id=1, source_target_pairs={{0,4},{1,5},{2,6},{3,7},{4,0},{5,1},{6,2},{7,3},{8,12},{9,13},{10,... | collective-permute-start | bytes 368648 | tf_op jit(solution)/shard_map/ppermute | solution.py:43
  144.0 6.3 %collective-permute-start.15 = (f32[96,640]{1,0:T(8,128)S(1)}, f32[96,640]{1,0:T(8,128)S(1)}, u32[]{:S(2)}, u32[]{:S(2)}) collective-permute-start(f32[96,640]{1,0:T(8,128)S(1)} %maximum_select_fusion.6), channel_id=1, source_target_pairs={{0,2},{1,3},{2,0},{3,1},{4,6},{5,7},{6,4},{7,5},{8,10},{9,11},{10,... | collective-permute-start | bytes 737288 | tf_op jit(solution)/shard_map/ppermute | solution.py:43
  150.3 1.9 collective-permute-start.16
  157.2 7.1 %collective-permute-start.17 = (f32[128,384]{1,0:T(8,128)S(1)}, f32[128,384]{1,0:T(8,128)S(1)}, u32[]{:S(2)}, u32[]{:S(2)}) collective-permute-start(f32[128,384]{1,0:T(8,128)S(1)} %fusion), channel_id=1, source_target_pairs={{0,16},{16,0},{1,17},{17,1},{2,18},{18,2},{3,19},{19,3},{4,20},{20... | collective-permute-start | bytes 589832 | tf_op jit(solution)/shard_map/ppermute | solution.py:56
  167.0 5.3 %collective-permute-start.19 = (f32[224,128]{1,0:T(8,128)S(1)}, f32[224,128]{1,0:T(8,128)S(1)}, u32[]{:S(2)}, u32[]{:S(2)}) collective-permute-start(f32[224,128]{1,0:T(8,128)S(1)} %constant_dynamic-slice_fusion.6), channel_id=1, source_target_pairs={{0,2},{1,3},{2,0},{3,1},{4,6},{5,7},{6,4},{7,5},{8,10},{9,11},{10,... | collective-permute-start | bytes 344072 | tf_op jit(solution)/shard_map/ppermute | solution.py:37
  172.2 4.2 %collective-permute-start.20 = (f32[112,128]{1,0:T(8,128)S(1)}, f32[112,128]{1,0:T(8,128)S(1)}, u32[]{:S(2)}, u32[]{:S(2)}) collective-permute-start(f32[112,128]{1,0:T(8,128)S(1)} %constant_dynamic-slice_fusion.5), channel_id=1, source_target_pairs={{0,4},{1,5},{2,6},{3,7},{4,0},{5,1},{6,2},{7,3},{8,12},{9,13},{10,... | collective-permute-start | bytes 172040 | tf_op jit(solution)/shard_map/ppermute | solution.py:37
  176.5 4.8 %collective-permute-start.21 = (f32[56,128]{1,0:T(8,128)S(1)}, f32[56,128]{1,0:T(8,128)S(1)}, u32[]{:S(2)}, u32[]{:S(2)}) collective-permute-start(f32[56,128]{1,0:T(8,128)S(1)} %constant_dynamic-slice_fusion.4), channel_id=1, source_target_pairs={{0,8},{1,9},{2,10},{3,11},{4,12},{5,13},{6,14},{7,15},{8,0},{9,1},... | collective-permute-start | bytes 86024 | tf_op jit(solution)/shard_map/ppermute | solution.py:37
  181.4 4.8 %collective-permute-start.22 = (f32[56,128]{1,0:T(8,128)S(1)}, f32[56,128]{1,0:T(8,128)S(1)}, u32[]{:S(2)}, u32[]{:S(2)}) collective-permute-start(f32[56,128]{1,0:T(8,128)S(1)} %dynamic-slice_add_fusion.14), channel_id=1, source_target_pairs={{0,8},{1,9},{2,10},{3,11},{4,12},{5,13},{6,14},{7,15},{8,0},{9,1},... | collective-permute-start | bytes 86024 | tf_op jit(solution)/shard_map/ppermute | solution.py:43
  186.1 4.2 %collective-permute-start.23 = (f32[112,128]{1,0:T(8,128)S(1)}, f32[112,128]{1,0:T(8,128)S(1)}, u32[]{:S(2)}, u32[]{:S(2)}) collective-permute-start(f32[112,128]{1,0:T(8,128)S(1)} %maximum_select_fusion.15), channel_id=1, source_target_pairs={{0,4},{1,5},{2,6},{3,7},{4,0},{5,1},{6,2},{7,3},{8,12},{9,13},{10,... | collective-permute-start | bytes 172040 | tf_op jit(solution)/shard_map/ppermute | solution.py:43
  190.4 4.9 %collective-permute-start.24 = (f32[224,128]{1,0:T(8,128)S(1)}, f32[224,128]{1,0:T(8,128)S(1)}, u32[]{:S(2)}, u32[]{:S(2)}) collective-permute-start(f32[224,128]{1,0:T(8,128)S(1)} %maximum_select_fusion.13), channel_id=1, source_target_pairs={{0,2},{1,3},{2,0},{3,1},{4,6},{5,7},{6,4},{7,5},{8,10},{9,11},{10,... | collective-permute-start | bytes 344072 | tf_op jit(solution)/shard_map/ppermute | solution.py:43
  195.3 1.6 collective-permute-start.25
  221.6 38.5 %collective-permute-start.26 = (f32[192,640]{1,0:T(8,128)S(1)}, f32[192,640]{1,0:T(8,128)}, u32[]{:S(2)}, u32[]{:S(2)}) collective-permute-start(f32[192,640]{1,0:T(8,128)S(1)} %constant_dynamic-slice_fusion.3), channel_id=1, source_target_pairs={{0,1},{1,0},{2,3},{3,2},{4,5},{5,4},{6,7},{7,6},{8,9},{9,8},{10,11... | collective-permute-start | bytes 1474568 | tf_op jit(solution)/shard_map/ppermute | solution.py:37
  261.2 11.3 %collective-permute-start.27 = (f32[96,640]{1,0:T(8,128)S(1)}, f32[96,640]{1,0:T(8,128)S(1)}, u32[]{:S(2)}, u32[]{:S(2)}) collective-permute-start(f32[96,640]{1,0:T(8,128)S(1)} %constant_dynamic-slice_fusion.2), channel_id=1, source_target_pairs={{0,2},{1,3},{2,0},{3,1},{4,6},{5,7},{6,4},{7,5},{8,10},{9,11},{10,... | collective-permute-start | bytes 737288 | tf_op jit(solution)/shard_map/ppermute | solution.py:37
  272.6 5.7 %collective-permute-start.28 = (f32[48,640]{1,0:T(8,128)S(1)}, f32[48,640]{1,0:T(8,128)S(1)}, u32[]{:S(2)}, u32[]{:S(2)}) collective-permute-start(f32[48,640]{1,0:T(8,128)S(1)} %constant_dynamic-slice_fusion.1), channel_id=1, source_target_pairs={{0,4},{1,5},{2,6},{3,7},{4,0},{5,1},{6,2},{7,3},{8,12},{9,13},{10,... | collective-permute-start | bytes 368648 | tf_op jit(solution)/shard_map/ppermute | solution.py:37
  278.3 5.5 %collective-permute-start.29 = (f32[24,640]{1,0:T(8,128)S(1)}, f32[24,640]{1,0:T(8,128)S(1)}, u32[]{:S(2)}, u32[]{:S(2)}) collective-permute-start(f32[24,640]{1,0:T(8,128)S(1)} %constant_dynamic-slice_fusion), channel_id=1, source_target_pairs={{0,8},{1,9},{2,10},{3,11},{4,12},{5,13},{6,14},{7,15},{8,0},{9,1},... | collective-permute-start | bytes 184328 | tf_op jit(solution)/shard_map/ppermute | solution.py:37
  283.8 5.2 %collective-permute-start.30 = (f32[24,640]{1,0:T(8,128)S(1)}, f32[24,640]{1,0:T(8,128)S(1)}, u32[]{:S(2)}, u32[]{:S(2)}) collective-permute-start(f32[24,640]{1,0:T(8,128)S(1)} %dynamic-slice_add_fusion.10), channel_id=1, source_target_pairs={{0,8},{1,9},{2,10},{3,11},{4,12},{5,13},{6,14},{7,15},{8,0},{9,1},... | collective-permute-start | bytes 184328 | tf_op jit(solution)/shard_map/ppermute | solution.py:43
  289.0 4.9 %collective-permute-start.31 = (f32[48,640]{1,0:T(8,128)S(1)}, f32[48,640]{1,0:T(8,128)S(1)}, u32[]{:S(2)}, u32[]{:S(2)}) collective-permute-start(f32[48,640]{1,0:T(8,128)S(1)} %maximum_select_fusion.11), channel_id=1, source_target_pairs={{0,4},{1,5},{2,6},{3,7},{4,0},{5,1},{6,2},{7,3},{8,12},{9,13},{10,... | collective-permute-start | bytes 368648 | tf_op jit(solution)/shard_map/ppermute | solution.py:43
  294.0 6.3 %collective-permute-start.32 = (f32[96,640]{1,0:T(8,128)S(1)}, f32[96,640]{1,0:T(8,128)S(1)}, u32[]{:S(2)}, u32[]{:S(2)}) collective-permute-start(f32[96,640]{1,0:T(8,128)S(1)} %maximum_select_fusion.7), channel_id=1, source_target_pairs={{0,2},{1,3},{2,0},{3,1},{4,6},{5,7},{6,4},{7,5},{8,10},{9,11},{10,... | collective-permute-start | bytes 737288 | tf_op jit(solution)/shard_map/ppermute | solution.py:43
  300.3 2.2 collective-permute-start.33
  (11 other events, 17.0 us)

commit v7 on v5

--- a/solution.py
+++ b/solution.py
@@ -118,7 +118,6 @@
     packed = tree_sum(packed, "member")
     gram_blocks = packed[: len(pairs) * size]
     slots = packed[len(pairs) * size:].reshape(n_member, width)[:, : obs + n_rows]
-    cross_loc, gram_blocks, slots = lax.optimization_barrier((cross_loc, gram_blocks, slots))
     cross_sum = tree_sum(cross_loc, "member")
 
     means = jnp.mean(slots, axis=0)
@@ -133,13 +132,14 @@
         part = gram_blocks[p * size:(p + 1) * size] + corr[i * size:(i + 1) * size, j * size:(j + 1) * size]
         part = part / (count - 1.0)
         if i == j:
-            part = 0.5 * (part + part.T) + jnp.diag(noise[i * size:(i + 1) * size])
+            part = part + jnp.eye(size, dtype=part.dtype) * noise[i * size:(i + 1) * size][None, :]
         blk[i][j] = part
     obs_anom = observed - obs_mean[None, :]
     rhs = (target - obs_mean)[:, None] - 0.5 * obs_anom.T
+    shift = lax.optimization_barrier(m_loc * tdot(dev_obs, dev_row) / (count - 1.0))
     gain = block_solve(blk, rhs, size)
 
-    cross = (cross_sum + m_loc * tdot(dev_obs, dev_row)) / (count - 1.0)
+    cross = cross_sum / (count - 1.0) + shift
     return gain, cross
 
 

time: 320 us -> 286 us (0.89)
  waiting for transfers between devices: 78 us -> 64.4 us
  local copies, waits for them, and re-layouts: 17 us -> 9.09 us
  starting transfers between devices: 52.9 us -> 45.6 us
  other arithmetic: 143 us -> 139 us
    ppermute x16, waiting for transfers between devices: 31.2 us -> 20.8 us  [tree_sum(): cur = keep + lax.ppermute(away, axis, perm)]
    ppermute x16, starting transfers between devices: 23.4 us -> 18.4 us  [tree_sum(): other = lax.ppermute(cur, axis, perm)]
    unnamed x41 -> x21, local copies, waits for them, and re-layouts: 6.02 us -> 2.58 us
    another operation x19 -> x18, other arithmetic: 75.3 us -> 74.9 us  [block_solve(): diag = lax.linalg.cholesky(blk[k][k], symmetrize_input=False)]
  transfers between devices with their start and end apart: 34 -> 34, of which waited for: 29 -> 25; matrix products, arithmetic and copies ran while one was open for 35% -> 56% of each run, Pallas kernels for 0% -> 0%
where the time goes in v7:
time: 286 us; the launch traced here: 282 us
  other arithmetic  139 us (49%)
  waiting for transfers between devices  64.4 us (23%)
  starting transfers between devices  45.6 us (16%)
  matrix products  22.5 us (8%)
  local copies, waits for them, and re-layouts  9.09 us (3%)
    another operation x18, other arithmetic, block_solve(): diag = lax.linalg.cholesky(blk[k][k], symmetrize_input=False)  74.9 us
    another operation x12, other arithmetic, block_solve(): inv[k] = lax.linalg.triangular_solve(diag, eye, left_side=True, lower=True)  62.8 us
    ppermute x16, waiting for transfers between devices, tree_sum(): other = lax.ppermute(cur, axis, perm)  33.3 us
    ppermute x16, starting transfers between devices, tree_sum(): cur = keep + lax.ppermute(away, axis, perm)  22.6 us
    ppermute x16, waiting for transfers between devices, tree_sum(): cur = keep + lax.ppermute(away, axis, perm)  20.8 us
    ppermute x16, starting transfers between devices, tree_sum(): other = lax.ppermute(cur, axis, perm)  18.4 us
    dot_general x29, matrix products, full_dot(): jnp.dot(left, right, precision=lax.Precision.HIGHEST, preferred_element_t...  10.8 us
    ppermute x2, waiting for transfers between devices, tree_sum_exact(): x = x + lax.ppermute(x, axis, perm)  10.3 us
  transfers between devices with their start and end apart: 34, of which 25 were waited for; matrix products, arithmetic and copies ran while one was open for 56% of the time, Pallas kernels for 0%

profile of v7, /device:TPU:0, one launch (start us, length us, event | category | flops | bytes accessed | tf_op | source)
XLA Modules:
  0.0 282.0 jit_solution(3879090701947702962)
XLA Ops:
  4.0 3.0 %collective-permute-start = (f32[128,384]{1,0:T(8,128)S(1)}, f32[128,384]{1,0:T(8,128)S(1)}, u32[]{:S(2)}, u32[]{:S(2)}) collective-permute-start(f32[128,384]{1,0:T(8,128)S(1)} %bitcast_select_fusion), channel_id=1, source_target_pairs={{0,16},{16,0},{1,17},{17,1},{2,18},{18,2},{3,19},{19,3},{4,20},{20... | collective-permute-start | bytes 589832 | tf_op jit(solution)/shard_map/ppermute | solution.py:56
  7.1 4.8 %collective-permute-done = f32[128,384]{1,0:T(8,128)S(1)} collective-permute-done((f32[128,384]{1,0:T(8,128)S(1)}, f32[128,384]{1,0:T(8,128)S(1)}, u32[]{:S(2)}, u32[]{:S(2)}) %collective-permute-start) | collective-permute-done | bytes 196640 | tf_op jit(solution)/shard_map/ppermute | solution.py:56
  17.4 2.5 collective-permute-done.2
  21.9 2.3 collective-permute-done.3
  24.2 2.9 %collective-permute-start.4 = (f32[56,128]{1,0:T(8,128)S(1)}, f32[56,128]{1,0:T(8,128)S(1)}, u32[]{:S(2)}, u32[]{:S(2)}) collective-permute-start(f32[56,128]{1,0:T(8,128)S(1)} %constant_dynamic-slice_fusion.12), channel_id=1, source_target_pairs={{0,8},{1,9},{2,10},{3,11},{4,12},{5,13},{6,14},{7,15},{8,0},{9,1},... | collective-permute-start | bytes 86024 | tf_op jit(solution)/shard_map/ppermute | solution.py:37
  29.0 2.8 %collective-permute-start.5 = (f32[56,128]{1,0:T(8,128)S(1)}, f32[56,128]{1,0:T(8,128)S(1)}, u32[]{:S(2)}, u32[]{:S(2)}) collective-permute-start(f32[56,128]{1,0:T(8,128)S(1)} %dynamic-slice_add_fusion.15), channel_id=1, source_target_pairs={{0,8},{1,9},{2,10},{3,11},{4,12},{5,13},{6,14},{7,15},{8,0},{9,1},... | collective-permute-start | bytes 86024 | tf_op jit(solution)/shard_map/ppermute | solution.py:43
  36.0 2.7 collective-permute-done.6
  45.4 2.5 collective-permute-start.12
  48.7 11.7 %custom-call.16 = f32[128,128]{1,0:T(8,128)S(1)} custom-call(f32[128,128]{1,0:T(8,128)S(1)} %fusion.88), custom_call_target="Cholesky" | custom-call | tf_op jit(solution)/shard_map/cholesky/custom-call.1 | solution.py:69
  61.8 9.8 %custom-call.17 = f32[1,128,128]{1,2,0:T(8,128)S(1)} custom-call(f32[1,128,128]{2,1,0:T(8,128)S(1)} %fusion.49), custom_call_target="InvertDiagBlocksLowerTriangular" | custom-call | tf_op jit(solution)/shard_map/triangular_solve/custom-call.0 | solution.py:70
  74.1 12.1 %custom-call.18 = f32[128,128]{1,0:T(8,128)S(1)} custom-call(f32[128,128]{1,0:T(8,128)S(1)} %convolution_subtract_fusion.19), custom_call_target="Cholesky" | custom-call | tf_op jit(solution)/shard_map/cholesky/custom-call.1 | solution.py:69
  87.5 9.8 %custom-call.19 = f32[1,128,128]{1,2,0:T(8,128)S(1)} custom-call(f32[1,128,128]{2,1,0:T(8,128)S(1)} %fusion.50), custom_call_target="InvertDiagBlocksLowerTriangular" | custom-call | tf_op jit(solution)/shard_map/triangular_solve/custom-call.0 | solution.py:70
  98.2 11.7 %custom-call.20 = f32[128,128]{1,0:T(8,128)S(1)} custom-call(f32[128,128]{1,0:T(8,128)S(1)} %convolution_subtract_fusion.15), custom_call_target="Cholesky" | custom-call | tf_op jit(solution)/shard_map/cholesky/custom-call.1 | solution.py:69
  111.2 9.8 %custom-call.21 = f32[1,128,128]{1,2,0:T(8,128)S(1)} custom-call(f32[1,128,128]{2,1,0:T(8,128)S(1)} %fusion.51), custom_call_target="InvertDiagBlocksLowerTriangular" | custom-call | tf_op jit(solution)/shard_map/triangular_solve/custom-call.0 | solution.py:70
  123.4 4.3 %collective-permute-done.13 = f32[24,640]{1,0:T(8,128)S(1)} collective-permute-done((f32[24,640]{1,0:T(8,128)S(1)}, f32[24,640]{1,0:T(8,128)S(1)}, u32[]{:S(2)}, u32[]{:S(2)}) %collective-permute-start.13) | collective-permute-done | bytes 61472 | tf_op jit(solution)/shard_map/ppermute | solution.py:43
  129.6 3.1 %collective-permute-done.14 = f32[48,640]{1,0:T(8,128)S(1)} collective-permute-done((f32[48,640]{1,0:T(8,128)S(1)}, f32[48,640]{1,0:T(8,128)S(1)}, u32[]{:S(2)}, u32[]{:S(2)}) %collective-permute-start.14) | collective-permute-done | bytes 122912 | tf_op jit(solution)/shard_map/ppermute | solution.py:43
  134.6 4.4 %collective-permute-done.15 = f32[96,640]{1,0:T(8,128)S(1)} collective-permute-done((f32[96,640]{1,0:T(8,128)S(1)}, f32[96,640]{1,0:T(8,128)S(1)}, u32[]{:S(2)}, u32[]{:S(2)}) %collective-permute-start.15) | collective-permute-done | bytes 245792 | tf_op jit(solution)/shard_map/ppermute | solution.py:43
  146.6 5.4 %collective-permute-done.17 = f32[128,384]{1,0:T(8,128)S(1)} collective-permute-done((f32[128,384]{1,0:T(8,128)S(1)}, f32[128,384]{1,0:T(8,128)S(1)}, u32[]{:S(2)}, u32[]{:S(2)}) %collective-permute-start.17) | collective-permute-done | bytes 196640 | tf_op jit(solution)/shard_map/ppermute | solution.py:56
  156.6 3.3 %collective-permute-done.19 = f32[224,128]{1,0:T(8,128)S(1)} collective-permute-done((f32[224,128]{1,0:T(8,128)S(1)}, f32[224,128]{1,0:T(8,128)S(1)}, u32[]{:S(2)}, u32[]{:S(2)}) %collective-permute-start.19) | collective-permute-done | bytes 114720 | tf_op jit(solution)/shard_map/ppermute | solution.py:37
  161.7 2.6 collective-permute-done.20
  166.0 3.1 %collective-permute-done.21 = f32[56,128]{1,0:T(8,128)S(1)} collective-permute-done((f32[56,128]{1,0:T(8,128)S(1)}, f32[56,128]{1,0:T(8,128)S(1)}, u32[]{:S(2)}, u32[]{:S(2)}) %collective-permute-start.21) | collective-permute-done | bytes 28704 | tf_op jit(solution)/shard_map/ppermute | solution.py:37
  175.6 2.6 collective-permute-done.23
  184.7 2.2 collective-permute-start.29
  187.8 11.7 %custom-call.22 = f32[128,128]{1,0:T(8,128)S(1)} custom-call(f32[128,128]{1,0:T(8,128)S(1)} %fusion.71), custom_call_target="Cholesky" | custom-call | tf_op jit(solution)/shard_map/cholesky/custom-call.1 | solution.py:69
  200.8 9.8 %custom-call.23 = f32[1,128,128]{1,2,0:T(8,128)S(1)} custom-call(f32[1,128,128]{2,1,0:T(8,128)S(1)} %fusion.52), custom_call_target="InvertDiagBlocksLowerTriangular" | custom-call | tf_op jit(solution)/shard_map/triangular_solve/custom-call.0 | solution.py:70
  213.2 11.9 %custom-call.24 = f32[128,128]{1,0:T(8,128)S(1)} custom-call(f32[128,128]{1,0:T(8,128)S(1)} %convolution_subtract_fusion.9), custom_call_target="Cholesky" | custom-call | tf_op jit(solution)/shard_map/cholesky/custom-call.1 | solution.py:69
  226.4 9.8 %custom-call.25 = f32[1,128,128]{1,2,0:T(8,128)S(1)} custom-call(f32[1,128,128]{2,1,0:T(8,128)S(1)} %fusion.53), custom_call_target="InvertDiagBlocksLowerTriangular" | custom-call | tf_op jit(solution)/shard_map/triangular_solve/custom-call.0 | solution.py:70
  237.1 11.7 %custom-call.26 = f32[128,128]{1,0:T(8,128)S(1)} custom-call(f32[128,128]{1,0:T(8,128)S(1)} %convolution_subtract_fusion.5), custom_call_target="Cholesky" | custom-call | tf_op jit(solution)/shard_map/cholesky/custom-call.1 | solution.py:69
  250.2 9.8 %custom-call.27 = f32[1,128,128]{1,2,0:T(8,128)S(1)} custom-call(f32[1,128,128]{2,1,0:T(8,128)S(1)} %fusion.54), custom_call_target="InvertDiagBlocksLowerTriangular" | custom-call | tf_op jit(solution)/shard_map/triangular_solve/custom-call.0 | solution.py:70
  262.8 4.0 %collective-permute-done.30 = f32[24,640]{1,0:T(8,128)S(1)} collective-permute-done((f32[24,640]{1,0:T(8,128)S(1)}, f32[24,640]{1,0:T(8,128)S(1)}, u32[]{:S(2)}, u32[]{:S(2)}) %collective-permute-start.30) | collective-permute-done | bytes 61472 | tf_op jit(solution)/shard_map/ppermute | solution.py:43
  268.9 2.9 %collective-permute-done.31 = f32[48,640]{1,0:T(8,128)S(1)} collective-permute-done((f32[48,640]{1,0:T(8,128)S(1)}, f32[48,640]{1,0:T(8,128)S(1)}, u32[]{:S(2)}, u32[]{:S(2)}) %collective-permute-start.31) | collective-permute-done | bytes 122912 | tf_op jit(solution)/shard_map/ppermute | solution.py:43
  273.8 4.3 %collective-permute-done.32 = f32[96,640]{1,0:T(8,128)S(1)} collective-permute-done((f32[96,640]{1,0:T(8,128)S(1)}, f32[96,640]{1,0:T(8,128)S(1)}, u32[]{:S(2)}, u32[]{:S(2)}) %collective-permute-start.32) | collective-permute-done | bytes 245792 | tf_op jit(solution)/shard_map/ppermute | solution.py:43
  (242 shorter events, 85.1 us)
Async XLA Ops:
  4.0 7.9 %collective-permute-start = (f32[128,384]{1,0:T(8,128)S(1)}, f32[128,384]{1,0:T(8,128)S(1)}, u32[]{:S(2)}, u32[]{:S(2)}) collective-permute-start(f32[128,384]{1,0:T(8,128)S(1)} %bitcast_select_fusion), channel_id=1, source_target_pairs={{0,16},{16,0},{1,17},{17,1},{2,18},{18,2},{3,19},{19,3},{4,20},{20... | collective-permute-start | bytes 589832 | tf_op jit(solution)/shard_map/ppermute | solution.py:56
  14.6 5.3 %collective-permute-start.2 = (f32[224,128]{1,0:T(8,128)S(1)}, f32[224,128]{1,0:T(8,128)S(1)}, u32[]{:S(2)}, u32[]{:S(2)}) collective-permute-start(f32[224,128]{1,0:T(8,128)S(1)} %constant_dynamic-slice_fusion.14), channel_id=1, source_target_pairs={{0,2},{1,3},{2,0},{3,1},{4,6},{5,7},{6,4},{7,5},{8,10},{9,11},{10,... | collective-permute-start | bytes 344072 | tf_op jit(solution)/shard_map/ppermute | solution.py:37
  19.9 4.2 %collective-permute-start.3 = (f32[112,128]{1,0:T(8,128)S(1)}, f32[112,128]{1,0:T(8,128)S(1)}, u32[]{:S(2)}, u32[]{:S(2)}) collective-permute-start(f32[112,128]{1,0:T(8,128)S(1)} %constant_dynamic-slice_fusion.13), channel_id=1, source_target_pairs={{0,4},{1,5},{2,6},{3,7},{4,0},{5,1},{6,2},{7,3},{8,12},{9,13},{10,... | collective-permute-start | bytes 172040 | tf_op jit(solution)/shard_map/ppermute | solution.py:37
  21.8 10.1 %collective-permute-start.9 = (f32[192,640]{1,0:T(8,128)S(1)}, f32[192,640]{1,0:T(8,128)S(1)}, u32[]{:S(2)}, u32[]{:S(2)}) collective-permute-start(f32[192,640]{1,0:T(8,128)S(1)} %constant_dynamic-slice_fusion.11), channel_id=1, source_target_pairs={{0,1},{1,0},{2,3},{3,2},{4,5},{5,4},{6,7},{7,6},{8,9},{9,8},{10,11... | collective-permute-start | bytes 1474568 | tf_op jit(solution)/shard_map/ppermute | solution.py:37
  24.2 4.8 %collective-permute-start.4 = (f32[56,128]{1,0:T(8,128)S(1)}, f32[56,128]{1,0:T(8,128)S(1)}, u32[]{:S(2)}, u32[]{:S(2)}) collective-permute-start(f32[56,128]{1,0:T(8,128)S(1)} %constant_dynamic-slice_fusion.12), channel_id=1, source_target_pairs={{0,8},{1,9},{2,10},{3,11},{4,12},{5,13},{6,14},{7,15},{8,0},{9,1},... | collective-permute-start | bytes 86024 | tf_op jit(solution)/shard_map/ppermute | solution.py:37
  29.0 4.8 %collective-permute-start.5 = (f32[56,128]{1,0:T(8,128)S(1)}, f32[56,128]{1,0:T(8,128)S(1)}, u32[]{:S(2)}, u32[]{:S(2)}) collective-permute-start(f32[56,128]{1,0:T(8,128)S(1)} %dynamic-slice_add_fusion.15), channel_id=1, source_target_pairs={{0,8},{1,9},{2,10},{3,11},{4,12},{5,13},{6,14},{7,15},{8,0},{9,1},... | collective-permute-start | bytes 86024 | tf_op jit(solution)/shard_map/ppermute | solution.py:43
  32.0 8.4 %collective-permute-start.10 = (f32[96,640]{1,0:T(8,128)S(1)}, f32[96,640]{1,0:T(8,128)S(1)}, u32[]{:S(2)}, u32[]{:S(2)}) collective-permute-start(f32[96,640]{1,0:T(8,128)S(1)} %constant_dynamic-slice_fusion.10), channel_id=1, source_target_pairs={{0,2},{1,3},{2,0},{3,1},{4,6},{5,7},{6,4},{7,5},{8,10},{9,11},{10,... | collective-permute-start | bytes 737288 | tf_op jit(solution)/shard_map/ppermute | solution.py:37
  33.8 5.0 %collective-permute-start.6 = (f32[112,128]{1,0:T(8,128)S(1)}, f32[112,128]{1,0:T(8,128)S(1)}, u32[]{:S(2)}, u32[]{:S(2)}) collective-permute-start(f32[112,128]{1,0:T(8,128)S(1)} %maximum_select_fusion.14), channel_id=1, source_target_pairs={{0,4},{1,5},{2,6},{3,7},{4,0},{5,1},{6,2},{7,3},{8,12},{9,13},{10,... | collective-permute-start | bytes 172040 | tf_op jit(solution)/shard_map/ppermute | solution.py:43
  38.8 4.9 %collective-permute-start.7 = (f32[224,128]{1,0:T(8,128)S(1)}, f32[224,128]{1,0:T(8,128)S(1)}, u32[]{:S(2)}, u32[]{:S(2)}) collective-permute-start(f32[224,128]{1,0:T(8,128)S(1)} %maximum_select_fusion.12), channel_id=1, source_target_pairs={{0,2},{1,3},{2,0},{3,1},{4,6},{5,7},{6,4},{7,5},{8,10},{9,11},{10,... | collective-permute-start | bytes 344072 | tf_op jit(solution)/shard_map/ppermute | solution.py:43
  40.4 4.9 %collective-permute-start.11 = (f32[48,640]{1,0:T(8,128)S(1)}, f32[48,640]{1,0:T(8,128)S(1)}, u32[]{:S(2)}, u32[]{:S(2)}) collective-permute-start(f32[48,640]{1,0:T(8,128)S(1)} %constant_dynamic-slice_fusion.9), channel_id=1, source_target_pairs={{0,4},{1,5},{2,6},{3,7},{4,0},{5,1},{6,2},{7,3},{8,12},{9,13},{10,... | collective-permute-start | bytes 368648 | tf_op jit(solution)/shard_map/ppermute | solution.py:37
  43.7 4.2 %collective-permute-start.8 = (f32[448,128]{1,0:T(8,128)S(1)}, f32[448,128]{1,0:T(8,128)S(1)}, u32[]{:S(2)}, u32[]{:S(2)}) collective-permute-start(f32[448,128]{1,0:T(8,128)S(1)} %maximum_select_fusion.8), channel_id=1, source_target_pairs={{0,1},{1,0},{2,3},{3,2},{4,5},{5,4},{6,7},{7,6},{8,9},{9,8},{10,11... | collective-permute-start | bytes 688136 | tf_op jit(solution)/shard_map/ppermute | solution.py:43
  45.4 77.1 %collective-permute-start.12 = (f32[24,640]{1,0:T(8,128)S(1)}, f32[24,640]{1,0:T(8,128)S(1)}, u32[]{:S(2)}, u32[]{:S(2)}) collective-permute-start(f32[24,640]{1,0:T(8,128)S(1)} %constant_dynamic-slice_fusion.8), channel_id=1, source_target_pairs={{0,8},{1,9},{2,10},{3,11},{4,12},{5,13},{6,14},{7,15},{8,0},{9,1},... | collective-permute-start | bytes 184328 | tf_op jit(solution)/shard_map/ppermute | solution.py:37
  122.5 5.2 %collective-permute-start.13 = (f32[24,640]{1,0:T(8,128)S(1)}, f32[24,640]{1,0:T(8,128)S(1)}, u32[]{:S(2)}, u32[]{:S(2)}) collective-permute-start(f32[24,640]{1,0:T(8,128)S(1)} %dynamic-slice_add_fusion.11), channel_id=1, source_target_pairs={{0,8},{1,9},{2,10},{3,11},{4,12},{5,13},{6,14},{7,15},{8,0},{9,1},... | collective-permute-start | bytes 184328 | tf_op jit(solution)/shard_map/ppermute | solution.py:43
  127.7 4.9 %collective-permute-start.14 = (f32[48,640]{1,0:T(8,128)S(1)}, f32[48,640]{1,0:T(8,128)S(1)}, u32[]{:S(2)}, u32[]{:S(2)}) collective-permute-start(f32[48,640]{1,0:T(8,128)S(1)} %maximum_select_fusion.10), channel_id=1, source_target_pairs={{0,4},{1,5},{2,6},{3,7},{4,0},{5,1},{6,2},{7,3},{8,12},{9,13},{10,... | collective-permute-start | bytes 368648 | tf_op jit(solution)/shard_map/ppermute | solution.py:43
  132.7 6.3 %collective-permute-start.15 = (f32[96,640]{1,0:T(8,128)S(1)}, f32[96,640]{1,0:T(8,128)S(1)}, u32[]{:S(2)}, u32[]{:S(2)}) collective-permute-start(f32[96,640]{1,0:T(8,128)S(1)} %maximum_select_fusion.6), channel_id=1, source_target_pairs={{0,2},{1,3},{2,0},{3,1},{4,6},{5,7},{6,4},{7,5},{8,10},{9,11},{10,... | collective-permute-start | bytes 737288 | tf_op jit(solution)/shard_map/ppermute | solution.py:43
  139.0 1.9 collective-permute-start.16
  145.1 7.0 %collective-permute-start.17 = (f32[128,384]{1,0:T(8,128)S(1)}, f32[128,384]{1,0:T(8,128)S(1)}, u32[]{:S(2)}, u32[]{:S(2)}) collective-permute-start(f32[128,384]{1,0:T(8,128)S(1)} %fusion), channel_id=1, source_target_pairs={{0,16},{16,0},{1,17},{17,1},{2,18},{18,2},{3,19},{19,3},{4,20},{20... | collective-permute-start | bytes 589832 | tf_op jit(solution)/shard_map/ppermute | solution.py:56
  154.7 5.3 %collective-permute-start.19 = (f32[224,128]{1,0:T(8,128)S(1)}, f32[224,128]{1,0:T(8,128)S(1)}, u32[]{:S(2)}, u32[]{:S(2)}) collective-permute-start(f32[224,128]{1,0:T(8,128)S(1)} %constant_dynamic-slice_fusion.6), channel_id=1, source_target_pairs={{0,2},{1,3},{2,0},{3,1},{4,6},{5,7},{6,4},{7,5},{8,10},{9,11},{10,... | collective-permute-start | bytes 344072 | tf_op jit(solution)/shard_map/ppermute | solution.py:37
  160.0 4.2 %collective-permute-start.20 = (f32[112,128]{1,0:T(8,128)S(1)}, f32[112,128]{1,0:T(8,128)S(1)}, u32[]{:S(2)}, u32[]{:S(2)}) collective-permute-start(f32[112,128]{1,0:T(8,128)S(1)} %constant_dynamic-slice_fusion.5), channel_id=1, source_target_pairs={{0,4},{1,5},{2,6},{3,7},{4,0},{5,1},{6,2},{7,3},{8,12},{9,13},{10,... | collective-permute-start | bytes 172040 | tf_op jit(solution)/shard_map/ppermute | solution.py:37
  161.6 9.3 %collective-permute-start.26 = (f32[192,640]{1,0:T(8,128)S(1)}, f32[192,640]{1,0:T(8,128)S(1)}, u32[]{:S(2)}, u32[]{:S(2)}) collective-permute-start(f32[192,640]{1,0:T(8,128)S(1)} %constant_dynamic-slice_fusion.3), channel_id=1, source_target_pairs={{0,1},{1,0},{2,3},{3,2},{4,5},{5,4},{6,7},{7,6},{8,9},{9,8},{10,11... | collective-permute-start | bytes 1474568 | tf_op jit(solution)/shard_map/ppermute | solution.py:37
  164.3 4.8 %collective-permute-start.21 = (f32[56,128]{1,0:T(8,128)S(1)}, f32[56,128]{1,0:T(8,128)S(1)}, u32[]{:S(2)}, u32[]{:S(2)}) collective-permute-start(f32[56,128]{1,0:T(8,128)S(1)} %constant_dynamic-slice_fusion.4), channel_id=1, source_target_pairs={{0,8},{1,9},{2,10},{3,11},{4,12},{5,13},{6,14},{7,15},{8,0},{9,1},... | collective-permute-start | bytes 86024 | tf_op jit(solution)/shard_map/ppermute | solution.py:37
  169.1 4.8 %collective-permute-start.22 = (f32[56,128]{1,0:T(8,128)S(1)}, f32[56,128]{1,0:T(8,128)S(1)}, u32[]{:S(2)}, u32[]{:S(2)}) collective-permute-start(f32[56,128]{1,0:T(8,128)S(1)} %dynamic-slice_add_fusion.14), channel_id=1, source_target_pairs={{0,8},{1,9},{2,10},{3,11},{4,12},{5,13},{6,14},{7,15},{8,0},{9,1},... | collective-permute-start | bytes 86024 | tf_op jit(solution)/shard_map/ppermute | solution.py:43
  171.0 8.7 %collective-permute-start.27 = (f32[96,640]{1,0:T(8,128)S(1)}, f32[96,640]{1,0:T(8,128)S(1)}, u32[]{:S(2)}, u32[]{:S(2)}) collective-permute-start(f32[96,640]{1,0:T(8,128)S(1)} %constant_dynamic-slice_fusion.2), channel_id=1, source_target_pairs={{0,2},{1,3},{2,0},{3,1},{4,6},{5,7},{6,4},{7,5},{8,10},{9,11},{10,... | collective-permute-start | bytes 737288 | tf_op jit(solution)/shard_map/ppermute | solution.py:37
  173.9 4.3 %collective-permute-start.23 = (f32[112,128]{1,0:T(8,128)S(1)}, f32[112,128]{1,0:T(8,128)S(1)}, u32[]{:S(2)}, u32[]{:S(2)}) collective-permute-start(f32[112,128]{1,0:T(8,128)S(1)} %maximum_select_fusion.15), channel_id=1, source_target_pairs={{0,4},{1,5},{2,6},{3,7},{4,0},{5,1},{6,2},{7,3},{8,12},{9,13},{10,... | collective-permute-start | bytes 172040 | tf_op jit(solution)/shard_map/ppermute | solution.py:43
  178.2 4.9 %collective-permute-start.24 = (f32[224,128]{1,0:T(8,128)S(1)}, f32[224,128]{1,0:T(8,128)S(1)}, u32[]{:S(2)}, u32[]{:S(2)}) collective-permute-start(f32[224,128]{1,0:T(8,128)S(1)} %maximum_select_fusion.13), channel_id=1, source_target_pairs={{0,2},{1,3},{2,0},{3,1},{4,6},{5,7},{6,4},{7,5},{8,10},{9,11},{10,... | collective-permute-start | bytes 344072 | tf_op jit(solution)/shard_map/ppermute | solution.py:43
  179.7 4.9 %collective-permute-start.28 = (f32[48,640]{1,0:T(8,128)S(1)}, f32[48,640]{1,0:T(8,128)S(1)}, u32[]{:S(2)}, u32[]{:S(2)}) collective-permute-start(f32[48,640]{1,0:T(8,128)S(1)} %constant_dynamic-slice_fusion.1), channel_id=1, source_target_pairs={{0,4},{1,5},{2,6},{3,7},{4,0},{5,1},{6,2},{7,3},{8,12},{9,13},{10,... | collective-permute-start | bytes 368648 | tf_op jit(solution)/shard_map/ppermute | solution.py:37
  183.1 3.9 %collective-permute-start.25 = (f32[448,128]{1,0:T(8,128)S(1)}, f32[448,128]{1,0:T(8,128)S(1)}, u32[]{:S(2)}, u32[]{:S(2)}) collective-permute-start(f32[448,128]{1,0:T(8,128)S(1)} %maximum_select_fusion.9), channel_id=1, source_target_pairs={{0,1},{1,0},{2,3},{3,2},{4,5},{5,4},{6,7},{7,6},{8,9},{9,8},{10,11... | collective-permute-start | bytes 688136 | tf_op jit(solution)/shard_map/ppermute | solution.py:43
  184.7 76.9 %collective-permute-start.29 = (f32[24,640]{1,0:T(8,128)S(1)}, f32[24,640]{1,0:T(8,128)S(1)}, u32[]{:S(2)}, u32[]{:S(2)}) collective-permute-start(f32[24,640]{1,0:T(8,128)S(1)} %constant_dynamic-slice_fusion), channel_id=1, source_target_pairs={{0,8},{1,9},{2,10},{3,11},{4,12},{5,13},{6,14},{7,15},{8,0},{9,1},... | collective-permute-start | bytes 184328 | tf_op jit(solution)/shard_map/ppermute | solution.py:37
  261.7 5.2 %collective-permute-start.30 = (f32[24,640]{1,0:T(8,128)S(1)}, f32[24,640]{1,0:T(8,128)S(1)}, u32[]{:S(2)}, u32[]{:S(2)}) collective-permute-start(f32[24,640]{1,0:T(8,128)S(1)} %dynamic-slice_add_fusion.10), channel_id=1, source_target_pairs={{0,8},{1,9},{2,10},{3,11},{4,12},{5,13},{6,14},{7,15},{8,0},{9,1},... | collective-permute-start | bytes 184328 | tf_op jit(solution)/shard_map/ppermute | solution.py:43
  266.9 4.9 %collective-permute-start.31 = (f32[48,640]{1,0:T(8,128)S(1)}, f32[48,640]{1,0:T(8,128)S(1)}, u32[]{:S(2)}, u32[]{:S(2)}) collective-permute-start(f32[48,640]{1,0:T(8,128)S(1)} %maximum_select_fusion.11), channel_id=1, source_target_pairs={{0,4},{1,5},{2,6},{3,7},{4,0},{5,1},{6,2},{7,3},{8,12},{9,13},{10,... | collective-permute-start | bytes 368648 | tf_op jit(solution)/shard_map/ppermute | solution.py:43
  271.8 6.3 %collective-permute-start.32 = (f32[96,640]{1,0:T(8,128)S(1)}, f32[96,640]{1,0:T(8,128)S(1)}, u32[]{:S(2)}, u32[]{:S(2)}) collective-permute-start(f32[96,640]{1,0:T(8,128)S(1)} %maximum_select_fusion.7), channel_id=1, source_target_pairs={{0,2},{1,3},{2,0},{3,1},{4,6},{5,7},{6,4},{7,5},{8,10},{9,11},{10,... | collective-permute-start | bytes 737288 | tf_op jit(solution)/shard_map/ppermute | solution.py:43
  278.1 1.9 collective-permute-start.33
  (7 other events, 14.7 us)

commit v8 on v6

--- a/solution.py
+++ b/solution.py
@@ -118,7 +118,6 @@
     packed = tree_sum(packed, "member")
     gram_blocks = packed[: len(pairs) * size]
     slots = packed[len(pairs) * size:].reshape(n_member, width)[:, : obs + n_rows]
-    cross_loc, gram_blocks, slots = lax.optimization_barrier((cross_loc, gram_blocks, slots))
     cross_sum = tree_sum(cross_loc, "member")
 
     means = jnp.mean(slots, axis=0)
@@ -152,8 +151,11 @@
         gain, cross = analyse(current, observed, obs_values[block], noise_var[block])
         if block + 1 < num_blocks:
             rows = obs_rows[block + 1]
-            cands = jnp.take(current, rows, axis=1) + full_dot(gain.T, jnp.take(cross, rows, axis=1))
-        current = current + full_dot(gain.T, cross)
+            picked = jnp.take(current, rows, axis=1)
+        step = full_dot(gain.T, cross)
+        if block + 1 < num_blocks:
+            cands = picked + jnp.take(step, rows, axis=1)
+        current = current + step
     return current
 
 

time: 308 us -> 283 us (0.919)
  waiting for transfers between devices: 77.8 us -> 63.9 us
  starting transfers between devices: 50.6 us -> 45.6 us
    ppermute x16, waiting for transfers between devices: 31.8 us -> 20.9 us  [tree_sum(): cur = keep + lax.ppermute(away, axis, perm)]
    ppermute x16, starting transfers between devices: 22.5 us -> 18.5 us  [tree_sum(): other = lax.ppermute(cur, axis, perm)]
    dot_general x29 -> x28, matrix products: 11.2 us -> 9.07 us  [full_dot(): jnp.dot(left, right, precision=lax.Precision.HIGHEST, preferred_element_t...]
  transfers between devices with their start and end apart: 34 -> 34, of which waited for: 29 -> 26; matrix products, arithmetic and copies ran while one was open for 36% -> 56% of each run, Pallas kernels for 0% -> 0%
where the time goes in v8:
time: 283 us; the launch traced here: 280 us
  other arithmetic  140 us (49%)
  waiting for transfers between devices  63.9 us (23%)
  starting transfers between devices  45.6 us (16%)
  matrix products  21.1 us (7%)
  local copies, waits for them, and re-layouts  7.87 us (3%)
    another operation x18, other arithmetic, block_solve(): diag = lax.linalg.cholesky(blk[k][k], symmetrize_input=False)  74.5 us
    another operation x12, other arithmetic, block_solve(): inv[k] = lax.linalg.triangular_solve(diag, eye, left_side=True, lower=True)  63.2 us
    ppermute x16, waiting for transfers between devices, tree_sum(): other = lax.ppermute(cur, axis, perm)  32.6 us
    ppermute x16, starting transfers between devices, tree_sum(): cur = keep + lax.ppermute(away, axis, perm)  22.5 us
    ppermute x16, waiting for transfers between devices, tree_sum(): cur = keep + lax.ppermute(away, axis, perm)  20.9 us
    ppermute x16, starting transfers between devices, tree_sum(): other = lax.ppermute(cur, axis, perm)  18.5 us
    ppermute x2, waiting for transfers between devices, tree_sum_exact(): x = x + lax.ppermute(x, axis, perm)  10.4 us
    dot_general x20, matrix products, tdot(): lax.dot_general(left, right, (((0,), (0,)), ((), ())), precision=lax.Prec...  10.3 us
  transfers between devices with their start and end apart: 34, of which 26 were waited for; matrix products, arithmetic and copies ran while one was open for 56% of the time, Pallas kernels for 0%

profile of v8, /device:TPU:0, one launch (start us, length us, event | category | flops | bytes accessed | tf_op | source)
XLA Modules:
  0.0 279.6 jit_solution(12944499876689189765)
XLA Ops:
  4.0 3.0 %collective-permute-start = (f32[128,384]{0,1:T(8,128)S(1)}, f32[128,384]{0,1:T(8,128)S(1)}, u32[]{:S(2)}, u32[]{:S(2)}) collective-permute-start(f32[128,384]{0,1:T(8,128)S(1)} %bitcast_select_fusion), channel_id=1, source_target_pairs={{0,16},{16,0},{1,17},{17,1},{2,18},{18,2},{3,19},{19,3},{4,20},{20... | collective-permute-start | bytes 589832 | tf_op jit(solution)/shard_map/ppermute | solution.py:56
  7.1 4.8 %collective-permute-done = f32[128,384]{0,1:T(8,128)S(1)} collective-permute-done((f32[128,384]{0,1:T(8,128)S(1)}, f32[128,384]{0,1:T(8,128)S(1)}, u32[]{:S(2)}, u32[]{:S(2)}) %collective-permute-start) | collective-permute-done | bytes 196640 | tf_op jit(solution)/shard_map/ppermute | solution.py:56
  17.7 2.5 collective-permute-done.2
  22.2 2.3 collective-permute-done.3
  24.5 2.9 %collective-permute-start.4 = (f32[56,128]{1,0:T(8,128)S(1)}, f32[56,128]{1,0:T(8,128)S(1)}, u32[]{:S(2)}, u32[]{:S(2)}) collective-permute-start(f32[56,128]{1,0:T(8,128)S(1)} %constant_dynamic-slice_fusion.12), channel_id=1, source_target_pairs={{0,8},{1,9},{2,10},{3,11},{4,12},{5,13},{6,14},{7,15},{8,0},{9,1},... | collective-permute-start | bytes 86024 | tf_op jit(solution)/shard_map/ppermute | solution.py:37
  29.3 2.8 %collective-permute-start.5 = (f32[56,128]{1,0:T(8,128)S(1)}, f32[56,128]{1,0:T(8,128)S(1)}, u32[]{:S(2)}, u32[]{:S(2)}) collective-permute-start(f32[56,128]{1,0:T(8,128)S(1)} %dynamic-slice_add_fusion.15), channel_id=1, source_target_pairs={{0,8},{1,9},{2,10},{3,11},{4,12},{5,13},{6,14},{7,15},{8,0},{9,1},... | collective-permute-start | bytes 86024 | tf_op jit(solution)/shard_map/ppermute | solution.py:43
  34.1 2.2 collective-permute-start.6
  36.3 2.7 collective-permute-done.6
  45.6 2.5 collective-permute-start.12
  49.0 11.7 %custom-call.16 = f32[128,128]{1,0:T(8,128)S(1)} custom-call(f32[128,128]{1,0:T(8,128)S(1)} %fusion.99), custom_call_target="Cholesky" | custom-call | tf_op jit(solution)/shard_map/cholesky/custom-call.1 | solution.py:69
  62.0 9.8 %custom-call.17 = f32[1,128,128]{1,2,0:T(8,128)S(1)} custom-call(f32[1,128,128]{2,1,0:T(8,128)S(1)} %fusion.60), custom_call_target="InvertDiagBlocksLowerTriangular" | custom-call | tf_op jit(solution)/shard_map/triangular_solve/custom-call.0 | solution.py:70
  74.3 11.7 %custom-call.18 = f32[128,128]{1,0:T(8,128)S(1)} custom-call(f32[128,128]{1,0:T(8,128)S(1)} %convolution_subtract_fusion.19), custom_call_target="Cholesky" | custom-call | tf_op jit(solution)/shard_map/cholesky/custom-call.1 | solution.py:69
  87.3 10.2 %custom-call.19 = f32[1,128,128]{1,2,0:T(8,128)S(1)} custom-call(f32[1,128,128]{2,1,0:T(8,128)S(1)} %fusion.61), custom_call_target="InvertDiagBlocksLowerTriangular" | custom-call | tf_op jit(solution)/shard_map/triangular_solve/custom-call.0 | solution.py:70
  98.4 11.7 %custom-call.20 = f32[128,128]{1,0:T(8,128)S(1)} custom-call(f32[128,128]{1,0:T(8,128)S(1)} %convolution_subtract_fusion.15), custom_call_target="Cholesky" | custom-call | tf_op jit(solution)/shard_map/cholesky/custom-call.1 | solution.py:69
  111.4 9.8 %custom-call.21 = f32[1,128,128]{1,2,0:T(8,128)S(1)} custom-call(f32[1,128,128]{2,1,0:T(8,128)S(1)} %fusion.62), custom_call_target="InvertDiagBlocksLowerTriangular" | custom-call | tf_op jit(solution)/shard_map/triangular_solve/custom-call.0 | solution.py:70
  123.1 4.3 %collective-permute-done.13 = f32[24,640]{1,0:T(8,128)S(1)} collective-permute-done((f32[24,640]{1,0:T(8,128)S(1)}, f32[24,640]{1,0:T(8,128)S(1)}, u32[]{:S(2)}, u32[]{:S(2)}) %collective-permute-start.13) | collective-permute-done | bytes 61472 | tf_op jit(solution)/shard_map/ppermute | solution.py:43
  129.3 3.1 %collective-permute-done.14 = f32[48,640]{1,0:T(8,128)S(1)} collective-permute-done((f32[48,640]{1,0:T(8,128)S(1)}, f32[48,640]{1,0:T(8,128)S(1)}, u32[]{:S(2)}, u32[]{:S(2)}) %collective-permute-start.14) | collective-permute-done | bytes 122912 | tf_op jit(solution)/shard_map/ppermute | solution.py:43
  133.9 4.8 %collective-permute-done.15 = f32[96,640]{1,0:T(8,128)S(1)} collective-permute-done((f32[96,640]{1,0:T(8,128)S(1)}, f32[96,640]{1,0:T(8,128)S(1)}, u32[]{:S(2)}, u32[]{:S(2)}) %collective-permute-start.15) | collective-permute-done | bytes 245792 | tf_op jit(solution)/shard_map/ppermute | solution.py:43
  144.8 5.6 %collective-permute-done.17 = f32[128,384]{0,1:T(8,128)S(1)} collective-permute-done((f32[128,384]{0,1:T(8,128)S(1)}, f32[128,384]{0,1:T(8,128)S(1)}, u32[]{:S(2)}, u32[]{:S(2)}) %collective-permute-start.17) | collective-permute-done | bytes 196640 | tf_op jit(solution)/shard_map/ppermute | solution.py:56
  155.1 3.4 %collective-permute-done.19 = f32[224,128]{1,0:T(8,128)S(1)} collective-permute-done((f32[224,128]{1,0:T(8,128)S(1)}, f32[224,128]{1,0:T(8,128)S(1)}, u32[]{:S(2)}, u32[]{:S(2)}) %collective-permute-start.19) | collective-permute-done | bytes 114720 | tf_op jit(solution)/shard_map/ppermute | solution.py:37
  160.1 2.6 collective-permute-done.20
  164.5 3.1 %collective-permute-done.21 = f32[56,128]{1,0:T(8,128)S(1)} collective-permute-done((f32[56,128]{1,0:T(8,128)S(1)}, f32[56,128]{1,0:T(8,128)S(1)}, u32[]{:S(2)}, u32[]{:S(2)}) %collective-permute-start.21) | collective-permute-done | bytes 28704 | tf_op jit(solution)/shard_map/ppermute | solution.py:37
  174.0 2.6 collective-permute-done.23
  186.2 11.7 %custom-call.22 = f32[128,128]{1,0:T(8,128)S(1)} custom-call(f32[128,128]{1,0:T(8,128)S(1)} %fusion.82), custom_call_target="Cholesky" | custom-call | tf_op jit(solution)/shard_map/cholesky/custom-call.1 | solution.py:69
  199.3 9.8 %custom-call.23 = f32[1,128,128]{1,2,0:T(8,128)S(1)} custom-call(f32[1,128,128]{2,1,0:T(8,128)S(1)} %fusion.63), custom_call_target="InvertDiagBlocksLowerTriangular" | custom-call | tf_op jit(solution)/shard_map/triangular_solve/custom-call.0 | solution.py:70
  211.5 11.9 %custom-call.24 = f32[128,128]{1,0:T(8,128)S(1)} custom-call(f32[128,128]{1,0:T(8,128)S(1)} %convolution_subtract_fusion.9), custom_call_target="Cholesky" | custom-call | tf_op jit(solution)/shard_map/cholesky/custom-call.1 | solution.py:69
  224.8 9.8 %custom-call.25 = f32[1,128,128]{1,2,0:T(8,128)S(1)} custom-call(f32[1,128,128]{2,1,0:T(8,128)S(1)} %fusion.64), custom_call_target="InvertDiagBlocksLowerTriangular" | custom-call | tf_op jit(solution)/shard_map/triangular_solve/custom-call.0 | solution.py:70
  235.4 11.7 %custom-call.26 = f32[128,128]{1,0:T(8,128)S(1)} custom-call(f32[128,128]{1,0:T(8,128)S(1)} %convolution_subtract_fusion.5), custom_call_target="Cholesky" | custom-call | tf_op jit(solution)/shard_map/cholesky/custom-call.1 | solution.py:69
  248.5 9.8 %custom-call.27 = f32[1,128,128]{1,2,0:T(8,128)S(1)} custom-call(f32[1,128,128]{2,1,0:T(8,128)S(1)} %fusion.65), custom_call_target="InvertDiagBlocksLowerTriangular" | custom-call | tf_op jit(solution)/shard_map/triangular_solve/custom-call.0 | solution.py:70
  260.7 3.8 %collective-permute-done.30 = f32[24,640]{1,0:T(8,128)S(1)} collective-permute-done((f32[24,640]{1,0:T(8,128)S(1)}, f32[24,640]{1,0:T(8,128)S(1)}, u32[]{:S(2)}, u32[]{:S(2)}) %collective-permute-start.30) | collective-permute-done | bytes 61472 | tf_op jit(solution)/shard_map/ppermute | solution.py:43
  266.5 2.9 %collective-permute-done.31 = f32[48,640]{1,0:T(8,128)S(1)} collective-permute-done((f32[48,640]{1,0:T(8,128)S(1)}, f32[48,640]{1,0:T(8,128)S(1)}, u32[]{:S(2)}, u32[]{:S(2)}) %collective-permute-start.31) | collective-permute-done | bytes 122912 | tf_op jit(solution)/shard_map/ppermute | solution.py:43
  271.0 4.7 %collective-permute-done.32 = f32[96,640]{1,0:T(8,128)S(1)} collective-permute-done((f32[96,640]{1,0:T(8,128)S(1)}, f32[96,640]{1,0:T(8,128)S(1)}, u32[]{:S(2)}, u32[]{:S(2)}) %collective-permute-start.32) | collective-permute-done | bytes 245792 | tf_op jit(solution)/shard_map/ppermute | solution.py:43
  (236 shorter events, 81.9 us)
Async XLA Ops:
  4.0 7.9 %collective-permute-start = (f32[128,384]{0,1:T(8,128)S(1)}, f32[128,384]{0,1:T(8,128)S(1)}, u32[]{:S(2)}, u32[]{:S(2)}) collective-permute-start(f32[128,384]{0,1:T(8,128)S(1)} %bitcast_select_fusion), channel_id=1, source_target_pairs={{0,16},{16,0},{1,17},{17,1},{2,18},{18,2},{3,19},{19,3},{4,20},{20... | collective-permute-start | bytes 589832 | tf_op jit(solution)/shard_map/ppermute | solution.py:56
  14.9 5.3 %collective-permute-start.2 = (f32[224,128]{1,0:T(8,128)S(1)}, f32[224,128]{1,0:T(8,128)S(1)}, u32[]{:S(2)}, u32[]{:S(2)}) collective-permute-start(f32[224,128]{1,0:T(8,128)S(1)} %constant_dynamic-slice_fusion.14), channel_id=1, source_target_pairs={{0,2},{1,3},{2,0},{3,1},{4,6},{5,7},{6,4},{7,5},{8,10},{9,11},{10,... | collective-permute-start | bytes 344072 | tf_op jit(solution)/shard_map/ppermute | solution.py:37
  20.2 4.2 %collective-permute-start.3 = (f32[112,128]{1,0:T(8,128)S(1)}, f32[112,128]{1,0:T(8,128)S(1)}, u32[]{:S(2)}, u32[]{:S(2)}) collective-permute-start(f32[112,128]{1,0:T(8,128)S(1)} %constant_dynamic-slice_fusion.13), channel_id=1, source_target_pairs={{0,4},{1,5},{2,6},{3,7},{4,0},{5,1},{6,2},{7,3},{8,12},{9,13},{10,... | collective-permute-start | bytes 172040 | tf_op jit(solution)/shard_map/ppermute | solution.py:37
  22.1 10.0 %collective-permute-start.9 = (f32[192,640]{1,0:T(8,128)S(1)}, f32[192,640]{1,0:T(8,128)S(1)}, u32[]{:S(2)}, u32[]{:S(2)}) collective-permute-start(f32[192,640]{1,0:T(8,128)S(1)} %constant_dynamic-slice_fusion.11), channel_id=1, source_target_pairs={{0,1},{1,0},{2,3},{3,2},{4,5},{5,4},{6,7},{7,6},{8,9},{9,8},{10,11... | collective-permute-start | bytes 1474568 | tf_op jit(solution)/shard_map/ppermute | solution.py:37
  24.5 4.8 %collective-permute-start.4 = (f32[56,128]{1,0:T(8,128)S(1)}, f32[56,128]{1,0:T(8,128)S(1)}, u32[]{:S(2)}, u32[]{:S(2)}) collective-permute-start(f32[56,128]{1,0:T(8,128)S(1)} %constant_dynamic-slice_fusion.12), channel_id=1, source_target_pairs={{0,8},{1,9},{2,10},{3,11},{4,12},{5,13},{6,14},{7,15},{8,0},{9,1},... | collective-permute-start | bytes 86024 | tf_op jit(solution)/shard_map/ppermute | solution.py:37
  29.3 4.8 %collective-permute-start.5 = (f32[56,128]{1,0:T(8,128)S(1)}, f32[56,128]{1,0:T(8,128)S(1)}, u32[]{:S(2)}, u32[]{:S(2)}) collective-permute-start(f32[56,128]{1,0:T(8,128)S(1)} %dynamic-slice_add_fusion.15), channel_id=1, source_target_pairs={{0,8},{1,9},{2,10},{3,11},{4,12},{5,13},{6,14},{7,15},{8,0},{9,1},... | collective-permute-start | bytes 86024 | tf_op jit(solution)/shard_map/ppermute | solution.py:43
  32.2 8.4 %collective-permute-start.10 = (f32[96,640]{1,0:T(8,128)S(1)}, f32[96,640]{1,0:T(8,128)S(1)}, u32[]{:S(2)}, u32[]{:S(2)}) collective-permute-start(f32[96,640]{1,0:T(8,128)S(1)} %constant_dynamic-slice_fusion.10), channel_id=1, source_target_pairs={{0,2},{1,3},{2,0},{3,1},{4,6},{5,7},{6,4},{7,5},{8,10},{9,11},{10,... | collective-permute-start | bytes 737288 | tf_op jit(solution)/shard_map/ppermute | solution.py:37
  34.1 5.0 %collective-permute-start.6 = (f32[112,128]{1,0:T(8,128)S(1)}, f32[112,128]{1,0:T(8,128)S(1)}, u32[]{:S(2)}, u32[]{:S(2)}) collective-permute-start(f32[112,128]{1,0:T(8,128)S(1)} %maximum_select_fusion.14), channel_id=1, source_target_pairs={{0,4},{1,5},{2,6},{3,7},{4,0},{5,1},{6,2},{7,3},{8,12},{9,13},{10,... | collective-permute-start | bytes 172040 | tf_op jit(solution)/shard_map/ppermute | solution.py:43
  39.1 4.9 %collective-permute-start.7 = (f32[224,128]{1,0:T(8,128)S(1)}, f32[224,128]{1,0:T(8,128)S(1)}, u32[]{:S(2)}, u32[]{:S(2)}) collective-permute-start(f32[224,128]{1,0:T(8,128)S(1)} %maximum_select_fusion.12), channel_id=1, source_target_pairs={{0,2},{1,3},{2,0},{3,1},{4,6},{5,7},{6,4},{7,5},{8,10},{9,11},{10,... | collective-permute-start | bytes 344072 | tf_op jit(solution)/shard_map/ppermute | solution.py:43
  40.7 4.9 %collective-permute-start.11 = (f32[48,640]{1,0:T(8,128)S(1)}, f32[48,640]{1,0:T(8,128)S(1)}, u32[]{:S(2)}, u32[]{:S(2)}) collective-permute-start(f32[48,640]{1,0:T(8,128)S(1)} %constant_dynamic-slice_fusion.9), channel_id=1, source_target_pairs={{0,4},{1,5},{2,6},{3,7},{4,0},{5,1},{6,2},{7,3},{8,12},{9,13},{10,... | collective-permute-start | bytes 368648 | tf_op jit(solution)/shard_map/ppermute | solution.py:37
  43.9 4.2 %collective-permute-start.8 = (f32[448,128]{1,0:T(8,128)S(1)}, f32[448,128]{1,0:T(8,128)S(1)}, u32[]{:S(2)}, u32[]{:S(2)}) collective-permute-start(f32[448,128]{1,0:T(8,128)S(1)} %maximum_select_fusion.8), channel_id=1, source_target_pairs={{0,1},{1,0},{2,3},{3,2},{4,5},{5,4},{6,7},{7,6},{8,9},{9,8},{10,11... | collective-permute-start | bytes 688136 | tf_op jit(solution)/shard_map/ppermute | solution.py:43
  45.6 76.5 %collective-permute-start.12 = (f32[24,640]{1,0:T(8,128)S(1)}, f32[24,640]{1,0:T(8,128)S(1)}, u32[]{:S(2)}, u32[]{:S(2)}) collective-permute-start(f32[24,640]{1,0:T(8,128)S(1)} %constant_dynamic-slice_fusion.8), channel_id=1, source_target_pairs={{0,8},{1,9},{2,10},{3,11},{4,12},{5,13},{6,14},{7,15},{8,0},{9,1},... | collective-permute-start | bytes 184328 | tf_op jit(solution)/shard_map/ppermute | solution.py:37
  122.2 5.2 %collective-permute-start.13 = (f32[24,640]{1,0:T(8,128)S(1)}, f32[24,640]{1,0:T(8,128)S(1)}, u32[]{:S(2)}, u32[]{:S(2)}) collective-permute-start(f32[24,640]{1,0:T(8,128)S(1)} %dynamic-slice_add_fusion.11), channel_id=1, source_target_pairs={{0,8},{1,9},{2,10},{3,11},{4,12},{5,13},{6,14},{7,15},{8,0},{9,1},... | collective-permute-start | bytes 184328 | tf_op jit(solution)/shard_map/ppermute | solution.py:43
  127.4 4.9 %collective-permute-start.14 = (f32[48,640]{1,0:T(8,128)S(1)}, f32[48,640]{1,0:T(8,128)S(1)}, u32[]{:S(2)}, u32[]{:S(2)}) collective-permute-start(f32[48,640]{1,0:T(8,128)S(1)} %maximum_select_fusion.10), channel_id=1, source_target_pairs={{0,4},{1,5},{2,6},{3,7},{4,0},{5,1},{6,2},{7,3},{8,12},{9,13},{10,... | collective-permute-start | bytes 368648 | tf_op jit(solution)/shard_map/ppermute | solution.py:43
  132.4 6.3 %collective-permute-start.15 = (f32[96,640]{1,0:T(8,128)S(1)}, f32[96,640]{1,0:T(8,128)S(1)}, u32[]{:S(2)}, u32[]{:S(2)}) collective-permute-start(f32[96,640]{1,0:T(8,128)S(1)} %maximum_select_fusion.6), channel_id=1, source_target_pairs={{0,2},{1,3},{2,0},{3,1},{4,6},{5,7},{6,4},{7,5},{8,10},{9,11},{10,... | collective-permute-start | bytes 737288 | tf_op jit(solution)/shard_map/ppermute | solution.py:43
  138.7 1.9 collective-permute-start.16
  143.3 7.1 %collective-permute-start.17 = (f32[128,384]{0,1:T(8,128)S(1)}, f32[128,384]{0,1:T(8,128)S(1)}, u32[]{:S(2)}, u32[]{:S(2)}) collective-permute-start(f32[128,384]{0,1:T(8,128)S(1)} %fusion.35), channel_id=1, source_target_pairs={{0,16},{16,0},{1,17},{17,1},{2,18},{18,2},{3,19},{19,3},{4,20},{20... | collective-permute-start | bytes 589832 | tf_op jit(solution)/shard_map/ppermute | solution.py:56
  153.2 5.3 %collective-permute-start.19 = (f32[224,128]{1,0:T(8,128)S(1)}, f32[224,128]{1,0:T(8,128)S(1)}, u32[]{:S(2)}, u32[]{:S(2)}) collective-permute-start(f32[224,128]{1,0:T(8,128)S(1)} %constant_dynamic-slice_fusion.6), channel_id=1, source_target_pairs={{0,2},{1,3},{2,0},{3,1},{4,6},{5,7},{6,4},{7,5},{8,10},{9,11},{10,... | collective-permute-start | bytes 344072 | tf_op jit(solution)/shard_map/ppermute | solution.py:37
  158.5 4.2 %collective-permute-start.20 = (f32[112,128]{1,0:T(8,128)S(1)}, f32[112,128]{1,0:T(8,128)S(1)}, u32[]{:S(2)}, u32[]{:S(2)}) collective-permute-start(f32[112,128]{1,0:T(8,128)S(1)} %constant_dynamic-slice_fusion.5), channel_id=1, source_target_pairs={{0,4},{1,5},{2,6},{3,7},{4,0},{5,1},{6,2},{7,3},{8,12},{9,13},{10,... | collective-permute-start | bytes 172040 | tf_op jit(solution)/shard_map/ppermute | solution.py:37
  160.1 9.3 %collective-permute-start.26 = (f32[192,640]{1,0:T(8,128)S(1)}, f32[192,640]{1,0:T(8,128)S(1)}, u32[]{:S(2)}, u32[]{:S(2)}) collective-permute-start(f32[192,640]{1,0:T(8,128)S(1)} %constant_dynamic-slice_fusion.3), channel_id=1, source_target_pairs={{0,1},{1,0},{2,3},{3,2},{4,5},{5,4},{6,7},{7,6},{8,9},{9,8},{10,11... | collective-permute-start | bytes 1474568 | tf_op jit(solution)/shard_map/ppermute | solution.py:37
  162.7 4.8 %collective-permute-start.21 = (f32[56,128]{1,0:T(8,128)S(1)}, f32[56,128]{1,0:T(8,128)S(1)}, u32[]{:S(2)}, u32[]{:S(2)}) collective-permute-start(f32[56,128]{1,0:T(8,128)S(1)} %constant_dynamic-slice_fusion.4), channel_id=1, source_target_pairs={{0,8},{1,9},{2,10},{3,11},{4,12},{5,13},{6,14},{7,15},{8,0},{9,1},... | collective-permute-start | bytes 86024 | tf_op jit(solution)/shard_map/ppermute | solution.py:37
  167.6 4.8 %collective-permute-start.22 = (f32[56,128]{1,0:T(8,128)S(1)}, f32[56,128]{1,0:T(8,128)S(1)}, u32[]{:S(2)}, u32[]{:S(2)}) collective-permute-start(f32[56,128]{1,0:T(8,128)S(1)} %dynamic-slice_add_fusion.14), channel_id=1, source_target_pairs={{0,8},{1,9},{2,10},{3,11},{4,12},{5,13},{6,14},{7,15},{8,0},{9,1},... | collective-permute-start | bytes 86024 | tf_op jit(solution)/shard_map/ppermute | solution.py:43
  169.4 8.7 %collective-permute-start.27 = (f32[96,640]{1,0:T(8,128)S(1)}, f32[96,640]{1,0:T(8,128)S(1)}, u32[]{:S(2)}, u32[]{:S(2)}) collective-permute-start(f32[96,640]{1,0:T(8,128)S(1)} %constant_dynamic-slice_fusion.2), channel_id=1, source_target_pairs={{0,2},{1,3},{2,0},{3,1},{4,6},{5,7},{6,4},{7,5},{8,10},{9,11},{10,... | collective-permute-start | bytes 737288 | tf_op jit(solution)/shard_map/ppermute | solution.py:37
  172.4 4.3 %collective-permute-start.23 = (f32[112,128]{1,0:T(8,128)S(1)}, f32[112,128]{1,0:T(8,128)S(1)}, u32[]{:S(2)}, u32[]{:S(2)}) collective-permute-start(f32[112,128]{1,0:T(8,128)S(1)} %maximum_select_fusion.15), channel_id=1, source_target_pairs={{0,4},{1,5},{2,6},{3,7},{4,0},{5,1},{6,2},{7,3},{8,12},{9,13},{10,... | collective-permute-start | bytes 172040 | tf_op jit(solution)/shard_map/ppermute | solution.py:43
  176.7 4.9 %collective-permute-start.24 = (f32[224,128]{1,0:T(8,128)S(1)}, f32[224,128]{1,0:T(8,128)S(1)}, u32[]{:S(2)}, u32[]{:S(2)}) collective-permute-start(f32[224,128]{1,0:T(8,128)S(1)} %maximum_select_fusion.13), channel_id=1, source_target_pairs={{0,2},{1,3},{2,0},{3,1},{4,6},{5,7},{6,4},{7,5},{8,10},{9,11},{10,... | collective-permute-start | bytes 344072 | tf_op jit(solution)/shard_map/ppermute | solution.py:43
  178.2 4.9 %collective-permute-start.28 = (f32[48,640]{1,0:T(8,128)S(1)}, f32[48,640]{1,0:T(8,128)S(1)}, u32[]{:S(2)}, u32[]{:S(2)}) collective-permute-start(f32[48,640]{1,0:T(8,128)S(1)} %constant_dynamic-slice_fusion.1), channel_id=1, source_target_pairs={{0,4},{1,5},{2,6},{3,7},{4,0},{5,1},{6,2},{7,3},{8,12},{9,13},{10,... | collective-permute-start | bytes 368648 | tf_op jit(solution)/shard_map/ppermute | solution.py:37
  181.5 3.8 %collective-permute-start.25 = (f32[448,128]{1,0:T(8,128)S(1)}, f32[448,128]{1,0:T(8,128)S(1)}, u32[]{:S(2)}, u32[]{:S(2)}) collective-permute-start(f32[448,128]{1,0:T(8,128)S(1)} %maximum_select_fusion.9), channel_id=1, source_target_pairs={{0,1},{1,0},{2,3},{3,2},{4,5},{5,4},{6,7},{7,6},{8,9},{9,8},{10,11... | collective-permute-start | bytes 688136 | tf_op jit(solution)/shard_map/ppermute | solution.py:43
  183.2 76.0 %collective-permute-start.29 = (f32[24,640]{1,0:T(8,128)S(1)}, f32[24,640]{1,0:T(8,128)S(1)}, u32[]{:S(2)}, u32[]{:S(2)}) collective-permute-start(f32[24,640]{1,0:T(8,128)S(1)} %constant_dynamic-slice_fusion), channel_id=1, source_target_pairs={{0,8},{1,9},{2,10},{3,11},{4,12},{5,13},{6,14},{7,15},{8,0},{9,1},... | collective-permute-start | bytes 184328 | tf_op jit(solution)/shard_map/ppermute | solution.py:37
  259.3 5.2 %collective-permute-start.30 = (f32[24,640]{1,0:T(8,128)S(1)}, f32[24,640]{1,0:T(8,128)S(1)}, u32[]{:S(2)}, u32[]{:S(2)}) collective-permute-start(f32[24,640]{1,0:T(8,128)S(1)} %dynamic-slice_add_fusion.10), channel_id=1, source_target_pairs={{0,8},{1,9},{2,10},{3,11},{4,12},{5,13},{6,14},{7,15},{8,0},{9,1},... | collective-permute-start | bytes 184328 | tf_op jit(solution)/shard_map/ppermute | solution.py:43
  264.5 4.9 %collective-permute-start.31 = (f32[48,640]{1,0:T(8,128)S(1)}, f32[48,640]{1,0:T(8,128)S(1)}, u32[]{:S(2)}, u32[]{:S(2)}) collective-permute-start(f32[48,640]{1,0:T(8,128)S(1)} %maximum_select_fusion.11), channel_id=1, source_target_pairs={{0,4},{1,5},{2,6},{3,7},{4,0},{5,1},{6,2},{7,3},{8,12},{9,13},{10,... | collective-permute-start | bytes 368648 | tf_op jit(solution)/shard_map/ppermute | solution.py:43
  269.4 6.3 %collective-permute-start.32 = (f32[96,640]{1,0:T(8,128)S(1)}, f32[96,640]{1,0:T(8,128)S(1)}, u32[]{:S(2)}, u32[]{:S(2)}) collective-permute-start(f32[96,640]{1,0:T(8,128)S(1)} %maximum_select_fusion.7), channel_id=1, source_target_pairs={{0,2},{1,3},{2,0},{3,1},{4,6},{5,7},{6,4},{7,5},{8,10},{9,11},{10,... | collective-permute-start | bytes 737288 | tf_op jit(solution)/shard_map/ppermute | solution.py:43
  275.7 1.9 collective-permute-start.33
  (6 other events, 11.8 us)

commit v9 on v7

--- a/solution.py
+++ b/solution.py
@@ -136,17 +136,17 @@
         blk[i][j] = part
     obs_anom = observed - obs_mean[None, :]
     rhs = (target - obs_mean)[:, None] - 0.5 * obs_anom.T
-    shift = lax.optimization_barrier(m_loc * tdot(dev_obs, dev_row) / (count - 1.0))
     gain = block_solve(blk, rhs, size)
 
-    cross = cross_sum / (count - 1.0) + shift
+    cross = (cross_sum + m_loc * tdot(dev_obs, dev_row)) / (count - 1.0)
     return gain, cross
 
 
 def shards(state, obs_values, noise_var, obs_rows, owner):
     num_blocks = obs_rows.shape[0]
     current = state
-    cands = jnp.take(current, obs_rows[0], axis=1)
+    onehot = (jnp.arange(current.shape[1], dtype=obs_rows.dtype)[:, None] == obs_rows[0][None, :]).astype(current.dtype)
+    cands = full_dot(current, onehot)
     for block in range(num_blocks):
         observed = exchange(cands, owner[block])
         gain, cross = analyse(current, observed, obs_values[block], noise_var[block])

time: 286 us -> 285 us (level)
  local copies, waits for them, and re-layouts: 9.09 us -> 6.19 us
    dot_general x29 -> x30, matrix products: 10.8 us -> 12.3 us  [full_dot(): jnp.dot(left, right, precision=lax.Precision.HIGHEST, preferred_element_t...]
where the time goes in v9:
time: 285 us; the launch traced here: 281 us
  other arithmetic  139 us (49%)
  waiting for transfers between devices  64.4 us (23%)
  starting transfers between devices  45.6 us (16%)
  matrix products  24.1 us (8%)
  local copies, waits for them, and re-layouts  6.19 us (2%)
    another operation x18, other arithmetic, block_solve(): diag = lax.linalg.cholesky(blk[k][k], symmetrize_input=False)  74.9 us
    another operation x12, other arithmetic, block_solve(): inv[k] = lax.linalg.triangular_solve(diag, eye, left_side=True, lower=True)  62.8 us
    ppermute x16, waiting for transfers between devices, tree_sum(): other = lax.ppermute(cur, axis, perm)  33.5 us
    ppermute x16, starting transfers between devices, tree_sum(): cur = keep + lax.ppermute(away, axis, perm)  22.6 us
    ppermute x16, waiting for transfers between devices, tree_sum(): cur = keep + lax.ppermute(away, axis, perm)  20.6 us
    ppermute x16, starting transfers between devices, tree_sum(): other = lax.ppermute(cur, axis, perm)  18.4 us
    dot_general x30, matrix products, full_dot(): jnp.dot(left, right, precision=lax.Precision.HIGHEST, preferred_element_t...  12.3 us
    ppermute x2, waiting for transfers between devices, tree_sum_exact(): x = x + lax.ppermute(x, axis, perm)  10.3 us
  transfers between devices with their start and end apart: 34, of which 25 were waited for; matrix products, arithmetic and copies ran while one was open for 56% of the time, Pallas kernels for 0%

profile of v9, /device:TPU:0, one launch (start us, length us, event | category | flops | bytes accessed | tf_op | source)
XLA Modules:
  0.0 281.2 jit_solution(11922541868987108089)
XLA Ops:
  3.2 3.0 %collective-permute-start = (f32[128,384]{1,0:T(8,128)S(1)}, f32[128,384]{1,0:T(8,128)S(1)}, u32[]{:S(2)}, u32[]{:S(2)}) collective-permute-start(f32[128,384]{1,0:T(8,128)S(1)} %fusion), channel_id=1, source_target_pairs={{0,16},{16,0},{1,17},{17,1},{2,18},{18,2},{3,19},{19,3},{4,20},{20... | collective-permute-start | bytes 589832 | tf_op jit(solution)/shard_map/ppermute | solution.py:56
  6.3 4.8 %collective-permute-done = f32[128,384]{1,0:T(8,128)S(1)} collective-permute-done((f32[128,384]{1,0:T(8,128)S(1)}, f32[128,384]{1,0:T(8,128)S(1)}, u32[]{:S(2)}, u32[]{:S(2)}) %collective-permute-start) | collective-permute-done | bytes 196640 | tf_op jit(solution)/shard_map/ppermute | solution.py:56
  16.6 2.5 collective-permute-done.2
  21.0 2.3 collective-permute-done.3
  23.3 2.9 %collective-permute-start.4 = (f32[56,128]{1,0:T(8,128)S(1)}, f32[56,128]{1,0:T(8,128)S(1)}, u32[]{:S(2)}, u32[]{:S(2)}) collective-permute-start(f32[56,128]{1,0:T(8,128)S(1)} %constant_dynamic-slice_fusion.12), channel_id=1, source_target_pairs={{0,8},{1,9},{2,10},{3,11},{4,12},{5,13},{6,14},{7,15},{8,0},{9,1},... | collective-permute-start | bytes 86024 | tf_op jit(solution)/shard_map/ppermute | solution.py:37
  28.2 2.8 %collective-permute-start.5 = (f32[56,128]{1,0:T(8,128)S(1)}, f32[56,128]{1,0:T(8,128)S(1)}, u32[]{:S(2)}, u32[]{:S(2)}) collective-permute-start(f32[56,128]{1,0:T(8,128)S(1)} %dynamic-slice_add_fusion.15), channel_id=1, source_target_pairs={{0,8},{1,9},{2,10},{3,11},{4,12},{5,13},{6,14},{7,15},{8,0},{9,1},... | collective-permute-start | bytes 86024 | tf_op jit(solution)/shard_map/ppermute | solution.py:43
  35.2 2.7 collective-permute-done.6
  44.5 2.5 collective-permute-start.12
  47.8 11.7 %custom-call.16 = f32[128,128]{1,0:T(8,128)S(1)} custom-call(f32[128,128]{1,0:T(8,128)S(1)} %fusion.90), custom_call_target="Cholesky" | custom-call | tf_op jit(solution)/shard_map/cholesky/custom-call.1 | solution.py:69
  60.9 9.8 %custom-call.17 = f32[1,128,128]{1,2,0:T(8,128)S(1)} custom-call(f32[1,128,128]{2,1,0:T(8,128)S(1)} %fusion.51), custom_call_target="InvertDiagBlocksLowerTriangular" | custom-call | tf_op jit(solution)/shard_map/triangular_solve/custom-call.0 | solution.py:70
  73.3 12.1 %custom-call.18 = f32[128,128]{1,0:T(8,128)S(1)} custom-call(f32[128,128]{1,0:T(8,128)S(1)} %convolution_subtract_fusion.19), custom_call_target="Cholesky" | custom-call | tf_op jit(solution)/shard_map/cholesky/custom-call.1 | solution.py:69
  86.7 9.8 %custom-call.19 = f32[1,128,128]{1,2,0:T(8,128)S(1)} custom-call(f32[1,128,128]{2,1,0:T(8,128)S(1)} %fusion.52), custom_call_target="InvertDiagBlocksLowerTriangular" | custom-call | tf_op jit(solution)/shard_map/triangular_solve/custom-call.0 | solution.py:70
  97.3 11.7 %custom-call.20 = f32[128,128]{1,0:T(8,128)S(1)} custom-call(f32[128,128]{1,0:T(8,128)S(1)} %convolution_subtract_fusion.15), custom_call_target="Cholesky" | custom-call | tf_op jit(solution)/shard_map/cholesky/custom-call.1 | solution.py:69
  110.4 9.8 %custom-call.21 = f32[1,128,128]{1,2,0:T(8,128)S(1)} custom-call(f32[1,128,128]{2,1,0:T(8,128)S(1)} %fusion.53), custom_call_target="InvertDiagBlocksLowerTriangular" | custom-call | tf_op jit(solution)/shard_map/triangular_solve/custom-call.0 | solution.py:70
  121.9 4.3 %collective-permute-done.13 = f32[24,640]{1,0:T(8,128)S(1)} collective-permute-done((f32[24,640]{1,0:T(8,128)S(1)}, f32[24,640]{1,0:T(8,128)S(1)}, u32[]{:S(2)}, u32[]{:S(2)}) %collective-permute-start.13) | collective-permute-done | bytes 61472 | tf_op jit(solution)/shard_map/ppermute | solution.py:43
  128.1 3.1 %collective-permute-done.14 = f32[48,640]{1,0:T(8,128)S(1)} collective-permute-done((f32[48,640]{1,0:T(8,128)S(1)}, f32[48,640]{1,0:T(8,128)S(1)}, u32[]{:S(2)}, u32[]{:S(2)}) %collective-permute-start.14) | collective-permute-done | bytes 122912 | tf_op jit(solution)/shard_map/ppermute | solution.py:43
  132.7 4.8 %collective-permute-done.15 = f32[96,640]{1,0:T(8,128)S(1)} collective-permute-done((f32[96,640]{1,0:T(8,128)S(1)}, f32[96,640]{1,0:T(8,128)S(1)}, u32[]{:S(2)}, u32[]{:S(2)}) %collective-permute-start.15) | collective-permute-done | bytes 245792 | tf_op jit(solution)/shard_map/ppermute | solution.py:43
  146.1 5.4 %collective-permute-done.17 = f32[128,384]{1,0:T(8,128)S(1)} collective-permute-done((f32[128,384]{1,0:T(8,128)S(1)}, f32[128,384]{1,0:T(8,128)S(1)}, u32[]{:S(2)}, u32[]{:S(2)}) %collective-permute-start.17) | collective-permute-done | bytes 196640 | tf_op jit(solution)/shard_map/ppermute | solution.py:56
  156.1 3.3 %collective-permute-done.19 = f32[224,128]{1,0:T(8,128)S(1)} collective-permute-done((f32[224,128]{1,0:T(8,128)S(1)}, f32[224,128]{1,0:T(8,128)S(1)}, u32[]{:S(2)}, u32[]{:S(2)}) %collective-permute-start.19) | collective-permute-done | bytes 114720 | tf_op jit(solution)/shard_map/ppermute | solution.py:37
  161.2 2.6 collective-permute-done.20
  165.6 3.1 %collective-permute-done.21 = f32[56,128]{1,0:T(8,128)S(1)} collective-permute-done((f32[56,128]{1,0:T(8,128)S(1)}, f32[56,128]{1,0:T(8,128)S(1)}, u32[]{:S(2)}, u32[]{:S(2)}) %collective-permute-start.21) | collective-permute-done | bytes 28704 | tf_op jit(solution)/shard_map/ppermute | solution.py:37
  175.1 2.6 collective-permute-done.23
  184.2 2.2 collective-permute-start.29
  187.3 11.7 %custom-call.22 = f32[128,128]{1,0:T(8,128)S(1)} custom-call(f32[128,128]{1,0:T(8,128)S(1)} %fusion.73), custom_call_target="Cholesky" | custom-call | tf_op jit(solution)/shard_map/cholesky/custom-call.1 | solution.py:69
  200.3 9.8 %custom-call.23 = f32[1,128,128]{1,2,0:T(8,128)S(1)} custom-call(f32[1,128,128]{2,1,0:T(8,128)S(1)} %fusion.54), custom_call_target="InvertDiagBlocksLowerTriangular" | custom-call | tf_op jit(solution)/shard_map/triangular_solve/custom-call.0 | solution.py:70
  212.7 11.9 %custom-call.24 = f32[128,128]{1,0:T(8,128)S(1)} custom-call(f32[128,128]{1,0:T(8,128)S(1)} %convolution_subtract_fusion.9), custom_call_target="Cholesky" | custom-call | tf_op jit(solution)/shard_map/cholesky/custom-call.1 | solution.py:69
  226.0 9.8 %custom-call.25 = f32[1,128,128]{1,2,0:T(8,128)S(1)} custom-call(f32[1,128,128]{2,1,0:T(8,128)S(1)} %fusion.55), custom_call_target="InvertDiagBlocksLowerTriangular" | custom-call | tf_op jit(solution)/shard_map/triangular_solve/custom-call.0 | solution.py:70
  236.6 11.7 %custom-call.26 = f32[128,128]{1,0:T(8,128)S(1)} custom-call(f32[128,128]{1,0:T(8,128)S(1)} %convolution_subtract_fusion.5), custom_call_target="Cholesky" | custom-call | tf_op jit(solution)/shard_map/cholesky/custom-call.1 | solution.py:69
  249.7 9.8 %custom-call.27 = f32[1,128,128]{1,2,0:T(8,128)S(1)} custom-call(f32[1,128,128]{2,1,0:T(8,128)S(1)} %fusion.56), custom_call_target="InvertDiagBlocksLowerTriangular" | custom-call | tf_op jit(solution)/shard_map/triangular_solve/custom-call.0 | solution.py:70
  262.0 4.1 %collective-permute-done.30 = f32[24,640]{1,0:T(8,128)S(1)} collective-permute-done((f32[24,640]{1,0:T(8,128)S(1)}, f32[24,640]{1,0:T(8,128)S(1)}, u32[]{:S(2)}, u32[]{:S(2)}) %collective-permute-start.30) | collective-permute-done | bytes 61472 | tf_op jit(solution)/shard_map/ppermute | solution.py:43
  268.1 2.9 %collective-permute-done.31 = f32[48,640]{1,0:T(8,128)S(1)} collective-permute-done((f32[48,640]{1,0:T(8,128)S(1)}, f32[48,640]{1,0:T(8,128)S(1)}, u32[]{:S(2)}, u32[]{:S(2)}) %collective-permute-start.31) | collective-permute-done | bytes 122912 | tf_op jit(solution)/shard_map/ppermute | solution.py:43
  272.6 4.7 %collective-permute-done.32 = f32[96,640]{1,0:T(8,128)S(1)} collective-permute-done((f32[96,640]{1,0:T(8,128)S(1)}, f32[96,640]{1,0:T(8,128)S(1)}, u32[]{:S(2)}, u32[]{:S(2)}) %collective-permute-start.32) | collective-permute-done | bytes 245792 | tf_op jit(solution)/shard_map/ppermute | solution.py:43
  (233 shorter events, 83.5 us)
Async XLA Ops:
  3.2 7.9 %collective-permute-start = (f32[128,384]{1,0:T(8,128)S(1)}, f32[128,384]{1,0:T(8,128)S(1)}, u32[]{:S(2)}, u32[]{:S(2)}) collective-permute-start(f32[128,384]{1,0:T(8,128)S(1)} %fusion), channel_id=1, source_target_pairs={{0,16},{16,0},{1,17},{17,1},{2,18},{18,2},{3,19},{19,3},{4,20},{20... | collective-permute-start | bytes 589832 | tf_op jit(solution)/shard_map/ppermute | solution.py:56
  13.7 5.3 %collective-permute-start.2 = (f32[224,128]{1,0:T(8,128)S(1)}, f32[224,128]{1,0:T(8,128)S(1)}, u32[]{:S(2)}, u32[]{:S(2)}) collective-permute-start(f32[224,128]{1,0:T(8,128)S(1)} %constant_dynamic-slice_fusion.14), channel_id=1, source_target_pairs={{0,2},{1,3},{2,0},{3,1},{4,6},{5,7},{6,4},{7,5},{8,10},{9,11},{10,... | collective-permute-start | bytes 344072 | tf_op jit(solution)/shard_map/ppermute | solution.py:37
  19.0 4.2 %collective-permute-start.3 = (f32[112,128]{1,0:T(8,128)S(1)}, f32[112,128]{1,0:T(8,128)S(1)}, u32[]{:S(2)}, u32[]{:S(2)}) collective-permute-start(f32[112,128]{1,0:T(8,128)S(1)} %constant_dynamic-slice_fusion.13), channel_id=1, source_target_pairs={{0,4},{1,5},{2,6},{3,7},{4,0},{5,1},{6,2},{7,3},{8,12},{9,13},{10,... | collective-permute-start | bytes 172040 | tf_op jit(solution)/shard_map/ppermute | solution.py:37
  20.9 10.1 %collective-permute-start.9 = (f32[192,640]{1,0:T(8,128)S(1)}, f32[192,640]{1,0:T(8,128)S(1)}, u32[]{:S(2)}, u32[]{:S(2)}) collective-permute-start(f32[192,640]{1,0:T(8,128)S(1)} %constant_dynamic-slice_fusion.11), channel_id=1, source_target_pairs={{0,1},{1,0},{2,3},{3,2},{4,5},{5,4},{6,7},{7,6},{8,9},{9,8},{10,11... | collective-permute-start | bytes 1474568 | tf_op jit(solution)/shard_map/ppermute | solution.py:37
  23.3 4.8 %collective-permute-start.4 = (f32[56,128]{1,0:T(8,128)S(1)}, f32[56,128]{1,0:T(8,128)S(1)}, u32[]{:S(2)}, u32[]{:S(2)}) collective-permute-start(f32[56,128]{1,0:T(8,128)S(1)} %constant_dynamic-slice_fusion.12), channel_id=1, source_target_pairs={{0,8},{1,9},{2,10},{3,11},{4,12},{5,13},{6,14},{7,15},{8,0},{9,1},... | collective-permute-start | bytes 86024 | tf_op jit(solution)/shard_map/ppermute | solution.py:37
  28.2 4.8 %collective-permute-start.5 = (f32[56,128]{1,0:T(8,128)S(1)}, f32[56,128]{1,0:T(8,128)S(1)}, u32[]{:S(2)}, u32[]{:S(2)}) collective-permute-start(f32[56,128]{1,0:T(8,128)S(1)} %dynamic-slice_add_fusion.15), channel_id=1, source_target_pairs={{0,8},{1,9},{2,10},{3,11},{4,12},{5,13},{6,14},{7,15},{8,0},{9,1},... | collective-permute-start | bytes 86024 | tf_op jit(solution)/shard_map/ppermute | solution.py:43
  31.1 8.4 %collective-permute-start.10 = (f32[96,640]{1,0:T(8,128)S(1)}, f32[96,640]{1,0:T(8,128)S(1)}, u32[]{:S(2)}, u32[]{:S(2)}) collective-permute-start(f32[96,640]{1,0:T(8,128)S(1)} %constant_dynamic-slice_fusion.10), channel_id=1, source_target_pairs={{0,2},{1,3},{2,0},{3,1},{4,6},{5,7},{6,4},{7,5},{8,10},{9,11},{10,... | collective-permute-start | bytes 737288 | tf_op jit(solution)/shard_map/ppermute | solution.py:37
  33.0 5.0 %collective-permute-start.6 = (f32[112,128]{1,0:T(8,128)S(1)}, f32[112,128]{1,0:T(8,128)S(1)}, u32[]{:S(2)}, u32[]{:S(2)}) collective-permute-start(f32[112,128]{1,0:T(8,128)S(1)} %maximum_select_fusion.14), channel_id=1, source_target_pairs={{0,4},{1,5},{2,6},{3,7},{4,0},{5,1},{6,2},{7,3},{8,12},{9,13},{10,... | collective-permute-start | bytes 172040 | tf_op jit(solution)/shard_map/ppermute | solution.py:43
  37.9 5.0 %collective-permute-start.7 = (f32[224,128]{1,0:T(8,128)S(1)}, f32[224,128]{1,0:T(8,128)S(1)}, u32[]{:S(2)}, u32[]{:S(2)}) collective-permute-start(f32[224,128]{1,0:T(8,128)S(1)} %maximum_select_fusion.12), channel_id=1, source_target_pairs={{0,2},{1,3},{2,0},{3,1},{4,6},{5,7},{6,4},{7,5},{8,10},{9,11},{10,... | collective-permute-start | bytes 344072 | tf_op jit(solution)/shard_map/ppermute | solution.py:43
  39.5 4.9 %collective-permute-start.11 = (f32[48,640]{1,0:T(8,128)S(1)}, f32[48,640]{1,0:T(8,128)S(1)}, u32[]{:S(2)}, u32[]{:S(2)}) collective-permute-start(f32[48,640]{1,0:T(8,128)S(1)} %constant_dynamic-slice_fusion.9), channel_id=1, source_target_pairs={{0,4},{1,5},{2,6},{3,7},{4,0},{5,1},{6,2},{7,3},{8,12},{9,13},{10,... | collective-permute-start | bytes 368648 | tf_op jit(solution)/shard_map/ppermute | solution.py:37
  43.0 4.0 %collective-permute-start.8 = (f32[448,128]{1,0:T(8,128)S(1)}, f32[448,128]{1,0:T(8,128)S(1)}, u32[]{:S(2)}, u32[]{:S(2)}) collective-permute-start(f32[448,128]{1,0:T(8,128)S(1)} %maximum_select_fusion.8), channel_id=1, source_target_pairs={{0,1},{1,0},{2,3},{3,2},{4,5},{5,4},{6,7},{7,6},{8,9},{9,8},{10,11... | collective-permute-start | bytes 688136 | tf_op jit(solution)/shard_map/ppermute | solution.py:43
  44.5 76.5 %collective-permute-start.12 = (f32[24,640]{1,0:T(8,128)S(1)}, f32[24,640]{1,0:T(8,128)S(1)}, u32[]{:S(2)}, u32[]{:S(2)}) collective-permute-start(f32[24,640]{1,0:T(8,128)S(1)} %constant_dynamic-slice_fusion.8), channel_id=1, source_target_pairs={{0,8},{1,9},{2,10},{3,11},{4,12},{5,13},{6,14},{7,15},{8,0},{9,1},... | collective-permute-start | bytes 184328 | tf_op jit(solution)/shard_map/ppermute | solution.py:37
  121.1 5.2 %collective-permute-start.13 = (f32[24,640]{1,0:T(8,128)S(1)}, f32[24,640]{1,0:T(8,128)S(1)}, u32[]{:S(2)}, u32[]{:S(2)}) collective-permute-start(f32[24,640]{1,0:T(8,128)S(1)} %dynamic-slice_add_fusion.11), channel_id=1, source_target_pairs={{0,8},{1,9},{2,10},{3,11},{4,12},{5,13},{6,14},{7,15},{8,0},{9,1},... | collective-permute-start | bytes 184328 | tf_op jit(solution)/shard_map/ppermute | solution.py:43
  126.3 4.9 %collective-permute-start.14 = (f32[48,640]{1,0:T(8,128)S(1)}, f32[48,640]{1,0:T(8,128)S(1)}, u32[]{:S(2)}, u32[]{:S(2)}) collective-permute-start(f32[48,640]{1,0:T(8,128)S(1)} %maximum_select_fusion.10), channel_id=1, source_target_pairs={{0,4},{1,5},{2,6},{3,7},{4,0},{5,1},{6,2},{7,3},{8,12},{9,13},{10,... | collective-permute-start | bytes 368648 | tf_op jit(solution)/shard_map/ppermute | solution.py:43
  131.3 6.3 %collective-permute-start.15 = (f32[96,640]{1,0:T(8,128)S(1)}, f32[96,640]{1,0:T(8,128)S(1)}, u32[]{:S(2)}, u32[]{:S(2)}) collective-permute-start(f32[96,640]{1,0:T(8,128)S(1)} %maximum_select_fusion.6), channel_id=1, source_target_pairs={{0,2},{1,3},{2,0},{3,1},{4,6},{5,7},{6,4},{7,5},{8,10},{9,11},{10,... | collective-permute-start | bytes 737288 | tf_op jit(solution)/shard_map/ppermute | solution.py:43
  137.6 1.9 collective-permute-start.16
  144.6 7.0 %collective-permute-start.17 = (f32[128,384]{1,0:T(8,128)S(1)}, f32[128,384]{1,0:T(8,128)S(1)}, u32[]{:S(2)}, u32[]{:S(2)}) collective-permute-start(f32[128,384]{1,0:T(8,128)S(1)} %fusion.1), channel_id=1, source_target_pairs={{0,16},{16,0},{1,17},{17,1},{2,18},{18,2},{3,19},{19,3},{4,20},{20... | collective-permute-start | bytes 589832 | tf_op jit(solution)/shard_map/ppermute | solution.py:56
  154.2 5.3 %collective-permute-start.19 = (f32[224,128]{1,0:T(8,128)S(1)}, f32[224,128]{1,0:T(8,128)S(1)}, u32[]{:S(2)}, u32[]{:S(2)}) collective-permute-start(f32[224,128]{1,0:T(8,128)S(1)} %constant_dynamic-slice_fusion.6), channel_id=1, source_target_pairs={{0,2},{1,3},{2,0},{3,1},{4,6},{5,7},{6,4},{7,5},{8,10},{9,11},{10,... | collective-permute-start | bytes 344072 | tf_op jit(solution)/shard_map/ppermute | solution.py:37
  159.5 4.2 %collective-permute-start.20 = (f32[112,128]{1,0:T(8,128)S(1)}, f32[112,128]{1,0:T(8,128)S(1)}, u32[]{:S(2)}, u32[]{:S(2)}) collective-permute-start(f32[112,128]{1,0:T(8,128)S(1)} %constant_dynamic-slice_fusion.5), channel_id=1, source_target_pairs={{0,4},{1,5},{2,6},{3,7},{4,0},{5,1},{6,2},{7,3},{8,12},{9,13},{10,... | collective-permute-start | bytes 172040 | tf_op jit(solution)/shard_map/ppermute | solution.py:37
  161.1 9.3 %collective-permute-start.26 = (f32[192,640]{1,0:T(8,128)S(1)}, f32[192,640]{1,0:T(8,128)S(1)}, u32[]{:S(2)}, u32[]{:S(2)}) collective-permute-start(f32[192,640]{1,0:T(8,128)S(1)} %constant_dynamic-slice_fusion.3), channel_id=1, source_target_pairs={{0,1},{1,0},{2,3},{3,2},{4,5},{5,4},{6,7},{7,6},{8,9},{9,8},{10,11... | collective-permute-start | bytes 1474568 | tf_op jit(solution)/shard_map/ppermute | solution.py:37
  163.8 4.8 %collective-permute-start.21 = (f32[56,128]{1,0:T(8,128)S(1)}, f32[56,128]{1,0:T(8,128)S(1)}, u32[]{:S(2)}, u32[]{:S(2)}) collective-permute-start(f32[56,128]{1,0:T(8,128)S(1)} %constant_dynamic-slice_fusion.4), channel_id=1, source_target_pairs={{0,8},{1,9},{2,10},{3,11},{4,12},{5,13},{6,14},{7,15},{8,0},{9,1},... | collective-permute-start | bytes 86024 | tf_op jit(solution)/shard_map/ppermute | solution.py:37
  168.6 4.8 %collective-permute-start.22 = (f32[56,128]{1,0:T(8,128)S(1)}, f32[56,128]{1,0:T(8,128)S(1)}, u32[]{:S(2)}, u32[]{:S(2)}) collective-permute-start(f32[56,128]{1,0:T(8,128)S(1)} %dynamic-slice_add_fusion.14), channel_id=1, source_target_pairs={{0,8},{1,9},{2,10},{3,11},{4,12},{5,13},{6,14},{7,15},{8,0},{9,1},... | collective-permute-start | bytes 86024 | tf_op jit(solution)/shard_map/ppermute | solution.py:43
  170.5 8.7 %collective-permute-start.27 = (f32[96,640]{1,0:T(8,128)S(1)}, f32[96,640]{1,0:T(8,128)S(1)}, u32[]{:S(2)}, u32[]{:S(2)}) collective-permute-start(f32[96,640]{1,0:T(8,128)S(1)} %constant_dynamic-slice_fusion.2), channel_id=1, source_target_pairs={{0,2},{1,3},{2,0},{3,1},{4,6},{5,7},{6,4},{7,5},{8,10},{9,11},{10,... | collective-permute-start | bytes 737288 | tf_op jit(solution)/shard_map/ppermute | solution.py:37
  173.4 4.3 %collective-permute-start.23 = (f32[112,128]{1,0:T(8,128)S(1)}, f32[112,128]{1,0:T(8,128)S(1)}, u32[]{:S(2)}, u32[]{:S(2)}) collective-permute-start(f32[112,128]{1,0:T(8,128)S(1)} %maximum_select_fusion.15), channel_id=1, source_target_pairs={{0,4},{1,5},{2,6},{3,7},{4,0},{5,1},{6,2},{7,3},{8,12},{9,13},{10,... | collective-permute-start | bytes 172040 | tf_op jit(solution)/shard_map/ppermute | solution.py:43
  177.7 4.9 %collective-permute-start.24 = (f32[224,128]{1,0:T(8,128)S(1)}, f32[224,128]{1,0:T(8,128)S(1)}, u32[]{:S(2)}, u32[]{:S(2)}) collective-permute-start(f32[224,128]{1,0:T(8,128)S(1)} %maximum_select_fusion.13), channel_id=1, source_target_pairs={{0,2},{1,3},{2,0},{3,1},{4,6},{5,7},{6,4},{7,5},{8,10},{9,11},{10,... | collective-permute-start | bytes 344072 | tf_op jit(solution)/shard_map/ppermute | solution.py:43
  179.3 4.9 %collective-permute-start.28 = (f32[48,640]{1,0:T(8,128)S(1)}, f32[48,640]{1,0:T(8,128)S(1)}, u32[]{:S(2)}, u32[]{:S(2)}) collective-permute-start(f32[48,640]{1,0:T(8,128)S(1)} %constant_dynamic-slice_fusion.1), channel_id=1, source_target_pairs={{0,4},{1,5},{2,6},{3,7},{4,0},{5,1},{6,2},{7,3},{8,12},{9,13},{10,... | collective-permute-start | bytes 368648 | tf_op jit(solution)/shard_map/ppermute | solution.py:37
  182.6 3.9 %collective-permute-start.25 = (f32[448,128]{1,0:T(8,128)S(1)}, f32[448,128]{1,0:T(8,128)S(1)}, u32[]{:S(2)}, u32[]{:S(2)}) collective-permute-start(f32[448,128]{1,0:T(8,128)S(1)} %maximum_select_fusion.9), channel_id=1, source_target_pairs={{0,1},{1,0},{2,3},{3,2},{4,5},{5,4},{6,7},{7,6},{8,9},{9,8},{10,11... | collective-permute-start | bytes 688136 | tf_op jit(solution)/shard_map/ppermute | solution.py:43
  184.2 76.6 %collective-permute-start.29 = (f32[24,640]{1,0:T(8,128)S(1)}, f32[24,640]{1,0:T(8,128)S(1)}, u32[]{:S(2)}, u32[]{:S(2)}) collective-permute-start(f32[24,640]{1,0:T(8,128)S(1)} %constant_dynamic-slice_fusion), channel_id=1, source_target_pairs={{0,8},{1,9},{2,10},{3,11},{4,12},{5,13},{6,14},{7,15},{8,0},{9,1},... | collective-permute-start | bytes 184328 | tf_op jit(solution)/shard_map/ppermute | solution.py:37
  260.9 5.2 %collective-permute-start.30 = (f32[24,640]{1,0:T(8,128)S(1)}, f32[24,640]{1,0:T(8,128)S(1)}, u32[]{:S(2)}, u32[]{:S(2)}) collective-permute-start(f32[24,640]{1,0:T(8,128)S(1)} %dynamic-slice_add_fusion.10), channel_id=1, source_target_pairs={{0,8},{1,9},{2,10},{3,11},{4,12},{5,13},{6,14},{7,15},{8,0},{9,1},... | collective-permute-start | bytes 184328 | tf_op jit(solution)/shard_map/ppermute | solution.py:43
  266.1 4.9 %collective-permute-start.31 = (f32[48,640]{1,0:T(8,128)S(1)}, f32[48,640]{1,0:T(8,128)S(1)}, u32[]{:S(2)}, u32[]{:S(2)}) collective-permute-start(f32[48,640]{1,0:T(8,128)S(1)} %maximum_select_fusion.11), channel_id=1, source_target_pairs={{0,4},{1,5},{2,6},{3,7},{4,0},{5,1},{6,2},{7,3},{8,12},{9,13},{10,... | collective-permute-start | bytes 368648 | tf_op jit(solution)/shard_map/ppermute | solution.py:43
  271.1 6.3 %collective-permute-start.32 = (f32[96,640]{1,0:T(8,128)S(1)}, f32[96,640]{1,0:T(8,128)S(1)}, u32[]{:S(2)}, u32[]{:S(2)}) collective-permute-start(f32[96,640]{1,0:T(8,128)S(1)} %maximum_select_fusion.7), channel_id=1, source_target_pairs={{0,2},{1,3},{2,0},{3,1},{4,6},{5,7},{6,4},{7,5},{8,10},{9,11},{10,... | collective-permute-start | bytes 737288 | tf_op jit(solution)/shard_map/ppermute | solution.py:43
  277.4 1.9 collective-permute-start.33
  (6 other events, 17.0 us)
